TPU v7x, 32 devices: a whole 2x2x4 slice. The times are simulated.
32 devices in a mesh: row: 8 (over z, y), col: 4 (over x, core).
Axes of the slice: x: 2, y: 2, z: 4, core: 2. Of those that a mesh axis runs over, the one named last changes fastest.
Arguments:
- inputs: bfloat16 [768, 16384], P('col', 'row'), may hold values from -6 to 6
- segments: int32 [8, 2048], P('row'), may hold values from 0 to 15, never falling along the last dimension, each value on 1 to 1024 neighbouring positions
- query_weight: bfloat16 [768, 768], P('row', 'col'), may hold values from -0.21875 to 0.21875
- key_weight: bfloat16 [768, 768], P('row', 'col'), may hold values from -0.21875 to 0.21875
- value_weight: bfloat16 [768, 768], P('row', 'col'), may hold values from -0.21875 to 0.21875
- query_bias: float32 [768], P('col'), may hold values from -3 to 3
- value_bias: float32 [768], P('col'), may hold values from -0.625 to 0.625
- output_weight: bfloat16 [768, 768], P('col', 'row'), may hold values from -1.75 to 1.75
- output_bias: float32 [768], P('col'), may hold values from -1.75 to 1.75
- attn_gain: float32 [768], P('col'), may hold values from 0.5 to 1.5
- attn_shift: float32 [768], P('col'), may hold values from -1.75 to 1.75
- up_weight: bfloat16 [768, 3072], P('row', 'col'), may hold values from -0.21875 to 0.21875
- up_bias: float32 [3072], P('col'), may hold values from -3 to 3
- down_weight: bfloat16 [3072, 768], P('col', 'row'), may hold values from -0.109375 to 0.109375
- down_bias: float32 [768], P('col'), may hold values from -1.75 to 1.75
- final_gain: float32 [768], P('col'), may hold values from 0.5 to 1.5
- final_shift: float32 [768], P('col'), may hold values from -1.75 to 1.75
- cotangent: bfloat16 [768, 16384], P('col', 'row'), may hold values from -6 to 6
Outputs:
- layer_out: bfloat16 [768, 16384], P('col', 'row')
- input_grad: bfloat16 [768, 16384], P('col', 'row')
- query_weight_grad: float32 [768, 768], P('row', 'col')
- key_weight_grad: float32 [768, 768], P('row', 'col')
- value_weight_grad: float32 [768, 768], P('row', 'col')
- query_bias_grad: float32 [768], P('col')
- value_bias_grad: float32 [768], P('col')
- output_weight_grad: float32 [768, 768], P('col', 'row')
- output_bias_grad: float32 [768], P('col')
- attn_gain_grad: float32 [768], P('col')
- attn_shift_grad: float32 [768], P('col')
- up_weight_grad: float32 [768, 3072], P('row', 'col')
- up_bias_grad: float32 [3072], P('col')
- down_weight_grad: float32 [3072, 768], P('col', 'row')
- down_bias_grad: float32 [768], P('col')
- final_gain_grad: float32 [768], P('col')
- final_shift_grad: float32 [768], P('col')
Inputs may be any that keep to these rules, and one draw needn't show every extreme that they name: `segments`: along each sequence of 2048 tokens the numbers never fall; 0 marks padding tokens; one number covers at most 1024 tokens of a sequence.
All inputs are finite; a program needn't handle non-finite values.
Results may differ from a plain program's by a relative error of at most 0.015.
Values may be sent and summed in bfloat16 or wider, within the bound.
No kernel may reach another device: no remote copies, remote signals or barrier semaphores. Data moves between devices by JAX's collectives and lax.ppermute only.
A program may use at most 256 MiB of HBM per device.

v0:
```python
from functools import partial

import jax
import jax.numpy as jnp
from jax import lax
from jax.sharding import PartitionSpec as P

D = 768
HEADS = 12


NORM_EPS = 1e-06


def feature_whole(blocked):
    return lax.all_gather(blocked, "col", axis=1, tiled=True)


def feature_sum(partial_rows):
    return lax.psum_scatter(partial_rows, "col", scatter_dimension=1, tiled=True)


def row_totals(first_term, second_term):
    return lax.psum((jnp.sum(first_term, axis=1), jnp.sum(second_term, axis=1)), "col")


def norm_forward(row_values, gain_row, shift_row):
    totals, squares = row_totals(row_values, row_values * row_values)
    mean_row = (totals / D)[:, None]
    var_row = (squares / D)[:, None] - mean_row * mean_row
    inverse = lax.rsqrt(var_row + NORM_EPS)
    normed = (row_values - mean_row) * inverse
    return (normed * gain_row + shift_row, normed, inverse)


def norm_backward(grad_rows, normed, inverse, gain_row):
    scaled = grad_rows * gain_row
    totals, along = row_totals(scaled, scaled * normed)
    back_rows = inverse * (scaled - (totals / D)[:, None] - normed * (along / D)[:, None])
    return (back_rows, jnp.sum(grad_rows * normed, axis=0), jnp.sum(grad_rows, axis=0))


def project_in(gathered, stacked):
    complete = lax.all_gather(stacked, "row", axis=1, tiled=True)
    return (
        jnp.einsum("td,kdc->ktc", gathered, complete, preferred_element_type=jnp.float32),
        complete,
    )


def project_in_back(grad_stack, stacked, complete):
    complete = lax.all_gather(stacked, "row", axis=1, tiled=True)
    return jnp.einsum("ktc,kdc->td", grad_stack, complete, preferred_element_type=jnp.float32)


def columns_whole(weight_block):
    return lax.all_gather(weight_block, "row", axis=1, tiled=True)


def project_out_back(grad_full, weight_block, complete):
    contract = (((1,), (1,)), ((), ()))
    complete = lax.all_gather(weight_block, "row", axis=1, tiled=True)
    return lax.dot_general(grad_full, complete, contract, preferred_element_type=jnp.float32)


def weight_grad(gathered, local_grad):
    own_rows = gathered.shape[1] // lax.axis_size("row")
    columns = lax.slice_in_dim(gathered, 0, lax.axis_size("row") * own_rows, axis=1)
    return lax.psum_scatter(
        lax.dot_general(
            columns, local_grad, (((0,), (0,)), ((), ())), preferred_element_type=jnp.float32
        ),
        "row",
        scatter_dimension=0,
        tiled=True,
    )


def allowed_mask(labels, offset, block_rows):
    places = jnp.arange(labels.shape[0])
    query_labels = labels[offset : offset + block_rows]
    query_places = offset + jnp.arange(block_rows)
    matching = (query_labels[:, None] == labels[None, :]) & (labels[None, :] > 0)
    return matching | (query_places[:, None] == places[None, :])


def attend_forward(queries, key_all, value_all, labels, score_scale):
    block_rows = min(512, queries.shape[0])
    outputs = []
    log_totals = []
    for offset in range(0, queries.shape[0], block_rows):
        query_part = queries[offset : offset + block_rows]
        scores = (
            jnp.einsum("qhd,khd->hqk", query_part, key_all, preferred_element_type=jnp.float32)
            * score_scale
        )
        scores = jnp.where(allowed_mask(labels, offset, block_rows)[None], scores, -1000000000.0)
        highest = jnp.max(scores, axis=-1, keepdims=True)
        exponent = jnp.exp(scores - highest)
        totals = jnp.sum(exponent, axis=-1, keepdims=True)
        probability = (exponent / totals).astype(jnp.bfloat16)
        outputs.append(
            jnp.einsum("hqk,khd->qhd", probability, value_all, preferred_element_type=jnp.float32)
        )
        log_totals.append(highest + jnp.log(totals))
    return (jnp.concatenate(outputs, axis=0), jnp.concatenate(log_totals, axis=1))


def attend_backward(queries, key_all, value_all, labels, log_totals, attended_grad, score_scale):
    block_rows = min(512, queries.shape[0])
    query_parts = []
    key_grad = jnp.zeros(key_all.shape, jnp.float32)
    value_grad = jnp.zeros(value_all.shape, jnp.float32)
    for offset in range(0, queries.shape[0], block_rows):
        query_part = queries[offset : offset + block_rows]
        grad_part = attended_grad[offset : offset + block_rows]
        scores = (
            jnp.einsum("qhd,khd->hqk", query_part, key_all, preferred_element_type=jnp.float32)
            * score_scale
        )
        probability = jnp.where(
            allowed_mask(labels, offset, block_rows)[None],
            jnp.exp(scores - log_totals[:, offset : offset + block_rows]),
            0.0,
        )
        prob_grad = jnp.einsum(
            "qhd,khd->hqk", grad_part, value_all, preferred_element_type=jnp.float32
        )
        row_inner = jnp.sum(probability * prob_grad, axis=-1, keepdims=True)
        score_grad = (probability * (prob_grad - row_inner)).astype(jnp.bfloat16)
        query_parts.append(
            jnp.einsum("hqk,khd->qhd", score_grad, key_all, preferred_element_type=jnp.float32)
            * score_scale
        )
        key_grad = (
            key_grad
            + jnp.einsum("hqk,qhd->khd", score_grad, query_part, preferred_element_type=jnp.float32)
            * score_scale
        )
        value_grad = value_grad + jnp.einsum(
            "hqk,qhd->khd",
            probability.astype(jnp.bfloat16),
            grad_part,
            preferred_element_type=jnp.float32,
        )
    return (jnp.concatenate(query_parts, axis=0), key_grad, value_grad)


def body(
    inputs,
    segments,
    query_weight,
    key_weight,
    value_weight,
    query_bias,
    value_bias,
    output_weight,
    output_bias,
    attn_gain,
    attn_shift,
    up_weight,
    up_bias,
    down_weight,
    down_bias,
    final_gain,
    final_shift,
    cotangent,
):
    head_size = D // HEADS
    score_scale = head_size ** (-0.5)
    labels = segments[0]
    token_rows = inputs.T
    out_grad = cotangent.T.astype(jnp.float32)
    token_count = token_rows.shape[0]
    heads_shape = (token_count, -1, head_size)
    inputs_full = feature_whole(token_rows)
    qkv_stack = jnp.stack([query_weight, key_weight, value_weight])
    projected, qkv_complete = project_in(inputs_full, qkv_stack)
    queries = (projected[0] + query_bias).astype(jnp.bfloat16)
    key_all = projected[1].astype(jnp.bfloat16)
    value_all = (projected[2] + value_bias).astype(jnp.bfloat16)
    attended_f, log_totals = attend_forward(
        queries.reshape(heads_shape),
        key_all.reshape(heads_shape),
        value_all.reshape(heads_shape),
        labels,
        score_scale,
    )
    attended = attended_f.reshape(token_count, -1).astype(jnp.bfloat16)
    output_complete = columns_whole(output_weight)
    attn_branch = feature_sum(
        jnp.dot(attended, output_complete, preferred_element_type=jnp.float32)
    )
    first_sum = token_rows.astype(jnp.float32) + attn_branch + output_bias
    hidden, normed_one, inverse_one = norm_forward(first_sum, attn_gain, attn_shift)
    hidden_full = feature_whole(hidden.astype(jnp.bfloat16))
    up_stack = up_weight[None]
    up_projected, up_complete = project_in(hidden_full, up_stack)
    upped = up_projected[0] + up_bias
    acted_f, gelu_pull = jax.vjp(partial(jax.nn.gelu, approximate=False), upped)
    acted = acted_f.astype(jnp.bfloat16)
    down_complete = columns_whole(down_weight)
    ffn_partial = jnp.dot(acted, down_complete, preferred_element_type=jnp.float32)
    second_sum = hidden + feature_sum(ffn_partial) + down_bias
    result, normed_two, inverse_two = norm_forward(second_sum, final_gain, final_shift)
    second_grad, final_gain_grad, final_shift_grad = norm_backward(
        out_grad, normed_two, inverse_two, final_gain
    )
    branch_grad = second_grad.astype(jnp.bfloat16)
    branch_full = feature_whole(branch_grad)
    down_weight_grad = weight_grad(branch_full, acted).T
    acted_grad = project_out_back(branch_full, down_weight, down_complete)
    upped_grad = gelu_pull(acted_grad)[0].astype(jnp.bfloat16)
    up_weight_grad = weight_grad(hidden_full, upped_grad)
    hidden_grad = second_grad + feature_sum(
        project_in_back(upped_grad[None], up_stack, up_complete)
    )
    first_grad, attn_gain_grad, attn_shift_grad = norm_backward(
        hidden_grad, normed_one, inverse_one, attn_gain
    )
    attn_branch_grad = first_grad.astype(jnp.bfloat16)
    attn_branch_full = feature_whole(attn_branch_grad)
    output_weight_grad = weight_grad(attn_branch_full, attended).T
    attended_grad = project_out_back(attn_branch_full, output_weight, output_complete).astype(
        jnp.bfloat16
    )
    query_grad_f, key_grad_f, value_grad_f = attend_backward(
        queries.reshape(heads_shape),
        key_all.reshape(heads_shape),
        value_all.reshape(heads_shape),
        labels,
        log_totals,
        attended_grad.reshape(heads_shape),
        score_scale,
    )
    query_grad = query_grad_f.reshape(token_count, -1).astype(jnp.bfloat16)
    key_grad = key_grad_f.reshape(token_count, -1).astype(jnp.bfloat16)
    value_grad = value_grad_f.reshape(token_count, -1).astype(jnp.bfloat16)
    column_count = query_weight.shape[1]
    qkv_grads = weight_grad(
        inputs_full, jnp.concatenate([query_grad, key_grad, value_grad], axis=1)
    )
    input_grad = first_grad + feature_sum(
        project_in_back(jnp.stack([query_grad, key_grad, value_grad]), qkv_stack, qkv_complete)
    )
    param_totals = lax.psum(
        (
            jnp.sum(query_grad.astype(jnp.float32), axis=0),
            jnp.sum(value_grad.astype(jnp.float32), axis=0),
            jnp.sum(attn_branch_grad.astype(jnp.float32), axis=0),
            attn_gain_grad,
            attn_shift_grad,
            jnp.sum(upped_grad.astype(jnp.float32), axis=0),
            jnp.sum(branch_grad.astype(jnp.float32), axis=0),
            final_gain_grad,
            final_shift_grad,
        ),
        "row",
    )
    return (
        result.astype(jnp.bfloat16).T,
        input_grad.astype(jnp.bfloat16).T,
        qkv_grads[:, :column_count],
        qkv_grads[:, column_count : 2 * column_count],
        qkv_grads[:, 2 * column_count :],
        param_totals[0],
        param_totals[1],
        output_weight_grad,
        param_totals[2],
        param_totals[3],
        param_totals[4],
        up_weight_grad,
        param_totals[5],
        down_weight_grad,
        param_totals[6],
        param_totals[7],
        param_totals[8],
    )


def solution(mesh):
    placed = (
        P("col", "row"),
        P("row", None),
        P("row", "col"),
        P("row", "col"),
        P("row", "col"),
        P("col"),
        P("col"),
        P("col", "row"),
        P("col"),
        P("col"),
        P("col"),
        P("row", "col"),
        P("col"),
        P("col", "row"),
        P("col"),
        P("col"),
        P("col"),
        P("col", "row"),
    )
    return jax.shard_map(
        body,
        mesh=mesh,
        in_specs=placed,
        out_specs=(
            P("col", "row"),
            P("col", "row"),
            P("row", "col"),
            P("row", "col"),
            P("row", "col"),
            P("col"),
            P("col"),
            P("col", "row"),
            P("col"),
            P("col"),
            P("col"),
            P("row", "col"),
            P("col"),
            P("col", "row"),
            P("col"),
            P("col"),
            P("col"),
        ),
        check_vma=False,
    )
```

profile of v0, /device:TPU:12, one launch (start us, length us, event | category | flops | bytes accessed | tf_op | source)
XLA Modules:
  0.0 996.4 jit_solution(5878474245332988571)
XLA Ops:
  12.2 30.5 %all_gather.30 = bf16[192,768]{0,1:T(8,128)(2,1)} all-gather(bf16[192,96]{0,1:T(8,128)(2,1)S(1)} %copy.52), channel_id=1, replica_groups=mesh['row'=8,'col'=4] {'row'}, dimensions={1}, use_global_device_ids=true | all-gather | bytes 331776 | tf_op jit(solution)/shard_map/all_gather | solution.py:57
  43.5 38.2 %all_gather.28 = bf16[3,768,192]{2,0,1:T(4,128)(2,1)} all-gather(bf16[3,96,192]{2,0,1:T(4,128)(2,1)S(1)} %copy.50), channel_id=1, replica_groups=mesh['row'=8,'col'=4] {'row'}, dimensions={1}, use_global_device_ids=true | all-gather | bytes 995328 | tf_op jit(solution)/shard_map/all_gather | solution.py:44
  126.8 6.9 fusion.83
  146.4 6.8 fusion.85
  178.3 61.5 %reduce-scatter.11.cloned.1.call-done = f32[2048,192]{0,1:T(8,128)} async-done(((f32[2048,768]{0,1:T(8,128)}), f32[2048,192]{0,1:T(8,128)}) %reduce-scatter.11.cloned.1.call-update) | async-done | bytes 1572880 | tf_op jit(solution)/shard_map/reduce_scatter | solution.py:20
  241.6 10.2 %all-reduce.4 = (f32[2048]{0:T(1024)S(1)}, f32[2048]{0:T(1024)S(1)}) all-reduce(f32[2048]{0:T(1024)S(1)} %get-tuple-element.77, f32[2048]{0:T(1024)S(1)} %get-tuple-element.76), channel_id=1, replica_groups=mesh['row'=8,'col'=4] {'col'}, use_global_device_ids=true, to_apply=%region_12.13 | all-reduce | flops 4096 | bytes 32768 | tf_op jit(solution)/shard_map/psum | solution.py:24
  253.8 28.3 %all-gather.10.cloned.1.call-done = bf16[2048,768]{0,1:T(8,128)(2,1)} async-done(((bf16[2048,192]{0,1:T(8,128)(2,1)}), bf16[2048,768]{0,1:T(8,128)(2,1)}) %all-gather.10.cloned.1.call-update) | async-done | bytes 3145744 | tf_op jit(solution)/shard_map/all_gather | solution.py:16
  282.1 19.3 %multiply_convert_fusion.4 = (bf16[2048,768]{1,0:T(8,128)(2,1)}, f32[2048,768]{1,0:T(8,128)}, f32[2048,768]{1,0:T(8,128)}) fusion(f32[768]{0:T(1024)S(1)} %copy-done.63, bf16[2048,768]{0,1:T(8,128)(2,1)} %all-gather.10.cloned.1.call-done, bf16[768,768]{1,0:T(8,128)(2,1)} %all-gather.18.cloned.1.call-done), kind=kOutput, calls=%fused_computation.36 | convolution fusion | flops 2519728128 | bytes 20057088 | tf_op jit(solution)/shard_map/td,kdc->ktc/dot_general | solution.py:46
  301.4 22.3 %all-gather.12.cloned.1.call-done = bf16[768,768]{0,1:T(8,128)(2,1)} async-done(((bf16[768,96]{0,1:T(8,128)(2,1)}), bf16[768,768]{0,1:T(8,128)(2,1)}) %all-gather.12.cloned.1.call-update) | async-done | bytes 1179664 | tf_op jit(solution)/shard_map/all_gather | solution.py:57
  323.7 7.5 fusion.122
  331.2 59.1 %reduce-scatter.13.cloned.1.call-done = f32[2048,192]{0,1:T(8,128)} async-done(((f32[2048,768]{0,1:T(8,128)}), f32[2048,192]{0,1:T(8,128)}) %reduce-scatter.13.cloned.1.call-update) | async-done | bytes 1572880 | tf_op jit(solution)/shard_map/reduce_scatter | solution.py:20
  393.5 10.2 %all-reduce.3 = (f32[2048]{0:T(1024)S(1)}, f32[2048]{0:T(1024)S(1)}) all-reduce(f32[2048]{0:T(1024)S(1)} %get-tuple-element.75, f32[2048]{0:T(1024)S(1)} %get-tuple-element.74), channel_id=1, replica_groups=mesh['row'=8,'col'=4] {'col'}, use_global_device_ids=true, to_apply=%region_17.18 | all-reduce | flops 4096 | bytes 32768 | tf_op jit(solution)/shard_map/psum | solution.py:24
  406.6 10.1 %all-reduce.2 = (f32[2048]{0:T(1024)S(1)}, f32[2048]{0:T(1024)S(1)}) all-reduce(f32[2048]{0:T(1024)S(1)} %get-tuple-element.71, f32[2048]{0:T(1024)S(1)} %get-tuple-element.78), channel_id=1, replica_groups=mesh['row'=8,'col'=4] {'col'}, use_global_device_ids=true, to_apply=%region_21.22 | all-reduce | flops 4096 | bytes 32768 | tf_op jit(solution)/shard_map/psum | solution.py:24
  420.4 28.9 %all-gather.14.cloned.1.call-done = bf16[2048,768]{0,1:T(8,128)(2,1)} async-done(((bf16[2048,192]{0,1:T(8,128)(2,1)}), bf16[2048,768]{0,1:T(8,128)(2,1)}) %all-gather.14.cloned.1.call-update) | async-done | bytes 3145744 | tf_op jit(solution)/shard_map/all_gather | solution.py:16
  449.3 11.5 %convert_reduce_fusion = (f32[768]{0:T(1024)}, bf16[2048,768]{1,0:T(8,128)(2,1)S(1)}) fusion(f32[2048,768]{1,0:T(8,128)} %get-tuple-element.107, f32[2048,768]{1,0:T(8,128)} %get-tuple-element.141, f32[768]{0:T(1024)S(1)} %copy-done.63, bf16[2048,768]{0,1:T(8,128)(2,1)} %all-gather.14.cloned.1.call-done, bf16[768,768]{0,1:T(8,128)(2,1)} %all-gather.12.cloned.1.call-done), kind=kOutput, calls=%fused_computation.34 | convolution fusion | flops 2442657024 | bytes 20060160 | tf_op jit(solution)/shard_map/dot_general | solution.py:63
  467.0 58.7 %reduce-scatter.15.cloned.1.call-done = f32[2048,192]{0,1:T(8,128)} async-done(((f32[2048,768]{0,1:T(8,128)}), f32[2048,192]{0,1:T(8,128)}) %reduce-scatter.15.cloned.1.call-update) | async-done | bytes 1572880 | tf_op jit(solution)/shard_map/reduce_scatter | solution.py:20
  530.9 10.3 %all-reduce.1 = (f32[2048]{0:T(1024)S(1)}, f32[2048]{0:T(1024)S(1)}) all-reduce(f32[2048]{0:T(1024)S(1)} %get-tuple-element.69, f32[2048]{0:T(1024)S(1)} %get-tuple-element.72), channel_id=1, replica_groups=mesh['row'=8,'col'=4] {'col'}, use_global_device_ids=true, to_apply=%region_26.27 | all-reduce | flops 4096 | bytes 32768 | tf_op jit(solution)/shard_map/psum | solution.py:24
  545.0 28.7 %all-gather.16.cloned.1.call-done = bf16[2048,768]{0,1:T(8,128)(2,1)} async-done(((bf16[2048,192]{0,1:T(8,128)(2,1)}), bf16[2048,768]{0,1:T(8,128)(2,1)}) %all-gather.16.cloned.1.call-update) | async-done | bytes 3145744 | tf_op jit(solution)/shard_map/all_gather | solution.py:16
  577.2 7.5 fusion.18
  584.7 10.5 %multiply_reduce_fusion.2 = (f32[3,512]{1,0:T(4,128)S(1)}, f32[3,512,2048]{2,1,0:T(8,128)}) fusion(f32[3,512,2048]{2,1,0:T(8,128)} %get-tuple-element.138, f32[3,512]{1,0:T(4,128)S(1)} %log_add_fusion.2, pred[512,2048]{1,0:T(8,128)(4,1)S(1)} %copy-done.12, bf16[512,3,64]{0,2,1:T(8,128)(2,1)S(1)} %bitcast.187, bf16[2048,3,64]{0,2,1:T(8,128)(2,1)S(1)} %add_convert_fusion.3), kind=kOutput, calls=%fused_computation.7 | convolution fusion | flops 418380288 | bytes 27209728 | tf_op jit(solution)/shard_map/qhd,khd->hqk/dot_general | solution.py:126
  595.3 8.2 multiply_reduce_fusion.3
  603.4 23.6 %multiply_convert_fusion.2 = (bf16[3,512,2048]{2,1,0:T(8,128)(2,1)}, bf16[3,512,2048]{2,1,0:T(8,128)(2,1)}) fusion(f32[3,512,2048]{2,1,0:T(8,128)} %get-tuple-element.145, f32[3,512,2048]{2,1,0:T(8,128)} %get-tuple-element.138, f32[3,512]{1,0:T(4,128)S(1)} %get-tuple-element.144, f32[3,512]{1,0:T(4,128)S(1)} %log_add_fusion.2, ...), kind=kLoop, calls=%fused_computation.6 | loop fusion | flops 37748736 | bytes 65036288 | tf_op jit(solution)/shard_map/convert_element_type | solution.py:130
  638.7 7.6 multiply_reduce_fusion.1
  648.3 7.9 fusion.39
  656.2 11.0 %multiply_reduce_fusion = (f32[3,512]{1,0:T(4,128)S(1)}, f32[3,512,2048]{2,1,0:T(8,128)}) fusion(f32[3,512,2048]{2,1,0:T(8,128)} %get-tuple-element.134, f32[3,512]{1,0:T(4,128)S(1)} %log_add_fusion, pred[512,2048]{1,0:T(8,128)(4,1)S(1)} %copy-done.7, bf16[512,3,64]{0,2,1:T(8,128)(2,1)S(1)} %bitcast.180, bf16[2048,3,64]{0,2,1:T(8,128)(2,1)S(1)} %add_convert_fusion.3), kind=kOutput, calls=%fused_computation.1 | convolution fusion | flops 418380288 | bytes 27209728 | tf_op jit(solution)/shard_map/qhd,khd->hqk/dot_general | solution.py:126
  676.4 18.3 %multiply_convert_fusion = (bf16[3,512,2048]{2,1,0:T(8,128)(2,1)}, bf16[3,512,2048]{2,1,0:T(8,128)(2,1)}) fusion(f32[3,512,2048]{2,1,0:T(8,128)} %get-tuple-element.149, f32[3,512,2048]{2,1,0:T(8,128)S(1)} %bitcast.159, f32[3,512]{1,0:T(4,128)S(1)} %get-tuple-element.148, f32[3,512]{1,0:T(4,128)S(1)} %log_add_fusion, pred[512,2048]{1,0:T(8,128)(4,1)S(1)} %copy-done.7, ...), kind=kLoop, calls=%fused_computation | loop fusion | flops 37748736 | bytes 65036288 | tf_op jit(solution)/shard_map/convert_element_type | solution.py:130
  725.8 7.1 fusion.127
  734.4 30.7 %all-reduce = (f32[192]{0:T(256)}, f32[192]{0:T(256)}, f32[192]{0:T(256)}, f32[192]{0:T(256)}, f32[192]{0:T(256)}, /*index=5*/f32[768]{0:T(1024)}, f32[192]{0:T(256)}, f32[192]{0:T(256)}, f32[192]{0:T(256)}) all-reduce(f32[192]{0:T(256)S(1)} %reduce_sum.246, f32[192]{0:T(256)S(1)} %reduce_sum.248, ...), channel_id=1, replica_groups=mesh['row'=8,'col'=4] {'row'}, use_global_device_ids=true, to_apply=%region_34.35 | all-reduce | flops 2304 | bytes 18432 | tf_op jit(solution)/shard_map/psum | solution.py:246
  766.7 14.1 %reduce-scatter.25.cloned.1.call-done = f32[96,576]{1,0:T(8,128)} async-done(((f32[768,576]{1,0:T(8,128)}), f32[96,576]{1,0:T(8,128)}) %reduce-scatter.25.cloned.1.call-update) | async-done | bytes 221200
  782.6 59.2 %reduce-scatter.17.cloned.1.call-done = f32[2048,192]{0,1:T(8,128)} async-done(((f32[2048,768]{0,1:T(8,128)}), f32[2048,192]{0,1:T(8,128)}) %reduce-scatter.17.cloned.1.call-update) | async-done | bytes 1572880 | tf_op jit(solution)/shard_map/reduce_scatter | solution.py:20
  844.6 70.9 %reduce-scatter.21.cloned.1.call-done = f32[96,768]{1,0:T(8,128)} async-done(((f32[768,768]{1,0:T(8,128)}), f32[96,768]{1,0:T(8,128)}) %reduce-scatter.21.cloned.1.call-update) | async-done | bytes 294928 | tf_op jit(solution)/shard_map/reduce_scatter | solution.py:69
  915.5 73.3 %reduce-scatter.23.cloned.1.call-done = f32[96,768]{1,0:T(8,128)} async-done(((f32[768,768]{1,0:T(8,128)}), f32[96,768]{1,0:T(8,128)}) %reduce-scatter.23.cloned.1.call-update) | async-done | bytes 294928 | tf_op jit(solution)/shard_map/reduce_scatter | solution.py:69
  (264 shorter events, 180.7 us)
Async XLA Ops:
  8.0 80.4 %all-gather.8.cloned.1.call-start = ((), (), s32[]{:S(2)}) async-start(), calls=%async_computation.8 | async-start | bytes 3932160 | tf_op jit(solution)/shard_map/all_gather | solution.py:16
  8.8 231.1 %reduce-scatter.11.cloned.1.call-start = ((), (), s32[]{:S(2)}) async-start(), calls=%async_computation.9 | async-start | bytes 7864320 | tf_op jit(solution)/shard_map/reduce_scatter | solution.py:20
  93.8 59.4 %copy-start.13 = (bf16[1,2048,192]{1,2,0:T(8,128)(2,1)}, bf16[1,2048,192]{1,2,0:T(8,128)(2,1)S(1)}, u32[]{:S(2)}) copy-start(bf16[1,2048,192]{1,2,0:T(8,128)(2,1)S(1)} %slice.137) | copy-start | bytes 2359300
  94.2 59.1 %copy-start.34 = (bf16[512,192]{0,1:T(8,128)(2,1)}, bf16[512,192]{0,1:T(8,128)(2,1)S(1)}, u32[]{:S(2)}) copy-start(bf16[512,192]{0,1:T(8,128)(2,1)S(1)} %get-tuple-element.117) | copy-start | bytes 589828
  173.7 66.1 %copy-start.22 = (bf16[192,2048]{1,0:T(8,128)(2,1)S(1)}, bf16[192,2048]{1,0:T(8,128)(2,1)}, u32[]{:S(2)}) copy-start(bf16[192,2048]{1,0:T(8,128)(2,1)} %param.18) | copy-start | bytes 2359300
  173.7 66.1 %copy-start.57 = (f32[192]{0:T(256)S(1)}, f32[192]{0:T(256)}, u32[]{:S(2)}) copy-start(f32[192]{0:T(256)} %param.26) | copy-start | bytes 2308
  177.3 74.6 %copy-start.46 = (f32[192]{0:T(256)S(1)}, f32[192]{0:T(256)}, u32[]{:S(2)}) copy-start(f32[192]{0:T(256)} %param.27) | copy-start | bytes 2308
  177.3 74.6 %copy-start.48 = (f32[192]{0:T(256)S(1)}, f32[192]{0:T(256)}, u32[]{:S(2)}) copy-start(f32[192]{0:T(256)} %param.28) | copy-start | bytes 2308
  177.3 104.8 %copy-start.63 = (f32[768]{0:T(1024)S(1)}, f32[768]{0:T(1024)}, u32[]{:S(2)}) copy-start(f32[768]{0:T(1024)} %param.30) | copy-start | bytes 9220
  177.3 76.5 %all-gather.18.cloned.1.call-start = ((), (), s32[]{:S(2)}) async-start(), calls=%async_computation.20 | async-start | bytes 1327104 | tf_op jit(solution)/shard_map/all_gather | solution.py:44
  177.9 104.2 %all-gather.10.cloned.1.call-start = ((), (), s32[]{:S(2)}) async-start(), calls=%async_computation.10 | async-start | bytes 3932160 | tf_op jit(solution)/shard_map/all_gather | solution.py:16
  241.6 299.6 %copy-start.2 = (f32[2048,192]{0,1:T(8,128)}, f32[2048,192]{0,1:T(8,128)S(1)}, u32[]{:S(2)}) copy-start(f32[2048,192]{0,1:T(8,128)S(1)} %get-tuple-element.108) | copy-start | bytes 4718596
  253.1 70.5 %all-gather.12.cloned.1.call-start = ((), (), s32[]{:S(2)}) async-start(), calls=%async_computation.11 | async-start | bytes 1327104 | tf_op jit(solution)/shard_map/all_gather | solution.py:57
  253.7 136.6 %reduce-scatter.13.cloned.1.call-start = ((), (), s32[]{:S(2)}) async-start(), calls=%async_computation.12 | async-start | bytes 7864320 | tf_op jit(solution)/shard_map/reduce_scatter | solution.py:20
  331.1 59.2 %copy-start.58 = (f32[192]{0:T(256)S(1)}, f32[192]{0:T(256)}, u32[]{:S(2)}) copy-start(f32[192]{0:T(256)} %param.32) | copy-start | bytes 2308
  331.1 72.6 %copy-start.17 = (bf16[192,2048]{1,0:T(8,128)(2,1)S(1)}, bf16[192,2048]{1,0:T(8,128)(2,1)}, u32[]{:S(2)}) copy-start(bf16[192,2048]{1,0:T(8,128)(2,1)} %param.35) | copy-start | bytes 2359300
  331.1 72.6 %copy-start.47 = (f32[192]{0:T(256)S(1)}, f32[192]{0:T(256)}, u32[]{:S(2)}) copy-start(f32[192]{0:T(256)} %param.33) | copy-start | bytes 2308
  331.2 118.1 %all-gather.14.cloned.1.call-start = ((), (), s32[]{:S(2)}) async-start(), calls=%async_computation.13 | async-start | bytes 3932160 | tf_op jit(solution)/shard_map/all_gather | solution.py:16
  420.2 105.5 %reduce-scatter.15.cloned.1.call-start = ((), (), s32[]{:S(2)}) async-start(), calls=%async_computation.14 | async-start | bytes 7864320 | tf_op jit(solution)/shard_map/reduce_scatter | solution.py:20
  466.8 58.9 %copy-start.59 = (f32[192]{0:T(256)S(1)}, f32[192]{0:T(256)}, u32[]{:S(2)}) copy-start(f32[192]{0:T(256)} %param.34) | copy-start | bytes 2308
  466.9 78.0 %copy-start.39 = (f32[3,512]{1,0:T(4,128)S(1)}, f32[3,512]{1,0:T(4,128)}, u32[]{:S(2)}) copy-start(f32[3,512]{1,0:T(4,128)} %copy-done.38) | copy-start | bytes 18436
  466.9 78.0 %copy-start.41 = (f32[3,512]{1,0:T(4,128)S(1)}, f32[3,512]{1,0:T(4,128)}, u32[]{:S(2)}) copy-start(f32[3,512]{1,0:T(4,128)} %copy-done.40) | copy-start | bytes 18436
  466.9 78.0 %copy-start.43 = (f32[3,512]{1,0:T(4,128)S(1)}, f32[3,512]{1,0:T(4,128)}, u32[]{:S(2)}) copy-start(f32[3,512]{1,0:T(4,128)} %copy-done.42) | copy-start | bytes 18436
  466.9 78.0 %copy-start.45 = (f32[3,512]{1,0:T(4,128)S(1)}, f32[3,512]{1,0:T(4,128)}, u32[]{:S(2)}) copy-start(f32[3,512]{1,0:T(4,128)} %copy-done.44) | copy-start | bytes 18436
  466.9 106.7 %all-gather.16.cloned.1.call-start = ((), (), s32[]{:S(2)}) async-start(), calls=%async_computation.15 | async-start | bytes 3932160 | tf_op jit(solution)/shard_map/all_gather | solution.py:16
  544.6 220.5 %reduce-scatter.19.cloned.1.call-start = ((), (), s32[]{:S(2)}) async-start(), calls=%async_computation.17 | async-start | bytes 884736 | tf_op jit(solution)/shard_map/reduce_scatter | solution.py:69
  648.2 132.6 %reduce-scatter.25.cloned.1.call-start = ((), (), s32[]{:S(2)}) async-start(), calls=%async_computation.21 | async-start | bytes 2211840
  711.1 130.7 %reduce-scatter.17.cloned.1.call-start = ((), (), s32[]{:S(2)}) async-start(), calls=%async_computation.16 | async-start | bytes 7864320 | tf_op jit(solution)/shard_map/reduce_scatter | solution.py:20
  717.5 198.0 %reduce-scatter.21.cloned.1.call-start = ((), (), s32[]{:S(2)}) async-start(), calls=%async_computation.18 | async-start | bytes 2654208 | tf_op jit(solution)/shard_map/reduce_scatter | solution.py:69
  725.4 116.4 %copy-start.3 = (f32[2048,192]{0,1:T(8,128)S(1)}, f32[2048,192]{0,1:T(8,128)}, u32[]{:S(2)}) copy-start(f32[2048,192]{0,1:T(8,128)} %copy-done.2) | copy-start | bytes 4718596
  725.4 116.3 %copy-start.16 = (f32[2048,192]{0,1:T(8,128)S(1)}, f32[2048,192]{0,1:T(8,128)}, u32[]{:S(2)}) copy-start(f32[2048,192]{0,1:T(8,128)} %get-tuple-element.104) | copy-start | bytes 4718596
  725.5 263.4 %reduce-scatter.23.cloned.1.call-start = ((), (), s32[]{:S(2)}) async-start(), calls=%async_computation.19 | async-start | bytes 2654208 | tf_op jit(solution)/shard_map/reduce_scatter | solution.py:69
  (61 other events, 690.5 us)
Sparse Core Ops, SparseCore 0:
  10.4 29.6 all-gather.7
  177.4 62.3 reduce-scatter.10
  420.3 28.9 all-gather.13
  544.7 28.8 all-gather.15
Sparse Core Ops, SparseCore 1:
  180.0 42.8 all-gather.17
  253.2 28.8 all-gather.9
  284.2 39.4 all-gather.11
  331.3 59.0 reduce-scatter.12
  466.9 58.7 reduce-scatter.14
  648.3 63.2 reduce-scatter.18
  714.9 65.9 reduce-scatter.24
  783.2 58.5 reduce-scatter.16
  845.7 69.7 reduce-scatter.20
  919.6 69.2 reduce-scatter.22
where the time goes:
time: 1010 us; the launch traced here: 996 us
  waiting for transfers between devices  507 us (50%)
  matrix products  213 us (21%)
  blocking collectives  140 us (14%)
  other arithmetic  103 us (10%)
  between operations  16.8 us (2%)
  local copies, waits for them, and re-layouts  14.6 us (1%)
    reduce_scatter x4, waiting for transfers between devices, feature_sum(): lax.psum_scatter(partial_rows, 'col', scatter_dimension=1, tiled=True)  238 us
    reduce_scatter x3, waiting for transfers between devices, weight_grad(): lax.psum_scatter(lax.dot_general(columns, local_grad, (((0,), (0,)), ((),...  144 us
    all_gather x4, waiting for transfers between devices, feature_whole(): return lax.all_gather(blocked, 'col', axis=1, tiled=True)  85.8 us
    convert_element_type x2, other arithmetic, attend_backward(): score_grad = (probability * (prob_grad - row_inner)).astype(jnp.bfloat16)  41.9 us
    psum x4, blocking collectives, row_totals(): lax.psum((jnp.sum(first_term, axis=1), jnp.sum(second_term, axis=1)), 'col')  40.9 us
    all_gather x1, blocking collectives, project_in(): complete = lax.all_gather(stacked, 'row', axis=1, tiled=True)  38.2 us
    dot_general x4, matrix products, attend_backward(): jnp.einsum('qhd,khd->hqk', grad_part, value_all, preferred_element_type=j...  37.3 us
    psum x1, blocking collectives, body(): lax.psum((jnp.sum(query_grad.astype(jnp.float32), axis=0), jnp.sum(value_...  30.7 us
  transfers between devices with their start and end apart: 14, of which 11 were waited for; matrix products, arithmetic and copies ran while one was open for 12% of the time, Pallas kernels for 0%

commit v1 on v0

--- a/solution.py
+++ b/solution.py
@@ -1,12 +1,126 @@
 from functools import partial
+import functools
 
 import jax
 import jax.numpy as jnp
 from jax import lax
+from jax.experimental import pallas as pl
+from jax.experimental.pallas import tpu as pltpu
 from jax.sharding import PartitionSpec as P
 
 D = 768
 HEADS = 12
+BQ = 256
+
+
+def _mask(lab_q, lab_k, q0, bq, nk):
+    rows = q0 + lax.broadcasted_iota(jnp.int32, (bq, nk), 0)
+    cols = lax.broadcasted_iota(jnp.int32, (bq, nk), 1)
+    return ((lab_q == lab_k) & (lab_k > 0)) | (rows == cols)
+
+
+def _fwd_kernel(scale, q_ref, k_ref, v_ref, lq_ref, lk_ref, o_ref, m_ref, l_ref):
+    i = pl.program_id(1)
+    bq = q_ref.shape[0]
+    nk = k_ref.shape[0]
+    s = lax.dot_general(q_ref[...], k_ref[...], (((1,), (1,)), ((), ())),
+                        preferred_element_type=jnp.float32) * scale
+    allowed = _mask(lq_ref[...], lk_ref[...], i * bq, bq, nk)
+    s = jnp.where(allowed, s, -1000000000.0)
+    m = jnp.max(s, axis=1, keepdims=True)
+    e = jnp.exp(s - m)
+    l = jnp.sum(e, axis=1, keepdims=True)
+    p = (e / l).astype(jnp.bfloat16)
+    o_ref[...] = jnp.dot(p, v_ref[...], preferred_element_type=jnp.float32).astype(o_ref.dtype)
+    m_ref[...] = m
+    l_ref[...] = l
+
+
+def _bwd_kernel(scale, q_ref, k_ref, v_ref, do_ref, lq_ref, lk_ref, m_ref, l_ref,
+                dq_ref, dk_ref, dv_ref):
+    i = pl.program_id(1)
+    bq = q_ref.shape[0]
+    nk = k_ref.shape[0]
+
+    @pl.when(i == 0)
+    def _():
+        dk_ref[...] = jnp.zeros_like(dk_ref)
+        dv_ref[...] = jnp.zeros_like(dv_ref)
+
+    q = q_ref[...]
+    k = k_ref[...]
+    s = lax.dot_general(q, k, (((1,), (1,)), ((), ())),
+                        preferred_element_type=jnp.float32) * scale
+    allowed = _mask(lq_ref[...], lk_ref[...], i * bq, bq, nk)
+    s = jnp.where(allowed, s, -1000000000.0)
+    p = jnp.where(allowed, jnp.exp(s - m_ref[...]) / l_ref[...], 0.0)
+    do = do_ref[...]
+    dp = lax.dot_general(do, v_ref[...], (((1,), (1,)), ((), ())),
+                         preferred_element_type=jnp.float32)
+    inner = jnp.sum(p * dp, axis=1, keepdims=True)
+    ds = (p * (dp - inner)).astype(jnp.bfloat16)
+    dq_ref[...] = (jnp.dot(ds, k, preferred_element_type=jnp.float32) * scale).astype(dq_ref.dtype)
+    dk_ref[...] += lax.dot_general(ds, q, (((0,), (0,)), ((), ())),
+                                   preferred_element_type=jnp.float32) * scale
+    dv_ref[...] += lax.dot_general(p.astype(jnp.bfloat16), do, (((0,), (0,)), ((), ())),
+                                   preferred_element_type=jnp.float32)
+
+
+def attention_forward(q, k, v, labels, scale):
+    nh, seq, hd = q.shape
+    bq = min(BQ, seq)
+    lq = labels.reshape(seq, 1)
+    lk = labels.reshape(1, seq)
+    grid = (nh, seq // bq)
+    qspec = pl.BlockSpec((None, bq, hd), lambda h, i: (h, i, 0))
+    kspec = pl.BlockSpec((None, seq, hd), lambda h, i: (h, 0, 0))
+    rowspec = pl.BlockSpec((None, bq, 1), lambda h, i: (h, i, 0))
+    flops = 4 * nh * seq * seq * hd
+    return pl.pallas_call(
+        functools.partial(_fwd_kernel, scale),
+        grid=grid,
+        in_specs=[qspec, kspec, kspec,
+                  pl.BlockSpec((bq, 1), lambda h, i: (i, 0)),
+                  pl.BlockSpec((1, seq), lambda h, i: (0, 0))],
+        out_specs=[qspec, rowspec, rowspec],
+        out_shape=[jax.ShapeDtypeStruct((nh, seq, hd), jnp.bfloat16),
+                   jax.ShapeDtypeStruct((nh, seq, 1), jnp.float32),
+                   jax.ShapeDtypeStruct((nh, seq, 1), jnp.float32)],
+        compiler_params=pltpu.CompilerParams(
+            dimension_semantics=("parallel", "arbitrary"),
+            vmem_limit_bytes=48 * 1024 * 1024),
+        cost_estimate=pl.CostEstimate(flops=flops, transcendentals=nh * seq * seq,
+                                      bytes_accessed=4 * nh * seq * hd * 2),
+    )(q, k, v, lq, lk)
+
+
+def attention_backward(q, k, v, do, labels, m, l, scale):
+    nh, seq, hd = q.shape
+    bq = min(BQ, seq)
+    lq = labels.reshape(seq, 1)
+    lk = labels.reshape(1, seq)
+    grid = (nh, seq // bq)
+    qspec = pl.BlockSpec((None, bq, hd), lambda h, i: (h, i, 0))
+    kspec = pl.BlockSpec((None, seq, hd), lambda h, i: (h, 0, 0))
+    rowspec = pl.BlockSpec((None, bq, 1), lambda h, i: (h, i, 0))
+    flops = 10 * nh * seq * seq * hd
+    return pl.pallas_call(
+        functools.partial(_bwd_kernel, scale),
+        grid=grid,
+        in_specs=[qspec, kspec, kspec, qspec,
+                  pl.BlockSpec((bq, 1), lambda h, i: (i, 0)),
+                  pl.BlockSpec((1, seq), lambda h, i: (0, 0)),
+                  rowspec, rowspec],
+        out_specs=[qspec, kspec, kspec],
+        out_shape=[jax.ShapeDtypeStruct((nh, seq, hd), jnp.bfloat16),
+                   jax.ShapeDtypeStruct((nh, seq, hd), jnp.float32),
+                   jax.ShapeDtypeStruct((nh, seq, hd), jnp.float32)],
+        compiler_params=pltpu.CompilerParams(
+            dimension_semantics=("parallel", "arbitrary"),
+            vmem_limit_bytes=48 * 1024 * 1024),
+        cost_estimate=pl.CostEstimate(flops=flops, transcendentals=nh * seq * seq,
+                                      bytes_accessed=8 * nh * seq * hd * 2),
+    )(q, k, v, do, lq, lk, m, l)
 
 
 NORM_EPS = 1e-06
@@ -76,74 +190,20 @@
     )
 
 
-def allowed_mask(labels, offset, block_rows):
-    places = jnp.arange(labels.shape[0])
-    query_labels = labels[offset : offset + block_rows]
-    query_places = offset + jnp.arange(block_rows)
-    matching = (query_labels[:, None] == labels[None, :]) & (labels[None, :] > 0)
-    return matching | (query_places[:, None] == places[None, :])
-
-
-def attend_forward(queries, key_all, value_all, labels, score_scale):
-    block_rows = min(512, queries.shape[0])
-    outputs = []
-    log_totals = []
-    for offset in range(0, queries.shape[0], block_rows):
-        query_part = queries[offset : offset + block_rows]
-        scores = (
-            jnp.einsum("qhd,khd->hqk", query_part, key_all, preferred_element_type=jnp.float32)
-            * score_scale
-        )
-        scores = jnp.where(allowed_mask(labels, offset, block_rows)[None], scores, -1000000000.0)
-        highest = jnp.max(scores, axis=-1, keepdims=True)
-        exponent = jnp.exp(scores - highest)
-        totals = jnp.sum(exponent, axis=-1, keepdims=True)
-        probability = (exponent / totals).astype(jnp.bfloat16)
-        outputs.append(
-            jnp.einsum("hqk,khd->qhd", probability, value_all, preferred_element_type=jnp.float32)
-        )
-        log_totals.append(highest + jnp.log(totals))
-    return (jnp.concatenate(outputs, axis=0), jnp.concatenate(log_totals, axis=1))
-
-
-def attend_backward(queries, key_all, value_all, labels, log_totals, attended_grad, score_scale):
-    block_rows = min(512, queries.shape[0])
-    query_parts = []
-    key_grad = jnp.zeros(key_all.shape, jnp.float32)
-    value_grad = jnp.zeros(value_all.shape, jnp.float32)
-    for offset in range(0, queries.shape[0], block_rows):
-        query_part = queries[offset : offset + block_rows]
-        grad_part = attended_grad[offset : offset + block_rows]
-        scores = (
-            jnp.einsum("qhd,khd->hqk", query_part, key_all, preferred_element_type=jnp.float32)
-            * score_scale
-        )
-        probability = jnp.where(
-            allowed_mask(labels, offset, block_rows)[None],
-            jnp.exp(scores - log_totals[:, offset : offset + block_rows]),
-            0.0,
-        )
-        prob_grad = jnp.einsum(
-            "qhd,khd->hqk", grad_part, value_all, preferred_element_type=jnp.float32
-        )
-        row_inner = jnp.sum(probability * prob_grad, axis=-1, keepdims=True)
-        score_grad = (probability * (prob_grad - row_inner)).astype(jnp.bfloat16)
-        query_parts.append(
-            jnp.einsum("hqk,khd->qhd", score_grad, key_all, preferred_element_type=jnp.float32)
-            * score_scale
-        )
-        key_grad = (
-            key_grad
-            + jnp.einsum("hqk,qhd->khd", score_grad, query_part, preferred_element_type=jnp.float32)
-            * score_scale
-        )
-        value_grad = value_grad + jnp.einsum(
-            "hqk,qhd->khd",
-            probability.astype(jnp.bfloat16),
-            grad_part,
-            preferred_element_type=jnp.float32,
-        )
-    return (jnp.concatenate(query_parts, axis=0), key_grad, value_grad)
+def heads_major(rows, head_size):
+    return rows.reshape(rows.shape[0], -1, head_size).transpose(1, 0, 2)
+
+
+def heads_beside(stacked):
+    return stacked.transpose(1, 0, 2).reshape(stacked.shape[1], -1)
+
+
+def full_norm(row_values, gain_full, shift_full):
+    mean_row = jnp.sum(row_values, axis=1, keepdims=True) / D
+    var_row = jnp.sum(row_values * row_values, axis=1, keepdims=True) / D - mean_row * mean_row
+    inverse = lax.rsqrt(var_row + NORM_EPS)
+    normed = (row_values - mean_row) * inverse
+    return (normed * gain_full + shift_full, normed, inverse)
 
 
 def body(
@@ -172,28 +232,35 @@
     token_rows = inputs.T
     out_grad = cotangent.T.astype(jnp.float32)
     token_count = token_rows.shape[0]
-    heads_shape = (token_count, -1, head_size)
+    own_features = token_rows.shape[1]
+    own_start = lax.axis_index("col") * own_features
     inputs_full = feature_whole(token_rows)
     qkv_stack = jnp.stack([query_weight, key_weight, value_weight])
     projected, qkv_complete = project_in(inputs_full, qkv_stack)
-    queries = (projected[0] + query_bias).astype(jnp.bfloat16)
-    key_all = projected[1].astype(jnp.bfloat16)
-    value_all = (projected[2] + value_bias).astype(jnp.bfloat16)
-    attended_f, log_totals = attend_forward(
-        queries.reshape(heads_shape),
-        key_all.reshape(heads_shape),
-        value_all.reshape(heads_shape),
-        labels,
-        score_scale,
-    )
-    attended = attended_f.reshape(token_count, -1).astype(jnp.bfloat16)
-    output_complete = columns_whole(output_weight)
-    attn_branch = feature_sum(
-        jnp.dot(attended, output_complete, preferred_element_type=jnp.float32)
-    )
-    first_sum = token_rows.astype(jnp.float32) + attn_branch + output_bias
-    hidden, normed_one, inverse_one = norm_forward(first_sum, attn_gain, attn_shift)
-    hidden_full = feature_whole(hidden.astype(jnp.bfloat16))
+    queries = heads_major((projected[0] + query_bias).astype(jnp.bfloat16), head_size)
+    key_all = heads_major(projected[1].astype(jnp.bfloat16), head_size)
+    value_all = heads_major((projected[2] + value_bias).astype(jnp.bfloat16), head_size)
+    attended_h, row_max, row_total = attention_forward(
+        queries, key_all, value_all, labels, score_scale
+    )
+    attended = heads_beside(attended_h)
+    attended_full = feature_whole(attended)
+    output_rows = columns_whole(output_weight)
+    output_complete = lax.all_gather(output_rows, "col", axis=0, tiled=True)
+    output_bias_full = lax.all_gather(output_bias, "col", axis=0, tiled=True)
+    gain_one_full = lax.all_gather(attn_gain, "col", axis=0, tiled=True)
+    shift_one_full = lax.all_gather(attn_shift, "col", axis=0, tiled=True)
+    first_sum_full = (
+        inputs_full.astype(jnp.float32)
+        + jnp.dot(attended_full, output_complete, preferred_element_type=jnp.float32)
+        + output_bias_full
+    )
+    hidden_full_f, normed_one_full, inverse_one = full_norm(
+        first_sum_full, gain_one_full, shift_one_full
+    )
+    hidden = lax.dynamic_slice_in_dim(hidden_full_f, own_start, own_features, axis=1)
+    normed_one = lax.dynamic_slice_in_dim(normed_one_full, own_start, own_features, axis=1)
+    hidden_full = hidden_full_f.astype(jnp.bfloat16)
     up_stack = up_weight[None]
     up_projected, up_complete = project_in(hidden_full, up_stack)
     upped = up_projected[0] + up_bias
@@ -221,21 +288,22 @@
     attn_branch_grad = first_grad.astype(jnp.bfloat16)
     attn_branch_full = feature_whole(attn_branch_grad)
     output_weight_grad = weight_grad(attn_branch_full, attended).T
-    attended_grad = project_out_back(attn_branch_full, output_weight, output_complete).astype(
+    attended_grad = project_out_back(attn_branch_full, output_weight, output_rows).astype(
         jnp.bfloat16
     )
-    query_grad_f, key_grad_f, value_grad_f = attend_backward(
-        queries.reshape(heads_shape),
-        key_all.reshape(heads_shape),
-        value_all.reshape(heads_shape),
+    query_grad_h, key_grad_h, value_grad_h = attention_backward(
+        queries,
+        key_all,
+        value_all,
+        heads_major(attended_grad, head_size),
         labels,
-        log_totals,
-        attended_grad.reshape(heads_shape),
+        row_max,
+        row_total,
         score_scale,
     )
-    query_grad = query_grad_f.reshape(token_count, -1).astype(jnp.bfloat16)
-    key_grad = key_grad_f.reshape(token_count, -1).astype(jnp.bfloat16)
-    value_grad = value_grad_f.reshape(token_count, -1).astype(jnp.bfloat16)
+    query_grad = heads_beside(query_grad_h)
+    key_grad = heads_beside(key_grad_h).astype(jnp.bfloat16)
+    value_grad = heads_beside(value_grad_h).astype(jnp.bfloat16)
     column_count = query_weight.shape[1]
     qkv_grads = weight_grad(
         inputs_full, jnp.concatenate([query_grad, key_grad, value_grad], axis=1)

time: 1010 us -> 900 us (0.89)
  matrix products: 213 us -> 87.2 us
  Pallas kernels: 0 us -> 116 us
  other arithmetic: 103 us -> 40.6 us
  waiting for transfers between devices: 507 us -> 459 us
  local copies, waits for them, and re-layouts: 14.6 us -> 31.5 us
    dot_general x25 -> x1, matrix products: 139 us -> 6.91 us  [body(): jnp.dot(attended_full, output_complete, preferred_element_type=jnp.float32)]
    pallas_call x0 -> x2, Pallas kernels: none -> 116 us  [the longest x1 68.6 us: attention_backward(): pl.pallas_call(functools.partial(_bwd_kernel, scale), grid=grid, in_specs...]
    reduce_scatter x4 -> x3, waiting for transfers between devices: 238 us -> 177 us  [feature_sum(): lax.psum_scatter(partial_rows, 'col', scatter_dimension=1, tiled=True)]
    convert_element_type x5 -> x1, other arithmetic: 43.5 us -> 2.09 us  [body(): key_grad = heads_beside(key_grad_h).astype(jnp.bfloat16)]
    all_gather x1, waiting for transfers between devices: 0.02 us -> 28.9 us  [project_in(): complete = lax.all_gather(stacked, 'row', axis=1, tiled=True)]
    reduce_sum x4 -> x1, other arithmetic: 27 us -> 2.21 us  [body(): jnp.sum(value_grad.astype(jnp.float32), axis=0)]
    all_gather x4, waiting for transfers between devices: 85.8 us -> 73.8 us  [feature_whole(): return lax.all_gather(blocked, 'col', axis=1, tiled=True)]
    unnamed x0 -> x1, blocking collectives: none -> 10.9 us
  transfers between devices with their start and end apart: 14 -> 14, of which waited for: 11 -> 11; matrix products, arithmetic and copies ran while one was open for 12% -> 12% of each run, Pallas kernels for 0% -> 13%
where the time goes in v1:
time: 900 us; the launch traced here: 891 us
  waiting for transfers between devices  459 us (51%)
  blocking collectives  141 us (16%)
  Pallas kernels  116 us (13%)
  matrix products  87.2 us (10%)
  other arithmetic  40.6 us (5%)
  local copies, waits for them, and re-layouts  31.5 us (4%)
  between operations  15.1 us (2%)
    reduce_scatter x3, waiting for transfers between devices, feature_sum(): lax.psum_scatter(partial_rows, 'col', scatter_dimension=1, tiled=True)  177 us
    reduce_scatter x3, waiting for transfers between devices, weight_grad(): lax.psum_scatter(lax.dot_general(columns, local_grad, (((0,), (0,)), ((),...  143 us
    all_gather x4, waiting for transfers between devices, feature_whole(): return lax.all_gather(blocked, 'col', axis=1, tiled=True)  73.8 us
    pallas_call x1, Pallas kernels, attention_backward(): pl.pallas_call(functools.partial(_bwd_kernel, scale), grid=grid, in_specs...  68.6 us
    pallas_call x1, Pallas kernels, attention_forward(): pl.pallas_call(functools.partial(_fwd_kernel, scale), grid=grid, in_specs...  47 us
    all_gather x1, blocking collectives, project_in(): complete = lax.all_gather(stacked, 'row', axis=1, tiled=True)  36.7 us
    psum x3, blocking collectives, row_totals(): lax.psum((jnp.sum(first_term, axis=1), jnp.sum(second_term, axis=1)), 'col')  34 us
    psum x1, blocking collectives, body(): lax.psum((jnp.sum(query_grad.astype(jnp.float32), axis=0), jnp.sum(value_...  30.5 us
  transfers between devices with their start and end apart: 14, of which 11 were waited for; matrix products, arithmetic and copies ran while one was open for 12% of the time, Pallas kernels for 13%

profile of v1, /device:TPU:12, one launch (start us, length us, event | category | flops | bytes accessed | tf_op | source)
XLA Modules:
  0.0 890.7 jit_solution(822924446962315003)
XLA Ops:
  8.9 28.9 %all_gather.43 = bf16[192,768]{0,1:T(8,128)(2,1)S(1)} all-gather(bf16[192,96]{0,1:T(8,128)(2,1)S(1)} %copy.112), channel_id=1, replica_groups=mesh['row'=8,'col'=4] {'row'}, dimensions={1}, use_global_device_ids=true | all-gather | bytes 331776 | tf_op jit(solution)/shard_map/all_gather | solution.py:171
  39.7 36.7 %all_gather.41 = bf16[3,768,192]{2,0,1:T(4,128)(2,1)S(1)} all-gather(bf16[3,96,192]{2,0,1:T(4,128)(2,1)S(1)} %copy.105), channel_id=1, replica_groups=mesh['row'=8,'col'=4] {'row'}, dimensions={1}, use_global_device_ids=true | all-gather | bytes 995328 | tf_op jit(solution)/shard_map/all_gather | solution.py:158
  88.6 4.6 fusion.27
  93.2 47.0 %shard_map.305 = (bf16[3,2048,64]{2,1,0:T(8,128)(2,1)S(1)}, f32[3,2048,1]{2,1,0:T(8,128)}, f32[3,2048,1]{2,1,0:T(8,128)}) custom-call(bf16[3,2048,64]{2,1,0:T(8,128)(2,1)S(1)} %get-tuple-element.169.q_ref, bf16[3,2048,64]{2,1,0:T(8,128)(2,1)S(1)} %bitcast.90, bf16[3,2048,64]{2,1,0:T(8,128)(2,1)} %get-tuple-element.170.v_ref, s32[2048,1]{1,0:T(8,128)S(1)} %copy-done.2, ...), custom_call_target="tpu_custom_call" | custom-call | flops 3221225472 | bytes 3145728 | tf_op jit(solution)/shard_map/pallas_call | solution.py:79
  146.1 10.9 %all-reduce.7 = (f32[768]{0:T(1024)S(1)}, f32[768]{0:T(1024)S(1)}, f32[768]{0:T(1024)S(1)}) all-reduce(f32[768]{0:T(1024)S(1)} %dynamic-update-slice, f32[768]{0:T(1024)S(1)} %dynamic-update-slice.2, f32[768]{0:T(1024)S(1)} %dynamic-update-slice.1), channel_id=1, replica_groups=mesh['row'=8,'col'=4] {'col'}, use_global_device_ids=true, to_apply=%add | all-reduce | flops 2304 | bytes 18432
  157.0 15.7 %all-gather.11.cloned.1.call-done = bf16[2048,768]{0,1:T(8,128)(2,1)} async-done(((bf16[2048,192]{0,1:T(8,128)(2,1)}), bf16[2048,768]{0,1:T(8,128)(2,1)}) %all-gather.11.cloned.1.call-update) | async-done | bytes 3145744 | tf_op jit(solution)/shard_map/all_gather | solution.py:130
  172.7 6.9 fusion.45
  179.6 5.8 multiply_add_fusion
  185.4 28.9 %all-gather.21.cloned.1.call-done = bf16[768,768]{1,0:T(8,128)(2,1)} async-done(((bf16[96,768]{1,0:T(8,128)(2,1)}), bf16[768,768]{1,0:T(8,128)(2,1)}) %all-gather.21.cloned.1.call-update) | async-done | bytes 1179664 | tf_op jit(solution)/shard_map/all_gather | solution.py:158
  214.3 19.6 %multiply_convert_fusion = (bf16[2048,768]{1,0:T(8,128)(2,1)}, f32[2048,768]{1,0:T(8,128)}, f32[2048,768]{1,0:T(8,128)}) fusion(f32[768]{0:T(1024)S(1)} %copy-done.31, bf16[768,768]{1,0:T(8,128)(2,1)} %all-gather.21.cloned.1.call-done, f32[2048,768]{0,1:T(8,128)} %get-tuple-element.153), kind=kOutput, calls=%fused_computation.4 | convolution fusion | flops 2521300992 | bytes 23202816 | tf_op jit(solution)/shard_map/td,kdc->ktc/dot_general | solution.py:160
  233.9 22.3 %all-gather.15.cloned.1.call-done = bf16[768,768]{0,1:T(8,128)(2,1)} async-done(((bf16[768,96]{0,1:T(8,128)(2,1)}), bf16[768,768]{0,1:T(8,128)(2,1)}) %all-gather.15.cloned.1.call-update) | async-done | bytes 1179664 | tf_op jit(solution)/shard_map/all_gather | solution.py:171
  256.2 7.5 fusion.53
  263.8 59.3 %reduce-scatter.10.cloned.1.call-done = f32[2048,192]{0,1:T(8,128)} async-done(((f32[2048,768]{0,1:T(8,128)}), f32[2048,192]{0,1:T(8,128)}) %reduce-scatter.10.cloned.1.call-update) | async-done | bytes 1572880 | tf_op jit(solution)/shard_map/reduce_scatter | solution.py:134
  326.0 11.7 %all-reduce.6 = (f32[2048]{0:T(1024)}, f32[2048]{0:T(1024)}) all-reduce(f32[2048]{0:T(1024)} %get-tuple-element.123, f32[2048]{0:T(1024)} %get-tuple-element.122), channel_id=1, replica_groups=mesh['row'=8,'col'=4] {'col'}, use_global_device_ids=true, to_apply=%region_6.0 | all-reduce | flops 4096 | bytes 32768 | tf_op jit(solution)/shard_map/psum | solution.py:138
  341.7 11.3 %all-reduce.5 = (f32[2048]{0:T(1024)}, f32[2048]{0:T(1024)}) all-reduce(f32[2048]{0:T(1024)} %get-tuple-element.119, f32[2048]{0:T(1024)} %get-tuple-element.124), channel_id=1, replica_groups=mesh['row'=8,'col'=4] {'col'}, use_global_device_ids=true, to_apply=%region_10.0 | all-reduce | flops 4096 | bytes 32768 | tf_op jit(solution)/shard_map/psum | solution.py:138
  357.7 29.1 %all-gather.17.cloned.1.call-done = bf16[2048,768]{0,1:T(8,128)(2,1)} async-done(((bf16[2048,192]{0,1:T(8,128)(2,1)}), bf16[2048,768]{0,1:T(8,128)(2,1)}) %all-gather.17.cloned.1.call-update) | async-done | bytes 3145744 | tf_op jit(solution)/shard_map/all_gather | solution.py:130
  386.7 11.4 %convert_reduce_fusion = (f32[768]{0:T(1024)}, bf16[2048,768]{1,0:T(8,128)(2,1)S(1)}) fusion(f32[2048,768]{1,0:T(8,128)} %get-tuple-element.152, f32[2048,768]{1,0:T(8,128)} %get-tuple-element.168, f32[768]{0:T(1024)} %param.30, bf16[2048,768]{0,1:T(8,128)(2,1)} %all-gather.17.cloned.1.call-done, bf16[768,768]{0,1:T(8,128)(2,1)} %all-gather.15.cloned.1.call-done), kind=kOutput, calls=%fused_computation.2 | convolution fusion | flops 2442657024 | bytes 20060160 | tf_op jit(solution)/shard_map/dot_general | solution.py:177
  399.9 4.6 fusion.54
  404.5 58.9 %reduce-scatter.12.cloned.1.call-done = f32[2048,192]{0,1:T(8,128)} async-done(((f32[2048,768]{0,1:T(8,128)}), f32[2048,192]{0,1:T(8,128)}) %reduce-scatter.12.cloned.1.call-update) | async-done | bytes 1572880 | tf_op jit(solution)/shard_map/reduce_scatter | solution.py:134
  463.5 5.3 multiply_reduce_fusion.1
  468.7 11.0 %all-reduce.4 = (f32[2048]{0:T(1024)S(1)}, f32[2048]{0:T(1024)S(1)}) all-reduce(f32[2048]{0:T(1024)} %get-tuple-element.115, f32[2048]{0:T(1024)} %get-tuple-element.120), channel_id=1, replica_groups=mesh['row'=8,'col'=4] {'col'}, use_global_device_ids=true, to_apply=%region_15.0 | all-reduce | flops 4096 | bytes 32768 | tf_op jit(solution)/shard_map/psum | solution.py:138
  483.6 29.1 %all-gather.19.cloned.1.call-done = bf16[2048,768]{0,1:T(8,128)(2,1)} async-done(((bf16[2048,192]{0,1:T(8,128)(2,1)}), bf16[2048,768]{0,1:T(8,128)(2,1)}) %all-gather.19.cloned.1.call-update) | async-done | bytes 3145744 | tf_op jit(solution)/shard_map/all_gather | solution.py:130
  523.8 68.6 %shard_map.306 = (bf16[3,2048,64]{2,1,0:T(8,128)(2,1)S(1)}, f32[3,2048,64]{2,1,0:T(8,128)}, f32[3,2048,64]{2,1,0:T(8,128)}) custom-call(bf16[3,2048,64]{2,1,0:T(8,128)(2,1)S(1)} %copy-done.1, bf16[3,2048,64]{2,1,0:T(8,128)(2,1)S(1)} %bitcast.91, bf16[3,2048,64]{2,1,0:T(8,128)(2,1)} %get-tuple-element.170.v_ref, bf16[3,2048,64]{2,1,0:T(8,128)(2,1)} %bitcast.99, ...), custom_call_target="tpu_custom_call" | custom-call | flops 8053063680 | bytes 6291456 | tf_op jit(solution)/shard_map/pallas_call | solution.py:107
  601.2 5.7 fusion.33
  609.9 6.3 convolution_bitcast_fusion
  616.2 7.0 fusion.56
  623.5 7.8 fusion.29
  633.4 30.5 %all-reduce.3 = (f32[192]{0:T(256)}, f32[192]{0:T(256)}, f32[192]{0:T(256)}, f32[192]{0:T(256)}, f32[192]{0:T(256)}, /*index=5*/f32[768]{0:T(1024)}, f32[192]{0:T(256)}, f32[192]{0:T(256)}, f32[192]{0:T(256)}) all-reduce(f32[192]{0:T(256)S(1)} %reduce_sum.166, f32[192]{0:T(256)S(1)} %reduce_sum.168, ...), channel_id=1, replica_groups=mesh['row'=8,'col'=4] {'row'}, use_global_device_ids=true, to_apply=%region_19.0 | all-reduce | flops 2304 | bytes 18432 | tf_op jit(solution)/shard_map/psum | solution.py:314
  665.5 11.5 %reduce-scatter.22.cloned.1.call-done = f32[96,576]{1,0:T(8,128)} async-done(((f32[768,576]{1,0:T(8,128)}), f32[96,576]{1,0:T(8,128)}) %reduce-scatter.22.cloned.1.call-update) | async-done | bytes 221200
  678.8 59.3 %reduce-scatter.14.cloned.1.call-done = f32[2048,192]{0,1:T(8,128)} async-done(((f32[2048,768]{0,1:T(8,128)}), f32[2048,192]{0,1:T(8,128)}) %reduce-scatter.14.cloned.1.call-update) | async-done | bytes 1572880 | tf_op jit(solution)/shard_map/reduce_scatter | solution.py:134
  741.4 69.8 %reduce-scatter.20.cloned.1.call-done = f32[96,768]{1,0:T(8,128)} async-done(((f32[768,768]{1,0:T(8,128)}), f32[96,768]{1,0:T(8,128)}) %reduce-scatter.20.cloned.1.call-update) | async-done | bytes 294928 | tf_op jit(solution)/shard_map/reduce_scatter | solution.py:183
  811.2 72.8 %reduce-scatter.18.cloned.1.call-done = f32[96,768]{1,0:T(8,128)} async-done(((f32[768,768]{1,0:T(8,128)}), f32[96,768]{1,0:T(8,128)}) %reduce-scatter.18.cloned.1.call-update) | async-done | bytes 294928 | tf_op jit(solution)/shard_map/reduce_scatter | solution.py:183
  (144 shorter events, 70.0 us)
Async XLA Ops:
  7.2 69.3 %copy-start.27 = (f32[192]{0:T(256)S(1)}, f32[192]{0:T(256)}, u32[]{:S(2)}) copy-start(f32[192]{0:T(256)} %param.23) | copy-start | bytes 2308
  7.2 69.3 %copy-start.28 = (f32[192]{0:T(256)S(1)}, f32[192]{0:T(256)}, u32[]{:S(2)}) copy-start(f32[192]{0:T(256)} %param.24) | copy-start | bytes 2308
  7.2 69.4 %copy-start.4 = (s32[1,2048]{1,0:T(1,128)S(1)}, s32[1,2048]{1,0:T(1,128)}, u32[]{:S(2)}) copy-start(s32[1,2048]{1,0:T(1,128)} %lk_ref.3) | copy-start | bytes 24580
  7.2 70.8 %all-gather.9.cloned.1.call-start = ((), (), s32[]{:S(2)}) async-start(), calls=%async_computation.7 | async-start | bytes 3932160 | tf_op jit(solution)/shard_map/all_gather | solution.py:130
  8.0 149.0 %all-gather.13.cloned.1.call-start = ((), (), s32[]{:S(2)}) async-start(), calls=%async_computation.9 | async-start | bytes 1474560 | tf_op jit(solution)/shard_map/all_gather | solution.py:249
  38.7 134.0 %all-gather.11.cloned.1.call-start = ((), (), s32[]{:S(2)}) async-start(), calls=%async_computation.8 | async-start | bytes 3932160 | tf_op jit(solution)/shard_map/all_gather | solution.py:130
  76.4 5.5 copy-start.6
  88.5 4.6 copy-start.2
  93.1 47.0 %copy-start = (bf16[3,2048,64]{2,1,0:T(8,128)(2,1)}, bf16[3,2048,64]{2,1,0:T(8,128)(2,1)S(1)}, u32[]{:S(2)}) copy-start(bf16[3,2048,64]{2,1,0:T(8,128)(2,1)S(1)} %get-tuple-element.169.q_ref) | copy-start | bytes 2359300
  140.2 4.6 copy-start.29
  140.2 4.8 copy-start.19
  141.6 72.7 %all-gather.21.cloned.1.call-start = ((), (), s32[]{:S(2)}) async-start(), calls=%async_computation.19 | async-start | bytes 1327104 | tf_op jit(solution)/shard_map/all_gather | solution.py:158
  142.2 114.0 %all-gather.15.cloned.1.call-start = ((), (), s32[]{:S(2)}) async-start(), calls=%async_computation.10 | async-start | bytes 1327104 | tf_op jit(solution)/shard_map/all_gather | solution.py:171
  142.8 180.3 %reduce-scatter.10.cloned.1.call-start = ((), (), s32[]{:S(2)}) async-start(), calls=%async_computation.11 | async-start | bytes 7864320 | tf_op jit(solution)/shard_map/reduce_scatter | solution.py:134
  179.6 34.7 %copy-start.31 = (f32[768]{0:T(1024)S(1)}, f32[768]{0:T(1024)}, u32[]{:S(2)}) copy-start(f32[768]{0:T(1024)} %param.30) | copy-start | bytes 9220
  263.8 123.0 %all-gather.17.cloned.1.call-start = ((), (), s32[]{:S(2)}) async-start(), calls=%async_computation.12 | async-start | bytes 3932160 | tf_op jit(solution)/shard_map/all_gather | solution.py:130
  338.4 3.3 copy-start.12
  357.6 105.8 %reduce-scatter.12.cloned.1.call-start = ((), (), s32[]{:S(2)}) async-start(), calls=%async_computation.13 | async-start | bytes 7864320 | tf_op jit(solution)/shard_map/reduce_scatter | solution.py:134
  386.7 13.1 %copy-start.30 = (bf16[768,768]{1,0:T(8,128)(2,1)S(1)}, bf16[768,768]{1,0:T(8,128)(2,1)}, u32[]{:S(2)}) copy-start(bf16[768,768]{1,0:T(8,128)(2,1)} %all-gather.21.cloned.1.call-done) | copy-start | bytes 3538948
  404.5 108.2 %all-gather.19.cloned.1.call-start = ((), (), s32[]{:S(2)}) async-start(), calls=%async_computation.14 | async-start | bytes 3932160 | tf_op jit(solution)/shard_map/all_gather | solution.py:130
  468.7 43.9 %copy-start.8 = (bf16[2048,3,64]{0,2,1:T(8,128)(2,1)S(1)}, bf16[2048,3,64]{0,2,1:T(8,128)(2,1)}, u32[]{:S(2)}) copy-start(bf16[2048,3,64]{0,2,1:T(8,128)(2,1)} %copy.111) | copy-start | bytes 2359300
  479.7 36.7 %copy-start.13 = (f32[2048]{0:T(1024)}, f32[2048]{0:T(1024)S(1)}, u32[]{:S(2)}) copy-start(f32[2048]{0:T(1024)S(1)} %broadcast_multiply_fusion) | copy-start | bytes 24580
  479.8 36.7 %copy-start.15 = (f32[2048]{0:T(1024)}, f32[2048]{0:T(1024)S(1)}, u32[]{:S(2)}) copy-start(f32[2048]{0:T(1024)S(1)} %broadcast_multiply_fusion.1) | copy-start | bytes 24580
  483.5 180.3 %reduce-scatter.16.cloned.1.call-start = ((), (), s32[]{:S(2)}) async-start(), calls=%async_computation.16 | async-start | bytes 884736 | tf_op jit(solution)/shard_map/reduce_scatter | solution.py:183
  516.4 160.5 %reduce-scatter.22.cloned.1.call-start = ((), (), s32[]{:S(2)}) async-start(), calls=%async_computation.20 | async-start | bytes 2211840
  609.8 128.3 %reduce-scatter.14.cloned.1.call-start = ((), (), s32[]{:S(2)}) async-start(), calls=%async_computation.15 | async-start | bytes 7864320 | tf_op jit(solution)/shard_map/reduce_scatter | solution.py:134
  616.2 195.0 %reduce-scatter.20.cloned.1.call-start = ((), (), s32[]{:S(2)}) async-start(), calls=%async_computation.18 | async-start | bytes 2654208 | tf_op jit(solution)/shard_map/reduce_scatter | solution.py:183
  623.3 260.7 %reduce-scatter.18.cloned.1.call-start = ((), (), s32[]{:S(2)}) async-start(), calls=%async_computation.17 | async-start | bytes 2654208 | tf_op jit(solution)/shard_map/reduce_scatter | solution.py:183
  631.3 106.8 %copy-start.5 = (f32[2048,192]{0,1:T(8,128)S(1)}, f32[2048,192]{0,1:T(8,128)}, u32[]{:S(2)}) copy-start(f32[2048,192]{0,1:T(8,128)} %get-tuple-element.149) | copy-start | bytes 4718596
  631.3 106.7 %copy-start.14 = (f32[2048]{0:T(1024)S(1)}, f32[2048]{0:T(1024)}, u32[]{:S(2)}) copy-start(f32[2048]{0:T(1024)} %copy-done.13) | copy-start | bytes 24580
  631.3 106.7 %copy-start.16 = (f32[2048]{0:T(1024)S(1)}, f32[2048]{0:T(1024)}, u32[]{:S(2)}) copy-start(f32[2048]{0:T(1024)} %copy-done.15) | copy-start | bytes 24580
  631.3 106.7 %copy-start.20 = (f32[192]{0:T(256)S(1)}, f32[192]{0:T(256)}, u32[]{:S(2)}) copy-start(f32[192]{0:T(256)} %param.27) | copy-start | bytes 2308
  (15 other events, 27.3 us)
Sparse Core Ops, SparseCore 0:
  9.6 29.6 all-gather.8
  41.4 18.2 all-gather.12
  141.7 30.9 all-gather.10
  174.7 39.5 all-gather.20
  216.4 39.8 all-gather.14
  263.9 59.1 reduce-scatter.9
  357.7 28.9 all-gather.16
  404.6 58.8 reduce-scatter.11
  483.6 28.9 all-gather.18
  516.6 63.0 reduce-scatter.15
  609.9 67.0 reduce-scatter.21
  679.4 58.6 reduce-scatter.13
  742.1 68.9 reduce-scatter.19
  815.1 68.8 reduce-scatter.17

commit v2 on v1

--- a/solution.py
+++ b/solution.py
@@ -188,6 +188,29 @@
         scatter_dimension=0,
         tiled=True,
     )
+
+
+def rows_gathered(block, axis):
+    pieces = lax.all_gather(block, "row", axis=0, tiled=False)
+    pieces = jnp.moveaxis(pieces, 0, axis)
+    shape = list(block.shape)
+    shape[axis] = shape[axis] * pieces.shape[axis]
+    return pieces.reshape(shape)
+
+
+def rows_gathered_many(blocks_and_axes):
+    flat = jnp.concatenate([block.reshape(-1) for block, _ in blocks_and_axes])
+    pieces = lax.all_gather(flat, "row", axis=0, tiled=False)
+    wholes = []
+    offset = 0
+    for block, axis in blocks_and_axes:
+        piece = pieces[:, offset : offset + block.size].reshape((-1,) + block.shape)
+        offset += block.size
+        piece = jnp.moveaxis(piece, 0, axis)
+        shape = list(block.shape)
+        shape[axis] = shape[axis] * piece.shape[axis]
+        wholes.append(piece.reshape(shape))
+    return wholes
 
 
 def heads_major(rows, head_size):
@@ -236,7 +259,15 @@
     own_start = lax.axis_index("col") * own_features
     inputs_full = feature_whole(token_rows)
     qkv_stack = jnp.stack([query_weight, key_weight, value_weight])
-    projected, qkv_complete = project_in(inputs_full, qkv_stack)
+    with jax.named_scope("weights_in"):
+        qkv_complete, output_rows = rows_gathered_many(((qkv_stack, 1), (output_weight, 1)))
+    with jax.named_scope("weights_out"):
+        output_complete = lax.all_gather(output_rows, "col", axis=0, tiled=True)
+    with jax.named_scope("weights_ffn"):
+        up_complete, down_complete = rows_gathered_many(((up_weight, 0), (down_weight, 1)))
+    projected = jnp.einsum(
+        "td,kdc->ktc", inputs_full, qkv_complete, preferred_element_type=jnp.float32
+    )
     queries = heads_major((projected[0] + query_bias).astype(jnp.bfloat16), head_size)
     key_all = heads_major(projected[1].astype(jnp.bfloat16), head_size)
     value_all = heads_major((projected[2] + value_bias).astype(jnp.bfloat16), head_size)
@@ -245,8 +276,6 @@
     )
     attended = heads_beside(attended_h)
     attended_full = feature_whole(attended)
-    output_rows = columns_whole(output_weight)
-    output_complete = lax.all_gather(output_rows, "col", axis=0, tiled=True)
     output_bias_full = lax.all_gather(output_bias, "col", axis=0, tiled=True)
     gain_one_full = lax.all_gather(attn_gain, "col", axis=0, tiled=True)
     shift_one_full = lax.all_gather(attn_shift, "col", axis=0, tiled=True)
@@ -261,12 +290,9 @@
     hidden = lax.dynamic_slice_in_dim(hidden_full_f, own_start, own_features, axis=1)
     normed_one = lax.dynamic_slice_in_dim(normed_one_full, own_start, own_features, axis=1)
     hidden_full = hidden_full_f.astype(jnp.bfloat16)
-    up_stack = up_weight[None]
-    up_projected, up_complete = project_in(hidden_full, up_stack)
-    upped = up_projected[0] + up_bias
+    upped = jnp.dot(hidden_full, up_complete, preferred_element_type=jnp.float32) + up_bias
     acted_f, gelu_pull = jax.vjp(partial(jax.nn.gelu, approximate=False), upped)
     acted = acted_f.astype(jnp.bfloat16)
-    down_complete = columns_whole(down_weight)
     ffn_partial = jnp.dot(acted, down_complete, preferred_element_type=jnp.float32)
     second_sum = hidden + feature_sum(ffn_partial) + down_bias
     result, normed_two, inverse_two = norm_forward(second_sum, final_gain, final_shift)
@@ -276,11 +302,15 @@
     branch_grad = second_grad.astype(jnp.bfloat16)
     branch_full = feature_whole(branch_grad)
     down_weight_grad = weight_grad(branch_full, acted).T
-    acted_grad = project_out_back(branch_full, down_weight, down_complete)
+    acted_grad = lax.dot_general(
+        branch_full, down_complete, (((1,), (1,)), ((), ())), preferred_element_type=jnp.float32
+    )
     upped_grad = gelu_pull(acted_grad)[0].astype(jnp.bfloat16)
     up_weight_grad = weight_grad(hidden_full, upped_grad)
     hidden_grad = second_grad + feature_sum(
-        project_in_back(upped_grad[None], up_stack, up_complete)
+        lax.dot_general(
+            upped_grad, up_complete, (((1,), (1,)), ((), ())), preferred_element_type=jnp.float32
+        )
     )
     first_grad, attn_gain_grad, attn_shift_grad = norm_backward(
         hidden_grad, normed_one, inverse_one, attn_gain
@@ -288,9 +318,9 @@
     attn_branch_grad = first_grad.astype(jnp.bfloat16)
     attn_branch_full = feature_whole(attn_branch_grad)
     output_weight_grad = weight_grad(attn_branch_full, attended).T
-    attended_grad = project_out_back(attn_branch_full, output_weight, output_rows).astype(
-        jnp.bfloat16
-    )
+    attended_grad = lax.dot_general(
+        attn_branch_full, output_rows, (((1,), (1,)), ((), ())), preferred_element_type=jnp.float32
+    ).astype(jnp.bfloat16)
     query_grad_h, key_grad_h, value_grad_h = attention_backward(
         queries,
         key_all,
@@ -309,7 +339,12 @@
         inputs_full, jnp.concatenate([query_grad, key_grad, value_grad], axis=1)
     )
     input_grad = first_grad + feature_sum(
-        project_in_back(jnp.stack([query_grad, key_grad, value_grad]), qkv_stack, qkv_complete)
+        jnp.einsum(
+            "ktc,kdc->td",
+            jnp.stack([query_grad, key_grad, value_grad]),
+            qkv_complete,
+            preferred_element_type=jnp.float32,
+        )
     )
     param_totals = lax.psum(
         (

time: 900 us -> 888 us (0.987)
  blocking collectives: 141 us -> 74.1 us
  waiting for transfers between devices: 459 us -> 500 us
  local copies, waits for them, and re-layouts: 31.5 us -> 56.4 us
    all_gather x2 -> x0, blocking collectives: 65.6 us -> none  [the longest x1 36.7 us: project_in(): complete = lax.all_gather(stacked, 'row', axis=1, tiled=True)]
    all_gather x4, waiting for transfers between devices: 73.8 us -> 100 us  [feature_whole(): return lax.all_gather(blocked, 'col', axis=1, tiled=True)]
    all_gather x2, waiting for transfers between devices: 51.2 us -> 67.4 us  [rows_gathered_many(): pieces = lax.all_gather(flat, 'row', axis=0, tiled=False)]
    reshape x0 -> x10, local copies, waits for them, and re-layouts: none -> 11.9 us  [the longest x3 4.87 us: rows_gathered_many(): wholes.append(piece.reshape(shape))]
  transfers between devices with their start and end apart: 14 -> 14, of which waited for: 11 -> 12; matrix products, arithmetic and copies ran while one was open for 12% -> 11% of each run, Pallas kernels for 13% -> 13%
where the time goes in v2:
time: 888 us; the launch traced here: 880 us
  waiting for transfers between devices  500 us (56%)
  Pallas kernels  116 us (13%)
  matrix products  82.1 us (9%)
  blocking collectives  74.1 us (8%)
  local copies, waits for them, and re-layouts  56.4 us (6%)
  other arithmetic  34.8 us (4%)
  between operations  15.2 us (2%)
    reduce_scatter x3, waiting for transfers between devices, feature_sum(): lax.psum_scatter(partial_rows, 'col', scatter_dimension=1, tiled=True)  177 us
    reduce_scatter x3, waiting for transfers between devices, weight_grad(): lax.psum_scatter(lax.dot_general(columns, local_grad, (((0,), (0,)), ((),...  143 us
    all_gather x4, waiting for transfers between devices, feature_whole(): return lax.all_gather(blocked, 'col', axis=1, tiled=True)  100 us
    pallas_call x1, Pallas kernels, attention_backward(): pl.pallas_call(functools.partial(_bwd_kernel, scale), grid=grid, in_specs...  68.9 us
    all_gather x2, waiting for transfers between devices, rows_gathered_many(): pieces = lax.all_gather(flat, 'row', axis=0, tiled=False)  67.4 us
    pallas_call x1, Pallas kernels, attention_forward(): pl.pallas_call(functools.partial(_fwd_kernel, scale), grid=grid, in_specs...  46.9 us
    psum x3, blocking collectives, row_totals(): lax.psum((jnp.sum(first_term, axis=1), jnp.sum(second_term, axis=1)), 'col')  31.3 us
    psum x1, blocking collectives, body(): lax.psum((jnp.sum(query_grad.astype(jnp.float32), axis=0), jnp.sum(value_...  30.5 us
  transfers between devices with their start and end apart: 14, of which 12 were waited for; matrix products, arithmetic and copies ran while one was open for 11% of the time, Pallas kernels for 13%

profile of v2, /device:TPU:12, one launch (start us, length us, event | category | flops | bytes accessed | tf_op | source)
XLA Modules:
  0.0 880.1 jit_solution(11364591055410620684)
XLA Ops:
  18.2 12.3 %all-reduce.7 = (f32[768]{0:T(1024)}, f32[768]{0:T(1024)}, f32[768]{0:T(1024)}) all-reduce(f32[768]{0:T(1024)S(1)} %dynamic-update-slice, f32[768]{0:T(1024)S(1)} %dynamic-update-slice.2, f32[768]{0:T(1024)S(1)} %dynamic-update-slice.1), channel_id=1, replica_groups=mesh['row'=8,'col'=4] {'col'}, use_global_device_ids=true, to_apply=%add | all-reduce | flops 2304 | bytes 18432
  30.4 21.1 %all-gather.20.cloned.1.call-done = bf16[589824]{0:T(1024)(128)(2,1)} async-done(((bf16[73728]{0:T(1024)(128)(2,1)}), bf16[589824]{0:T(1024)(128)(2,1)}) %all-gather.20.cloned.1.call-update) | async-done | bytes 1179664 | tf_op jit(solution)/shard_map/weights_in/all_gather | solution.py:203
  59.1 46.4 %all-gather.22.cloned.1.call-done = bf16[1179648]{0:T(1024)(128)(2,1)} async-done(((bf16[147456]{0:T(1024)(128)(2,1)}), bf16[1179648]{0:T(1024)(128)(2,1)}) %all-gather.22.cloned.1.call-update) | async-done | bytes 2359312 | tf_op jit(solution)/shard_map/weights_ffn/all_gather | solution.py:203
  105.5 4.1 reshape.174
  109.6 25.4 %all-gather.10.cloned.1.call-done = bf16[2048,768]{0,1:T(8,128)(2,1)} async-done(((bf16[2048,192]{0,1:T(8,128)(2,1)}), bf16[2048,768]{0,1:T(8,128)(2,1)}) %all-gather.10.cloned.1.call-update) | async-done | bytes 3145744 | tf_op jit(solution)/shard_map/all_gather | solution.py:130
  135.1 3.9 convolution_bitcast_fusion.1
  145.6 4.5 fusion.27
  150.1 46.9 %shard_map.305 = (bf16[3,2048,64]{2,1,0:T(8,128)(2,1)S(1)}, f32[3,2048,1]{2,1,0:T(8,128)}, f32[3,2048,1]{2,1,0:T(8,128)}) custom-call(bf16[3,2048,64]{2,1,0:T(8,128)(2,1)S(1)} %get-tuple-element.154.q_ref, bf16[3,2048,64]{2,1,0:T(8,128)(2,1)S(1)} %bitcast.100, bf16[3,2048,64]{2,1,0:T(8,128)(2,1)} %get-tuple-element.155.v_ref, s32[2048,1]{1,0:T(8,128)S(1)} %copy-done.2, ...), custom_call_target="tpu_custom_call" | custom-call | flops 3221225472 | bytes 3145728 | tf_op jit(solution)/shard_map/pallas_call | solution.py:79
  210.3 16.8 %all-gather.12.cloned.1.call-done = bf16[2048,768]{0,1:T(8,128)(2,1)} async-done(((bf16[2048,192]{0,1:T(8,128)(2,1)}), bf16[2048,768]{0,1:T(8,128)(2,1)}) %all-gather.12.cloned.1.call-update) | async-done | bytes 3145744 | tf_op jit(solution)/shard_map/all_gather | solution.py:130
  227.2 6.9 fusion.43
  237.9 18.0 %multiply_convert_fusion = (bf16[2048,768]{1,0:T(8,128)(2,1)S(1)}, f32[2048,768]{1,0:T(8,128)}, f32[2048,768]{1,0:T(8,128)}) fusion(f32[768]{0:T(1024)S(1)} %copy-done.27, bf16[768,768]{1,0:T(8,128)(2,1)S(1)} %copy-done.10, f32[2048,768]{0,1:T(8,128)S(1)} %get-tuple-element.136), kind=kOutput, calls=%fused_computation.4 | convolution fusion | flops 2521300992 | bytes 23202816 | tf_op jit(solution)/shard_map/dot_general | solution.py:293
  257.6 4.6 fusion.52
  262.3 58.9 %reduce-scatter.10.cloned.1.call-done = f32[2048,192]{0,1:T(8,128)} async-done(((f32[2048,768]{0,1:T(8,128)}), f32[2048,192]{0,1:T(8,128)}) %reduce-scatter.10.cloned.1.call-update) | async-done | bytes 1572880 | tf_op jit(solution)/shard_map/reduce_scatter | solution.py:134
  323.5 10.3 %all-reduce.6 = (f32[2048]{0:T(1024)S(1)}, f32[2048]{0:T(1024)S(1)}) all-reduce(f32[2048]{0:T(1024)S(1)} %get-tuple-element.106, f32[2048]{0:T(1024)S(1)} %get-tuple-element.105), channel_id=1, replica_groups=mesh['row'=8,'col'=4] {'col'}, use_global_device_ids=true, to_apply=%region_6.0 | all-reduce | flops 4096 | bytes 32768 | tf_op jit(solution)/shard_map/psum | solution.py:138
  335.9 10.7 %all-reduce.5 = (f32[2048]{0:T(1024)S(1)}, f32[2048]{0:T(1024)S(1)}) all-reduce(f32[2048]{0:T(1024)S(1)} %get-tuple-element.102, f32[2048]{0:T(1024)S(1)} %get-tuple-element.107), channel_id=1, replica_groups=mesh['row'=8,'col'=4] {'col'}, use_global_device_ids=true, to_apply=%region_10.0 | all-reduce | flops 4096 | bytes 32768 | tf_op jit(solution)/shard_map/psum | solution.py:138
  349.2 29.1 %all-gather.16.cloned.1.call-done = bf16[2048,768]{0,1:T(8,128)(2,1)} async-done(((bf16[2048,192]{0,1:T(8,128)(2,1)}), bf16[2048,768]{0,1:T(8,128)(2,1)}) %all-gather.16.cloned.1.call-update) | async-done | bytes 3145744 | tf_op jit(solution)/shard_map/all_gather | solution.py:130
  378.3 10.9 %convert_reduce_fusion = (f32[768]{0:T(1024)S(1)}, bf16[2048,768]{1,0:T(8,128)(2,1)S(1)}) fusion(f32[2048,768]{1,0:T(8,128)} %get-tuple-element.135, f32[2048,768]{1,0:T(8,128)} %get-tuple-element.153, f32[768]{0:T(1024)S(1)} %copy-done.27, bf16[2048,768]{0,1:T(8,128)(2,1)} %all-gather.16.cloned.1.call-done, bf16[768,768]{0,1:T(8,128)(2,1)} %bitcast.114), kind=kOutput, calls=%fused_computation.2 | convolution fusion | flops 2442657024 | bytes 20060160 | tf_op jit(solution)/shard_map/dot_general | solution.py:305
  390.9 4.6 fusion.53
  395.6 58.9 %reduce-scatter.12.cloned.1.call-done = f32[2048,192]{0,1:T(8,128)} async-done(((f32[2048,768]{0,1:T(8,128)}), f32[2048,192]{0,1:T(8,128)}) %reduce-scatter.12.cloned.1.call-update) | async-done | bytes 1572880 | tf_op jit(solution)/shard_map/reduce_scatter | solution.py:134
  454.5 4.7 multiply_reduce_fusion.1
  459.2 10.4 %all-reduce.4 = (f32[2048]{0:T(1024)S(1)}, f32[2048]{0:T(1024)S(1)}) all-reduce(f32[2048]{0:T(1024)S(1)} %get-tuple-element.98, f32[2048]{0:T(1024)S(1)} %get-tuple-element.103), channel_id=1, replica_groups=mesh['row'=8,'col'=4] {'col'}, use_global_device_ids=true, to_apply=%region_15.0 | all-reduce | flops 4096 | bytes 32768 | tf_op jit(solution)/shard_map/psum | solution.py:138
  472.8 29.1 %all-gather.18.cloned.1.call-done = bf16[2048,768]{0,1:T(8,128)(2,1)} async-done(((bf16[2048,192]{0,1:T(8,128)(2,1)}), bf16[2048,768]{0,1:T(8,128)(2,1)}) %all-gather.18.cloned.1.call-update) | async-done | bytes 3145744 | tf_op jit(solution)/shard_map/all_gather | solution.py:130
  512.9 68.9 %shard_map.306 = (bf16[3,2048,64]{2,1,0:T(8,128)(2,1)S(1)}, f32[3,2048,64]{2,1,0:T(8,128)}, f32[3,2048,64]{2,1,0:T(8,128)}) custom-call(bf16[3,2048,64]{2,1,0:T(8,128)(2,1)S(1)} %copy-done.1, bf16[3,2048,64]{2,1,0:T(8,128)(2,1)S(1)} %bitcast.101, bf16[3,2048,64]{2,1,0:T(8,128)(2,1)} %get-tuple-element.155.v_ref, bf16[3,2048,64]{2,1,0:T(8,128)(2,1)} %bitcast.112, ...), custom_call_target="tpu_custom_call" | custom-call | flops 8053063680 | bytes 6291456 | tf_op jit(solution)/shard_map/pallas_call | solution.py:107
  590.5 5.7 fusion.33
  599.2 6.2 convolution_bitcast_fusion
  605.4 7.0 fusion.55
  612.8 7.8 fusion.29
  622.5 30.5 %all-reduce.3 = (f32[192]{0:T(256)}, f32[192]{0:T(256)}, f32[192]{0:T(256)}, f32[192]{0:T(256)}, f32[192]{0:T(256)}, /*index=5*/f32[768]{0:T(1024)}, f32[192]{0:T(256)}, f32[192]{0:T(256)}, f32[192]{0:T(256)}) all-reduce(f32[192]{0:T(256)S(1)} %reduce_sum.166, f32[192]{0:T(256)S(1)} %reduce_sum.168, ...), channel_id=1, replica_groups=mesh['row'=8,'col'=4] {'row'}, use_global_device_ids=true, to_apply=%region_19.0 | all-reduce | flops 2304 | bytes 18432 | tf_op jit(solution)/shard_map/psum | solution.py:349
  654.7 11.5 %reduce-scatter.22.cloned.1.call-done = f32[96,576]{1,0:T(8,128)} async-done(((f32[768,576]{1,0:T(8,128)}), f32[96,576]{1,0:T(8,128)}) %reduce-scatter.22.cloned.1.call-update) | async-done | bytes 221200
  668.0 59.3 %reduce-scatter.14.cloned.1.call-done = f32[2048,192]{0,1:T(8,128)} async-done(((f32[2048,768]{0,1:T(8,128)}), f32[2048,192]{0,1:T(8,128)}) %reduce-scatter.14.cloned.1.call-update) | async-done | bytes 1572880 | tf_op jit(solution)/shard_map/reduce_scatter | solution.py:134
  730.6 69.8 %reduce-scatter.20.cloned.1.call-done = f32[96,768]{1,0:T(8,128)} async-done(((f32[768,768]{1,0:T(8,128)}), f32[96,768]{1,0:T(8,128)}) %reduce-scatter.20.cloned.1.call-update) | async-done | bytes 294928 | tf_op jit(solution)/shard_map/reduce_scatter | solution.py:183
  800.4 72.9 %reduce-scatter.18.cloned.1.call-done = f32[96,768]{1,0:T(8,128)} async-done(((f32[768,768]{1,0:T(8,128)}), f32[96,768]{1,0:T(8,128)}) %reduce-scatter.18.cloned.1.call-update) | async-done | bytes 294928 | tf_op jit(solution)/shard_map/reduce_scatter | solution.py:183
  (159 shorter events, 86.8 us)
Async XLA Ops:
  7.2 9.0 %copy-start.29 = (u32[32]{0:T(128)S(1)}, u32[32]{0:T(128)}, u32[]{:S(2)}) copy-start(u32[32]{0:T(128)} %constant.89) | copy-start | bytes 388
  7.2 7.6 copy-start.4
  7.2 10.2 %copy-start.23 = (f32[192]{0:T(256)S(1)}, f32[192]{0:T(256)}, u32[]{:S(2)}) copy-start(f32[192]{0:T(256)} %param.26) | copy-start | bytes 2308
  7.2 10.5 %copy-start.16 = (f32[192]{0:T(256)S(1)}, f32[192]{0:T(256)}, u32[]{:S(2)}) copy-start(f32[192]{0:T(256)} %param.27) | copy-start | bytes 2308
  7.3 10.7 %copy-start.24 = (f32[192]{0:T(256)S(1)}, f32[192]{0:T(256)}, u32[]{:S(2)}) copy-start(f32[192]{0:T(256)} %param.28) | copy-start | bytes 2308
  7.3 44.2 %all-gather.20.cloned.1.call-start = ((), (), s32[]{:S(2)}) async-start(), calls=%async_computation.18 | async-start | bytes 1327104 | tf_op jit(solution)/shard_map/weights_in/all_gather | solution.py:203
  10.0 95.5 %all-gather.22.cloned.1.call-start = ((), (), s32[]{:S(2)}) async-start(), calls=%async_computation.19 | async-start | bytes 2654208 | tf_op jit(solution)/shard_map/weights_ffn/all_gather | solution.py:203
  13.3 121.8 %all-gather.10.cloned.1.call-start = ((), (), s32[]{:S(2)}) async-start(), calls=%async_computation.7 | async-start | bytes 3932160 | tf_op jit(solution)/shard_map/all_gather | solution.py:130
  14.0 196.3 %all-gather.14.cloned.1.call-start = ((), (), s32[]{:S(2)}) async-start(), calls=%async_computation.9 | async-start | bytes 1474560 | tf_op jit(solution)/shard_map/weights_out/all_gather | solution.py:265
  57.1 77.9 %copy-start.13 = (bf16[3,768,192]{1,2,0:T(8,128)(2,1)}, bf16[3,768,192]{1,2,0:T(8,128)(2,1)S(1)}, u32[]{:S(2)}) copy-start(bf16[3,768,192]{1,2,0:T(8,128)(2,1)S(1)} %reshape.162) | copy-start | bytes 2654212
  58.8 168.3 %all-gather.12.cloned.1.call-start = ((), (), s32[]{:S(2)}) async-start(), calls=%async_computation.8 | async-start | bytes 3932160 | tf_op jit(solution)/shard_map/all_gather | solution.py:130
  150.1 46.9 %copy-start = (bf16[3,2048,64]{2,1,0:T(8,128)(2,1)}, bf16[3,2048,64]{2,1,0:T(8,128)(2,1)S(1)}, u32[]{:S(2)}) copy-start(bf16[3,2048,64]{2,1,0:T(8,128)(2,1)S(1)} %get-tuple-element.154.q_ref) | copy-start | bytes 2359300
  198.5 122.8 %reduce-scatter.10.cloned.1.call-start = ((), (), s32[]{:S(2)}) async-start(), calls=%async_computation.10 | async-start | bytes 7864320 | tf_op jit(solution)/shard_map/reduce_scatter | solution.py:134
  206.0 21.1 %copy-start.28 = (f32[768]{0:T(1024)S(1)}, f32[768]{0:T(1024)}, u32[]{:S(2)}) copy-start(f32[768]{0:T(1024)} %get-tuple-element.123) | copy-start | bytes 9220
  227.1 7.0 copy-start.20
  237.9 18.0 %copy-start.6 = (f32[2048,768]{0,1:T(8,128)}, f32[2048,768]{0,1:T(8,128)S(1)}, u32[]{:S(2)}) copy-start(f32[2048,768]{0,1:T(8,128)S(1)} %get-tuple-element.136) | copy-start | bytes 18874372
  237.9 19.8 %copy-start.12 = (bf16[768,8,96]{0,2,1:T(8,128)(2,1)S(1)}, bf16[768,8,96]{0,2,1:T(8,128)(2,1)}, u32[]{:S(2)}) copy-start(bf16[768,8,96]{0,2,1:T(8,128)(2,1)} %copy.88) | copy-start | bytes 3538948
  262.2 59.0 %copy-start.25 = (f32[192]{0:T(256)S(1)}, f32[192]{0:T(256)}, u32[]{:S(2)}) copy-start(f32[192]{0:T(256)} %param.32) | copy-start | bytes 2308
  262.2 71.6 %copy-start.17 = (f32[192]{0:T(256)S(1)}, f32[192]{0:T(256)}, u32[]{:S(2)}) copy-start(f32[192]{0:T(256)} %param.33) | copy-start | bytes 2308
  262.3 116.1 %all-gather.16.cloned.1.call-start = ((), (), s32[]{:S(2)}) async-start(), calls=%async_computation.11 | async-start | bytes 3932160 | tf_op jit(solution)/shard_map/all_gather | solution.py:130
  349.2 105.3 %reduce-scatter.12.cloned.1.call-start = ((), (), s32[]{:S(2)}) async-start(), calls=%async_computation.12 | async-start | bytes 7864320 | tf_op jit(solution)/shard_map/reduce_scatter | solution.py:134
  378.3 12.6 %copy-start.11 = (bf16[768,768]{1,0:T(8,128)(2,1)S(1)}, bf16[768,768]{1,0:T(8,128)(2,1)}, u32[]{:S(2)}) copy-start(bf16[768,768]{1,0:T(8,128)(2,1)} %reshape.168) | copy-start | bytes 3538948
  395.5 59.0 %copy-start.26 = (f32[192]{0:T(256)S(1)}, f32[192]{0:T(256)}, u32[]{:S(2)}) copy-start(f32[192]{0:T(256)} %param.34) | copy-start | bytes 2308
  395.5 106.4 %all-gather.18.cloned.1.call-start = ((), (), s32[]{:S(2)}) async-start(), calls=%async_computation.13 | async-start | bytes 3932160 | tf_op jit(solution)/shard_map/all_gather | solution.py:130
  459.2 42.7 %copy-start.7 = (bf16[2048,3,64]{0,2,1:T(8,128)(2,1)S(1)}, bf16[2048,3,64]{0,2,1:T(8,128)(2,1)}, u32[]{:S(2)}) copy-start(bf16[2048,3,64]{0,2,1:T(8,128)(2,1)} %copy.85) | copy-start | bytes 2359300
  472.8 33.2 %copy-start.9 = (bf16[192,768]{1,0:T(8,128)(2,1)S(1)}, bf16[192,768]{1,0:T(8,128)(2,1)}, u32[]{:S(2)}) copy-start(bf16[192,768]{1,0:T(8,128)(2,1)} %reshape.165) | copy-start | bytes 884740
  472.8 180.2 %reduce-scatter.16.cloned.1.call-start = ((), (), s32[]{:S(2)}) async-start(), calls=%async_computation.15 | async-start | bytes 884736 | tf_op jit(solution)/shard_map/reduce_scatter | solution.py:183
  505.7 160.5 %reduce-scatter.22.cloned.1.call-start = ((), (), s32[]{:S(2)}) async-start(), calls=%async_computation.20 | async-start | bytes 2211840
  599.1 128.1 %reduce-scatter.14.cloned.1.call-start = ((), (), s32[]{:S(2)}) async-start(), calls=%async_computation.14 | async-start | bytes 7864320 | tf_op jit(solution)/shard_map/reduce_scatter | solution.py:134
  605.4 195.0 %reduce-scatter.20.cloned.1.call-start = ((), (), s32[]{:S(2)}) async-start(), calls=%async_computation.17 | async-start | bytes 2654208 | tf_op jit(solution)/shard_map/reduce_scatter | solution.py:183
  612.5 260.8 %reduce-scatter.18.cloned.1.call-start = ((), (), s32[]{:S(2)}) async-start(), calls=%async_computation.16 | async-start | bytes 2654208 | tf_op jit(solution)/shard_map/reduce_scatter | solution.py:183
  620.6 106.7 %copy-start.5 = (f32[2048,192]{0,1:T(8,128)S(1)}, f32[2048,192]{0,1:T(8,128)}, u32[]{:S(2)}) copy-start(f32[2048,192]{0,1:T(8,128)} %get-tuple-element.132) | copy-start | bytes 4718596
  (14 other events, 48.3 us)
Sparse Core Ops, SparseCore 0:
  10.8 40.6 all-gather.19
  54.3 51.1 all-gather.21
  107.1 27.9 all-gather.9
  137.1 17.4 all-gather.13
  198.6 28.5 all-gather.11
  262.4 58.8 reduce-scatter.9
  349.3 28.9 all-gather.15
  395.6 58.8 reduce-scatter.11
  472.9 28.9 all-gather.17
  505.8 63.0 reduce-scatter.15
  599.2 66.9 reduce-scatter.21
  668.6 58.6 reduce-scatter.13
  731.3 69.0 reduce-scatter.19
  804.3 68.9 reduce-scatter.17

commit v3 on v2

--- a/solution.py
+++ b/solution.py
@@ -177,25 +177,35 @@
     return lax.dot_general(grad_full, complete, contract, preferred_element_type=jnp.float32)
 
 
+def row_scatter_sum(partial_rows):
+    count = lax.axis_size("row")
+    me = lax.axis_index("row")
+    blocks = partial_rows.reshape((count, partial_rows.shape[0] // count) + partial_rows.shape[1:])
+    total = blocks[me]
+    for shift in range(1, count):
+        outgoing = blocks[lax.rem(me + shift, count)]
+        total = total + lax.ppermute(
+            outgoing, "row", [(i, (i + shift) % count) for i in range(count)]
+        )
+    return total
+
+
+def row_sum(values):
+    count = lax.axis_size("row")
+    total = values
+    for shift in range(1, count):
+        total = total + lax.ppermute(
+            values, "row", [(i, (i + shift) % count) for i in range(count)]
+        )
+    return total
+
+
 def weight_grad(gathered, local_grad):
-    own_rows = gathered.shape[1] // lax.axis_size("row")
-    columns = lax.slice_in_dim(gathered, 0, lax.axis_size("row") * own_rows, axis=1)
-    return lax.psum_scatter(
+    return row_scatter_sum(
         lax.dot_general(
-            columns, local_grad, (((0,), (0,)), ((), ())), preferred_element_type=jnp.float32
-        ),
-        "row",
-        scatter_dimension=0,
-        tiled=True,
-    )
-
-
-def rows_gathered(block, axis):
-    pieces = lax.all_gather(block, "row", axis=0, tiled=False)
-    pieces = jnp.moveaxis(pieces, 0, axis)
-    shape = list(block.shape)
-    shape[axis] = shape[axis] * pieces.shape[axis]
-    return pieces.reshape(shape)
+            gathered, local_grad, (((0,), (0,)), ((), ())), preferred_element_type=jnp.float32
+        )
+    )
 
 
 def rows_gathered_many(blocks_and_axes):
@@ -346,20 +356,23 @@
             preferred_element_type=jnp.float32,
         )
     )
-    param_totals = lax.psum(
-        (
-            jnp.sum(query_grad.astype(jnp.float32), axis=0),
-            jnp.sum(value_grad.astype(jnp.float32), axis=0),
-            jnp.sum(attn_branch_grad.astype(jnp.float32), axis=0),
-            attn_gain_grad,
-            attn_shift_grad,
-            jnp.sum(upped_grad.astype(jnp.float32), axis=0),
-            jnp.sum(branch_grad.astype(jnp.float32), axis=0),
-            final_gain_grad,
-            final_shift_grad,
-        ),
-        "row",
-    )
+    param_parts = (
+        jnp.sum(query_grad.astype(jnp.float32), axis=0),
+        jnp.sum(value_grad.astype(jnp.float32), axis=0),
+        jnp.sum(attn_branch_grad.astype(jnp.float32), axis=0),
+        attn_gain_grad,
+        attn_shift_grad,
+        jnp.sum(upped_grad.astype(jnp.float32), axis=0),
+        jnp.sum(branch_grad.astype(jnp.float32), axis=0),
+        final_gain_grad,
+        final_shift_grad,
+    )
+    param_flat = row_sum(jnp.concatenate(param_parts))
+    param_totals = []
+    offset = 0
+    for part in param_parts:
+        param_totals.append(param_flat[offset : offset + part.shape[0]])
+        offset += part.shape[0]
     return (
         result.astype(jnp.bfloat16).T,
         input_grad.astype(jnp.bfloat16).T,

time: 888 us -> 811 us (0.913)
  waiting for transfers between devices: 500 us -> 413 us
  starting transfers between devices: 1.51 us -> 39.2 us
  blocking collectives: 74.1 us -> 42.5 us
    reduce_scatter x3 -> x0, waiting for transfers between devices: 143 us -> none  [weight_grad(): lax.psum_scatter(lax.dot_general(columns, local_grad, (((0,), (0,)), ((),...]
    ppermute x0 -> x35, waiting for transfers between devices: none -> 127 us  [the longest x28 127 us: row_scatter_sum(): lax.ppermute(outgoing, 'row', [(i, (i + shift) % count) for i in range(co...]
    reduce_scatter x3, waiting for transfers between devices: 177 us -> 118 us  [feature_sum(): lax.psum_scatter(partial_rows, 'col', scatter_dimension=1, tiled=True)]
    ppermute x0 -> x35, starting transfers between devices: none -> 37.7 us  [the longest x28 26.6 us: row_scatter_sum(): lax.ppermute(outgoing, 'row', [(i, (i + shift) % count) for i in range(co...]
    psum x1 -> x0, blocking collectives: 30.5 us -> none  [body(): lax.psum((jnp.sum(query_grad.astype(jnp.float32), axis=0), jnp.sum(value_...]
    unnamed x15 -> x10, waiting for transfers between devices: 12.4 us -> 0.83 us
  transfers between devices with their start and end apart: 14 -> 45, of which waited for: 12 -> 26; matrix products, arithmetic and copies ran while one was open for 11% -> 10% of each run, Pallas kernels for 13% -> 6%
where the time goes in v3:
time: 811 us; the launch traced here: 805 us
  waiting for transfers between devices  413 us (51%)
  Pallas kernels  115 us (14%)
  matrix products  77.4 us (10%)
  local copies, waits for them, and re-layouts  59.8 us (7%)
  blocking collectives  42.5 us (5%)
  other arithmetic  41.6 us (5%)
  starting transfers between devices  39.2 us (5%)
  between operations  16 us (2%)
    ppermute x28, waiting for transfers between devices, row_scatter_sum(): lax.ppermute(outgoing, 'row', [(i, (i + shift) % count) for i in range(co...  127 us
    reduce_scatter x3, waiting for transfers between devices, feature_sum(): lax.psum_scatter(partial_rows, 'col', scatter_dimension=1, tiled=True)  118 us
    all_gather x4, waiting for transfers between devices, feature_whole(): return lax.all_gather(blocked, 'col', axis=1, tiled=True)  99.9 us
    pallas_call x1, Pallas kernels, attention_backward(): pl.pallas_call(functools.partial(_bwd_kernel, scale), grid=grid, in_specs...  68.6 us
    all_gather x2, waiting for transfers between devices, rows_gathered_many(): pieces = lax.all_gather(flat, 'row', axis=0, tiled=False)  67.8 us
    pallas_call x1, Pallas kernels, attention_forward(): pl.pallas_call(functools.partial(_fwd_kernel, scale), grid=grid, in_specs...  46.9 us
    psum x3, blocking collectives, row_totals(): lax.psum((jnp.sum(first_term, axis=1), jnp.sum(second_term, axis=1)), 'col')  30.9 us
    ppermute x28, starting transfers between devices, row_scatter_sum(): lax.ppermute(outgoing, 'row', [(i, (i + shift) % count) for i in range(co...  26.6 us
  transfers between devices with their start and end apart: 45, of which 26 were waited for; matrix products, arithmetic and copies ran while one was open for 10% of the time, Pallas kernels for 6%

profile of v3, /device:TPU:12, one launch (start us, length us, event | category | flops | bytes accessed | tf_op | source)
XLA Modules:
  0.0 805.1 jit_solution(6945590627087439818)
XLA Ops:
  17.5 11.6 %all-reduce.6 = (f32[768]{0:T(1024)S(1)}, f32[768]{0:T(1024)S(1)}, f32[768]{0:T(1024)S(1)}) all-reduce(f32[768]{0:T(1024)S(1)} %dynamic-update-slice, f32[768]{0:T(1024)S(1)} %dynamic-update-slice.2, f32[768]{0:T(1024)S(1)} %dynamic-update-slice.1), channel_id=1, replica_groups=mesh['row'=8,'col'=4] {'col'}, use_global_device_ids=true, to_apply=%add | all-reduce | flops 2304 | bytes 18432
  29.1 22.4 %all-gather.20.cloned.1.call-done = bf16[589824]{0:T(1024)(128)(2,1)} async-done(((bf16[73728]{0:T(1024)(128)(2,1)}), bf16[589824]{0:T(1024)(128)(2,1)}) %all-gather.20.cloned.1.call-update) | async-done | bytes 1179664 | tf_op jit(solution)/shard_map/weights_in/all_gather | solution.py:213
  60.0 45.4 %all-gather.22.cloned.1.call-done = bf16[1179648]{0:T(1024)(128)(2,1)} async-done(((bf16[147456]{0:T(1024)(128)(2,1)}), bf16[1179648]{0:T(1024)(128)(2,1)}) %all-gather.22.cloned.1.call-update) | async-done | bytes 2359312 | tf_op jit(solution)/shard_map/weights_ffn/all_gather | solution.py:213
  109.6 25.4 %all-gather.10.cloned.1.call-done = bf16[2048,768]{0,1:T(8,128)(2,1)} async-done(((bf16[2048,192]{0,1:T(8,128)(2,1)}), bf16[2048,768]{0,1:T(8,128)(2,1)}) %all-gather.10.cloned.1.call-update) | async-done | bytes 3145744 | tf_op jit(solution)/shard_map/all_gather | solution.py:130
  146.5 4.6 fusion.27
  151.1 46.9 %shard_map.305 = (bf16[3,2048,64]{2,1,0:T(8,128)(2,1)S(1)}, f32[3,2048,1]{2,1,0:T(8,128)}, f32[3,2048,1]{2,1,0:T(8,128)}) custom-call(bf16[3,2048,64]{2,1,0:T(8,128)(2,1)S(1)} %get-tuple-element.164.q_ref, bf16[3,2048,64]{2,1,0:T(8,128)(2,1)S(1)} %bitcast.225, bf16[3,2048,64]{2,1,0:T(8,128)(2,1)} %get-tuple-element.165.v_ref, s32[2048,1]{1,0:T(8,128)S(1)} %copy-done.2, ...), custom_call_target="tpu_custom_call" | custom-call | flops 3221225472 | bytes 3145728 | tf_op jit(solution)/shard_map/pallas_call | solution.py:79
  211.5 16.5 %all-gather.12.cloned.1.call-done = bf16[2048,768]{0,1:T(8,128)(2,1)} async-done(((bf16[2048,192]{0,1:T(8,128)(2,1)}), bf16[2048,768]{0,1:T(8,128)(2,1)}) %all-gather.12.cloned.1.call-update) | async-done | bytes 3145744 | tf_op jit(solution)/shard_map/all_gather | solution.py:130
  228.0 6.9 fusion.69
  238.7 18.0 %multiply_convert_fusion = (bf16[2048,768]{1,0:T(8,128)(2,1)S(1)}, f32[2048,768]{1,0:T(8,128)}, f32[2048,768]{1,0:T(8,128)}) fusion(f32[768]{0:T(1024)S(1)} %copy-done.39, bf16[768,768]{1,0:T(8,128)(2,1)S(1)} %copy-done.12, f32[2048,768]{0,1:T(8,128)S(1)} %get-tuple-element.110), kind=kOutput, calls=%fused_computation.4 | convolution fusion | flops 2521300992 | bytes 23202816 | tf_op jit(solution)/shard_map/dot_general | solution.py:303
  263.1 59.0 %reduce-scatter.4.cloned.1.call-done = f32[2048,192]{0,1:T(8,128)} async-done(((f32[2048,768]{0,1:T(8,128)}), f32[2048,192]{0,1:T(8,128)}) %reduce-scatter.4.cloned.1.call-update) | async-done | bytes 1572880 | tf_op jit(solution)/shard_map/reduce_scatter | solution.py:134
  324.3 10.2 %all-reduce.5 = (f32[2048]{0:T(1024)S(1)}, f32[2048]{0:T(1024)S(1)}) all-reduce(f32[2048]{0:T(1024)S(1)} %get-tuple-element.89, f32[2048]{0:T(1024)S(1)} %get-tuple-element.88), channel_id=1, replica_groups=mesh['row'=8,'col'=4] {'col'}, use_global_device_ids=true, to_apply=%region_6.0 | all-reduce | flops 4096 | bytes 32768 | tf_op jit(solution)/shard_map/psum | solution.py:138
  336.7 10.3 %all-reduce.4 = (f32[2048]{0:T(1024)S(1)}, f32[2048]{0:T(1024)S(1)}) all-reduce(f32[2048]{0:T(1024)S(1)} %get-tuple-element.85, f32[2048]{0:T(1024)S(1)} %get-tuple-element.90), channel_id=1, replica_groups=mesh['row'=8,'col'=4] {'col'}, use_global_device_ids=true, to_apply=%region_10.0 | all-reduce | flops 4096 | bytes 32768 | tf_op jit(solution)/shard_map/psum | solution.py:138
  349.6 29.1 %all-gather.16.cloned.1.call-done = bf16[2048,768]{0,1:T(8,128)(2,1)} async-done(((bf16[2048,192]{0,1:T(8,128)(2,1)}), bf16[2048,768]{0,1:T(8,128)(2,1)}) %all-gather.16.cloned.1.call-update) | async-done | bytes 3145744 | tf_op jit(solution)/shard_map/all_gather | solution.py:130
  378.7 10.9 %convert_reduce_fusion = (f32[768]{0:T(1024)S(1)}, bf16[2048,768]{1,0:T(8,128)(2,1)S(1)}) fusion(f32[2048,768]{1,0:T(8,128)} %get-tuple-element.109, f32[2048,768]{1,0:T(8,128)} %get-tuple-element.163, f32[768]{0:T(1024)S(1)} %copy-done.39, bf16[2048,768]{0,1:T(8,128)(2,1)} %all-gather.16.cloned.1.call-done, bf16[768,768]{0,1:T(8,128)(2,1)} %bitcast.246), kind=kOutput, calls=%fused_computation.2 | convolution fusion | flops 2442657024 | bytes 20060160 | tf_op jit(solution)/shard_map/dot_general | solution.py:315
  395.9 58.9 %reduce-scatter.6.cloned.1.call-done = f32[2048,192]{0,1:T(8,128)} async-done(((f32[2048,768]{0,1:T(8,128)}), f32[2048,192]{0,1:T(8,128)}) %reduce-scatter.6.cloned.1.call-update) | async-done | bytes 1572880 | tf_op jit(solution)/shard_map/reduce_scatter | solution.py:134
  454.9 4.6 multiply_reduce_fusion.1
  459.5 10.4 %all-reduce.3 = (f32[2048]{0:T(1024)S(1)}, f32[2048]{0:T(1024)S(1)}) all-reduce(f32[2048]{0:T(1024)S(1)} %get-tuple-element.81, f32[2048]{0:T(1024)S(1)} %get-tuple-element.86), channel_id=1, replica_groups=mesh['row'=8,'col'=4] {'col'}, use_global_device_ids=true, to_apply=%region_15.0 | all-reduce | flops 4096 | bytes 32768 | tf_op jit(solution)/shard_map/psum | solution.py:138
  473.4 28.9 %all-gather.18.cloned.1.call-done = bf16[2048,768]{0,1:T(8,128)(2,1)} async-done(((bf16[2048,192]{0,1:T(8,128)(2,1)}), bf16[2048,768]{0,1:T(8,128)(2,1)}) %all-gather.18.cloned.1.call-update) | async-done | bytes 3145744 | tf_op jit(solution)/shard_map/all_gather | solution.py:130
  509.1 68.6 %shard_map.306 = (bf16[3,2048,64]{2,1,0:T(8,128)(2,1)S(1)}, f32[3,2048,64]{2,1,0:T(8,128)}, f32[3,2048,64]{2,1,0:T(8,128)}) custom-call(bf16[3,2048,64]{2,1,0:T(8,128)(2,1)S(1)} %copy-done.1, bf16[3,2048,64]{2,1,0:T(8,128)(2,1)S(1)} %bitcast.226, bf16[3,2048,64]{2,1,0:T(8,128)(2,1)} %get-tuple-element.165.v_ref, bf16[3,2048,64]{2,1,0:T(8,128)(2,1)} %bitcast.244, ...), custom_call_target="tpu_custom_call" | custom-call | flops 8053063680 | bytes 6291456 | tf_op jit(solution)/shard_map/pallas_call | solution.py:107
  585.6 7.3 convolution_bitcast_fusion
  593.0 5.4 fusion.82
  604.5 4.9 fusion.29
  613.6 24.9 %collective-permute-done.29 = f32[96,768]{1,0:T(8,128)S(1)} collective-permute-done((f32[96,768]{1,0:T(8,128)S(1)}, f32[96,768]{1,0:T(8,128)S(1)}, u32[]{:S(2)}, u32[]{:S(2)}) %collective-permute-start.29) | collective-permute-done | bytes 294944 | tf_op jit(solution)/shard_map/ppermute | solution.py:187
  638.8 6.6 collective-permute-done.30
  645.4 6.4 collective-permute-done.31
  651.9 20.7 %collective-permute-done.33 = f32[96,768]{1,0:T(8,128)S(1)} collective-permute-done((f32[96,768]{1,0:T(8,128)S(1)}, f32[96,768]{1,0:T(8,128)S(1)}, u32[]{:S(2)}, u32[]{:S(2)}) %collective-permute-start.33) | collective-permute-done | bytes 294944 | tf_op jit(solution)/shard_map/ppermute | solution.py:187
  679.9 16.3 %collective-permute-done.23 = f32[96,768]{1,0:T(8,128)} collective-permute-done((f32[96,768]{1,0:T(8,128)}, f32[96,768]{1,0:T(8,128)}, u32[]{:S(2)}, u32[]{:S(2)}) %collective-permute-start.23) | collective-permute-done | bytes 294944 | tf_op jit(solution)/shard_map/ppermute | solution.py:187
  696.1 5.6 collective-permute-done.24
  714.3 5.4 fusion.33
  726.1 4.7 collective-permute-start.9
  752.9 9.1 %collective-permute-done.19 = f32[96,192]{1,0:T(8,128)S(1)} collective-permute-done((f32[96,192]{1,0:T(8,128)S(1)}, f32[96,192]{1,0:T(8,128)S(1)}, u32[]{:S(2)}, u32[]{:S(2)}) %collective-permute-start.19) | collective-permute-done | bytes 73760 | tf_op jit(solution)/shard_map/ppermute | solution.py:187
  765.3 15.2 %collective-permute-done.1 = f32[96,576]{1,0:T(8,128)S(1)} collective-permute-done((f32[96,576]{1,0:T(8,128)S(1)}, f32[96,576]{1,0:T(8,128)S(1)}, u32[]{:S(2)}, u32[]{:S(2)}) %collective-permute-start.1) | collective-permute-done | bytes 221216 | tf_op jit(solution)/shard_map/ppermute | solution.py:187
  (252 shorter events, 168.0 us)
Async XLA Ops:
  7.3 44.2 %all-gather.20.cloned.1.call-start = ((), (), s32[]{:S(2)}) async-start(), calls=%async_computation.11 | async-start | bytes 1327104 | tf_op jit(solution)/shard_map/weights_in/all_gather | solution.py:213
  10.0 95.4 %all-gather.22.cloned.1.call-start = ((), (), s32[]{:S(2)}) async-start(), calls=%async_computation.12 | async-start | bytes 2654208 | tf_op jit(solution)/shard_map/weights_ffn/all_gather | solution.py:213
  13.3 121.8 %all-gather.10.cloned.1.call-start = ((), (), s32[]{:S(2)}) async-start(), calls=%async_computation.3 | async-start | bytes 3932160 | tf_op jit(solution)/shard_map/all_gather | solution.py:130
  14.0 197.5 %all-gather.14.cloned.1.call-start = ((), (), s32[]{:S(2)}) async-start(), calls=%async_computation.5 | async-start | bytes 1474560 | tf_op jit(solution)/shard_map/weights_out/all_gather | solution.py:275
  59.7 168.3 %all-gather.12.cloned.1.call-start = ((), (), s32[]{:S(2)}) async-start(), calls=%async_computation.4 | async-start | bytes 3932160 | tf_op jit(solution)/shard_map/all_gather | solution.py:130
  199.4 122.7 %reduce-scatter.4.cloned.1.call-start = ((), (), s32[]{:S(2)}) async-start(), calls=%async_computation.6 | async-start | bytes 7864320 | tf_op jit(solution)/shard_map/reduce_scatter | solution.py:134
  263.0 115.7 %all-gather.16.cloned.1.call-start = ((), (), s32[]{:S(2)}) async-start(), calls=%async_computation.7 | async-start | bytes 3932160 | tf_op jit(solution)/shard_map/all_gather | solution.py:130
  349.6 105.3 %reduce-scatter.6.cloned.1.call-start = ((), (), s32[]{:S(2)}) async-start(), calls=%async_computation.8 | async-start | bytes 7864320 | tf_op jit(solution)/shard_map/reduce_scatter | solution.py:134
  395.9 106.4 %all-gather.18.cloned.1.call-start = ((), (), s32[]{:S(2)}) async-start(), calls=%async_computation.9 | async-start | bytes 3932160 | tf_op jit(solution)/shard_map/all_gather | solution.py:130
  473.1 321.3 %reduce-scatter.8.cloned.1.call-start = ((), (), s32[]{:S(2)}) async-start(), calls=%async_computation.10 | async-start | bytes 7864320 | tf_op jit(solution)/shard_map/reduce_scatter | solution.py:134
  600.1 38.4 %collective-permute-start.29 = (f32[96,768]{1,0:T(8,128)S(1)}, f32[96,768]{1,0:T(8,128)S(1)}, u32[]{:S(2)}, u32[]{:S(2)}) collective-permute-start(f32[96,768]{1,0:T(8,128)S(1)} %get-tuple-element.122), channel_id=1, source_target_pairs={{0,8},{4,12},{8,16},{12,20},{16,24},{20,28},{24,0},{28,4},{1,9},{5... | collective-permute-start | bytes 884744 | tf_op jit(solution)/shard_map/ppermute | solution.py:187
  601.6 43.8 %collective-permute-start.30 = (f32[96,768]{1,0:T(8,128)S(1)}, f32[96,768]{1,0:T(8,128)S(1)}, u32[]{:S(2)}, u32[]{:S(2)}) collective-permute-start(f32[96,768]{1,0:T(8,128)S(1)} %get-tuple-element.121), channel_id=1, source_target_pairs={{0,12},{4,16},{8,20},{12,24},{16,28},{20,0},{24,4},{28,8},{1,13},{... | collective-permute-start | bytes 884744 | tf_op jit(solution)/shard_map/ppermute | solution.py:187
  603.0 48.8 %collective-permute-start.31 = (f32[96,768]{1,0:T(8,128)S(1)}, f32[96,768]{1,0:T(8,128)S(1)}, u32[]{:S(2)}, u32[]{:S(2)}) collective-permute-start(f32[96,768]{1,0:T(8,128)S(1)} %get-tuple-element.120), channel_id=1, source_target_pairs={{0,16},{4,20},{8,24},{12,28},{16,0},{20,4},{24,8},{28,12},{1,17},{... | collective-permute-start | bytes 884744 | tf_op jit(solution)/shard_map/ppermute | solution.py:187
  609.5 42.3 %collective-permute-start.32 = (f32[96,768]{1,0:T(8,128)S(1)}, f32[96,768]{1,0:T(8,128)S(1)}, u32[]{:S(2)}, u32[]{:S(2)}) collective-permute-start(f32[96,768]{1,0:T(8,128)S(1)} %get-tuple-element.119), channel_id=1, source_target_pairs={{0,20},{4,24},{8,28},{12,0},{16,4},{20,8},{24,12},{28,16},{1,21},{... | collective-permute-start | bytes 884744 | tf_op jit(solution)/shard_map/ppermute | solution.py:187
  612.0 60.5 %collective-permute-start.33 = (f32[96,768]{1,0:T(8,128)S(1)}, f32[96,768]{1,0:T(8,128)S(1)}, u32[]{:S(2)}, u32[]{:S(2)}) collective-permute-start(f32[96,768]{1,0:T(8,128)S(1)} %get-tuple-element.118), channel_id=1, source_target_pairs={{0,24},{4,28},{8,0},{12,4},{16,8},{20,12},{24,16},{28,20},{1,25},{... | collective-permute-start | bytes 884744 | tf_op jit(solution)/shard_map/ppermute | solution.py:187
  638.5 34.6 %collective-permute-start.34 = (f32[96,768]{1,0:T(8,128)S(1)}, f32[96,768]{1,0:T(8,128)S(1)}, u32[]{:S(2)}, u32[]{:S(2)}) collective-permute-start(f32[96,768]{1,0:T(8,128)S(1)} %get-tuple-element.117), channel_id=1, source_target_pairs={{0,28},{4,0},{8,4},{12,8},{16,12},{20,16},{24,20},{28,24},{1,29},{... | collective-permute-start | bytes 884744 | tf_op jit(solution)/shard_map/ppermute | solution.py:187
  645.4 27.8 %collective-permute-start.21 = (f32[96,768]{1,0:T(8,128)S(1)}, f32[96,768]{1,0:T(8,128)S(1)}, u32[]{:S(2)}, u32[]{:S(2)}) collective-permute-start(f32[96,768]{1,0:T(8,128)S(1)} %get-tuple-element.123), channel_id=1, source_target_pairs={{0,4},{4,8},{8,12},{12,16},{16,20},{20,24},{24,28},{28,0},{1,5},{5... | collective-permute-start | bytes 884744 | tf_op jit(solution)/shard_map/ppermute | solution.py:187
  651.8 21.8 %collective-permute-start.22 = (f32[96,768]{1,0:T(8,128)S(1)}, f32[96,768]{1,0:T(8,128)S(1)}, u32[]{:S(2)}, u32[]{:S(2)}) collective-permute-start(f32[96,768]{1,0:T(8,128)S(1)} %get-tuple-element.129), channel_id=1, source_target_pairs={{0,8},{4,12},{8,16},{12,20},{16,24},{20,28},{24,0},{28,4},{1,9},{5... | collective-permute-start | bytes 884744 | tf_op jit(solution)/shard_map/ppermute | solution.py:187
  651.8 44.3 %collective-permute-start.23 = (f32[96,768]{1,0:T(8,128)}, f32[96,768]{1,0:T(8,128)}, u32[]{:S(2)}, u32[]{:S(2)}) collective-permute-start(f32[96,768]{1,0:T(8,128)} %get-tuple-element.128), channel_id=1, source_target_pairs={{0,12},{4,16},{8,20},{12,24},{16,28},{20,0},{24,4},{28,8},{1,13},{... | collective-permute-start | bytes 884744 | tf_op jit(solution)/shard_map/ppermute | solution.py:187
  672.5 29.2 %collective-permute-start.24 = (f32[96,768]{1,0:T(8,128)}, f32[96,768]{1,0:T(8,128)}, u32[]{:S(2)}, u32[]{:S(2)}) collective-permute-start(f32[96,768]{1,0:T(8,128)} %get-tuple-element.127), channel_id=1, source_target_pairs={{0,16},{4,20},{8,24},{12,28},{16,0},{20,4},{24,8},{28,12},{1,17},{... | collective-permute-start | bytes 884744 | tf_op jit(solution)/shard_map/ppermute | solution.py:187
  673.2 28.6 %collective-permute-start.25 = (f32[96,768]{1,0:T(8,128)}, f32[96,768]{1,0:T(8,128)}, u32[]{:S(2)}, u32[]{:S(2)}) collective-permute-start(f32[96,768]{1,0:T(8,128)} %get-tuple-element.126), channel_id=1, source_target_pairs={{0,20},{4,24},{8,28},{12,0},{16,4},{20,8},{24,12},{28,16},{1,21},{... | collective-permute-start | bytes 884744 | tf_op jit(solution)/shard_map/ppermute | solution.py:187
  673.2 31.0 %collective-permute-start.26 = (f32[96,768]{1,0:T(8,128)}, f32[96,768]{1,0:T(8,128)}, u32[]{:S(2)}, u32[]{:S(2)}) collective-permute-start(f32[96,768]{1,0:T(8,128)} %get-tuple-element.125), channel_id=1, source_target_pairs={{0,24},{4,28},{8,0},{12,4},{16,8},{20,12},{24,16},{28,20},{1,25},{... | collective-permute-start | bytes 884744 | tf_op jit(solution)/shard_map/ppermute | solution.py:187
  673.6 31.2 %collective-permute-start.27 = (f32[96,768]{1,0:T(8,128)S(1)}, f32[96,768]{1,0:T(8,128)}, u32[]{:S(2)}, u32[]{:S(2)}) collective-permute-start(f32[96,768]{1,0:T(8,128)S(1)} %get-tuple-element.124), channel_id=1, source_target_pairs={{0,28},{4,0},{8,4},{12,8},{16,12},{20,16},{24,20},{28,24},{1,29},{... | collective-permute-start | bytes 884744 | tf_op jit(solution)/shard_map/ppermute | solution.py:187
  709.9 21.0 %collective-permute-start.12 = (f32[2304]{0:T(1024)}, f32[2304]{0:T(1024)}, u32[]{:S(2)}, u32[]{:S(2)}) collective-permute-start(f32[2304]{0:T(1024)} %concatenate.15), channel_id=1, source_target_pairs={{0,24},{4,28},{8,0},{12,4},{16,8},{20,12},{24,16},{28,20},{1,25},{... | collective-permute-start | bytes 27656 | tf_op jit(solution)/shard_map/ppermute | solution.py:197
  710.9 20.1 %collective-permute-start.13 = (f32[2304]{0:T(1024)}, f32[2304]{0:T(1024)}, u32[]{:S(2)}, u32[]{:S(2)}) collective-permute-start(f32[2304]{0:T(1024)} %concatenate.15), channel_id=1, source_target_pairs={{0,28},{4,0},{8,4},{12,8},{16,12},{20,16},{24,20},{28,24},{1,29},{... | collective-permute-start | bytes 27656 | tf_op jit(solution)/shard_map/ppermute | solution.py:197
  738.6 23.5 %collective-permute-start.19 = (f32[96,192]{1,0:T(8,128)S(1)}, f32[96,192]{1,0:T(8,128)S(1)}, u32[]{:S(2)}, u32[]{:S(2)}) collective-permute-start(f32[96,192]{1,0:T(8,128)S(1)} %get-tuple-element.142), channel_id=1, source_target_pairs={{0,24},{4,28},{8,0},{12,4},{16,8},{20,12},{24,16},{28,20},{1,25},{... | collective-permute-start | bytes 221192 | tf_op jit(solution)/shard_map/ppermute | solution.py:187
  743.5 20.3 %collective-permute-start.20 = (f32[96,192]{1,0:T(8,128)S(1)}, f32[96,192]{1,0:T(8,128)S(1)}, u32[]{:S(2)}, u32[]{:S(2)}) collective-permute-start(f32[96,192]{1,0:T(8,128)S(1)} %get-tuple-element.141), channel_id=1, source_target_pairs={{0,28},{4,0},{8,4},{12,8},{16,12},{20,16},{24,20},{28,24},{1,29},{... | collective-permute-start | bytes 221192 | tf_op jit(solution)/shard_map/ppermute | solution.py:187
  749.4 31.1 %collective-permute-start.1 = (f32[96,576]{1,0:T(8,128)S(1)}, f32[96,576]{1,0:T(8,128)S(1)}, u32[]{:S(2)}, u32[]{:S(2)}) collective-permute-start(f32[96,576]{1,0:T(8,128)S(1)} %get-tuple-element.138), channel_id=1, source_target_pairs={{0,8},{4,12},{8,16},{12,20},{16,24},{20,28},{24,0},{28,4},{1,9},{5... | collective-permute-start | bytes 663560 | tf_op jit(solution)/shard_map/ppermute | solution.py:187
  752.9 32.9 %collective-permute-start.2 = (f32[96,576]{1,0:T(8,128)}, f32[96,576]{1,0:T(8,128)}, u32[]{:S(2)}, u32[]{:S(2)}) collective-permute-start(f32[96,576]{1,0:T(8,128)} %get-tuple-element.137), channel_id=1, source_target_pairs={{0,12},{4,16},{8,20},{12,24},{16,28},{20,0},{24,4},{28,8},{1,13},{... | collective-permute-start | bytes 663560 | tf_op jit(solution)/shard_map/ppermute | solution.py:187
  762.1 26.7 %collective-permute-start.3 = (f32[96,576]{1,0:T(8,128)}, f32[96,576]{1,0:T(8,128)}, u32[]{:S(2)}, u32[]{:S(2)}) collective-permute-start(f32[96,576]{1,0:T(8,128)} %get-tuple-element.136), channel_id=1, source_target_pairs={{0,16},{4,20},{8,24},{12,28},{16,0},{20,4},{24,8},{28,12},{1,17},{... | collective-permute-start | bytes 663560 | tf_op jit(solution)/shard_map/ppermute | solution.py:187
  763.8 25.0 %collective-permute-start.4 = (f32[96,576]{1,0:T(8,128)}, f32[96,576]{1,0:T(8,128)}, u32[]{:S(2)}, u32[]{:S(2)}) collective-permute-start(f32[96,576]{1,0:T(8,128)} %get-tuple-element.135), channel_id=1, source_target_pairs={{0,20},{4,24},{8,28},{12,0},{16,4},{20,8},{24,12},{28,16},{1,21},{... | collective-permute-start | bytes 663560 | tf_op jit(solution)/shard_map/ppermute | solution.py:187
  763.8 27.2 %collective-permute-start.5 = (f32[96,576]{1,0:T(8,128)}, f32[96,576]{1,0:T(8,128)}, u32[]{:S(2)}, u32[]{:S(2)}) collective-permute-start(f32[96,576]{1,0:T(8,128)} %get-tuple-element.134), channel_id=1, source_target_pairs={{0,24},{4,28},{8,0},{12,4},{16,8},{20,12},{24,16},{28,20},{1,25},{... | collective-permute-start | bytes 663560 | tf_op jit(solution)/shard_map/ppermute | solution.py:187
  (57 other events, 1148.1 us)
Sparse Core Ops, SparseCore 0:
  10.8 40.5 all-gather.19
  54.2 51.1 all-gather.21
  107.0 27.9 all-gather.9
  137.0 17.4 all-gather.13
  199.5 28.4 all-gather.11
  263.1 58.8 reduce-scatter.3
  349.7 28.9 all-gather.15
  396.0 58.8 reduce-scatter.5
  473.3 28.9 all-gather.17
  593.1 58.8 reduce-scatter.7

commit v4 on v3

--- a/solution.py
+++ b/solution.py
@@ -177,10 +177,9 @@
     return lax.dot_general(grad_full, complete, contract, preferred_element_type=jnp.float32)
 
 
-def row_scatter_sum(partial_rows):
+def row_scatter_sum(blocks):
     count = lax.axis_size("row")
     me = lax.axis_index("row")
-    blocks = partial_rows.reshape((count, partial_rows.shape[0] // count) + partial_rows.shape[1:])
     total = blocks[me]
     for shift in range(1, count):
         outgoing = blocks[lax.rem(me + shift, count)]
@@ -200,6 +199,25 @@
     return total
 
 
+def row_gather(values, axis="row"):
+    count = lax.axis_size(axis)
+    me = lax.axis_index(axis)
+    arrived = [values]
+    for shift in range(1, count):
+        arrived.append(
+            lax.ppermute(values, axis, [(i, (i + shift) % count) for i in range(count)])
+        )
+    stacked = jnp.stack(arrived)
+    order = lax.rem(me - jnp.arange(count) + count, count)
+    return stacked[order]
+
+
+def weight_partial(gathered, local_grad):
+    return lax.dot_general(
+        gathered, local_grad, (((0,), (0,)), ((), ())), preferred_element_type=jnp.float32
+    )
+
+
 def weight_grad(gathered, local_grad):
     return row_scatter_sum(
         lax.dot_general(
@@ -210,7 +228,7 @@
 
 def rows_gathered_many(blocks_and_axes):
     flat = jnp.concatenate([block.reshape(-1) for block, _ in blocks_and_axes])
-    pieces = lax.all_gather(flat, "row", axis=0, tiled=False)
+    pieces = row_gather(flat)
     wholes = []
     offset = 0
     for block, axis in blocks_and_axes:
@@ -270,11 +288,11 @@
     inputs_full = feature_whole(token_rows)
     qkv_stack = jnp.stack([query_weight, key_weight, value_weight])
     with jax.named_scope("weights_in"):
-        qkv_complete, output_rows = rows_gathered_many(((qkv_stack, 1), (output_weight, 1)))
+        qkv_complete, output_rows, up_complete, down_complete = rows_gathered_many(
+            ((qkv_stack, 1), (output_weight, 1), (up_weight, 0), (down_weight, 1))
+        )
     with jax.named_scope("weights_out"):
         output_complete = lax.all_gather(output_rows, "col", axis=0, tiled=True)
-    with jax.named_scope("weights_ffn"):
-        up_complete, down_complete = rows_gathered_many(((up_weight, 0), (down_weight, 1)))
     projected = jnp.einsum(
         "td,kdc->ktc", inputs_full, qkv_complete, preferred_element_type=jnp.float32
     )
@@ -286,9 +304,10 @@
     )
     attended = heads_beside(attended_h)
     attended_full = feature_whole(attended)
-    output_bias_full = lax.all_gather(output_bias, "col", axis=0, tiled=True)
-    gain_one_full = lax.all_gather(attn_gain, "col", axis=0, tiled=True)
-    shift_one_full = lax.all_gather(attn_shift, "col", axis=0, tiled=True)
+    vectors_full = row_gather(jnp.stack([output_bias, attn_gain, attn_shift]), "col")
+    output_bias_full, gain_one_full, shift_one_full = (
+        vectors_full[:, which].reshape(-1) for which in range(3)
+    )
     first_sum_full = (
         inputs_full.astype(jnp.float32)
         + jnp.dot(attended_full, output_complete, preferred_element_type=jnp.float32)
@@ -311,12 +330,12 @@
     )
     branch_grad = second_grad.astype(jnp.bfloat16)
     branch_full = feature_whole(branch_grad)
-    down_weight_grad = weight_grad(branch_full, acted).T
+    down_partial = weight_partial(branch_full, acted)
     acted_grad = lax.dot_general(
         branch_full, down_complete, (((1,), (1,)), ((), ())), preferred_element_type=jnp.float32
     )
     upped_grad = gelu_pull(acted_grad)[0].astype(jnp.bfloat16)
-    up_weight_grad = weight_grad(hidden_full, upped_grad)
+    up_partial = weight_partial(hidden_full, upped_grad)
     hidden_grad = second_grad + feature_sum(
         lax.dot_general(
             upped_grad, up_complete, (((1,), (1,)), ((), ())), preferred_element_type=jnp.float32
@@ -327,7 +346,7 @@
     )
     attn_branch_grad = first_grad.astype(jnp.bfloat16)
     attn_branch_full = feature_whole(attn_branch_grad)
-    output_weight_grad = weight_grad(attn_branch_full, attended).T
+    output_partial = weight_partial(attn_branch_full, attended)
     attended_grad = lax.dot_general(
         attn_branch_full, output_rows, (((1,), (1,)), ((), ())), preferred_element_type=jnp.float32
     ).astype(jnp.bfloat16)
@@ -345,7 +364,7 @@
     key_grad = heads_beside(key_grad_h).astype(jnp.bfloat16)
     value_grad = heads_beside(value_grad_h).astype(jnp.bfloat16)
     column_count = query_weight.shape[1]
-    qkv_grads = weight_grad(
+    qkv_partial = weight_partial(
         inputs_full, jnp.concatenate([query_grad, key_grad, value_grad], axis=1)
     )
     input_grad = first_grad + feature_sum(
@@ -367,7 +386,28 @@
         final_gain_grad,
         final_shift_grad,
     )
-    param_flat = row_sum(jnp.concatenate(param_parts))
+    param_flat = jnp.concatenate(param_parts)
+    row_count = lax.axis_size("row")
+    partials = (down_partial, up_partial, output_partial, qkv_partial)
+    joined = jnp.concatenate(partials, axis=1)
+    joined = joined.reshape(row_count, joined.shape[0] // row_count, joined.shape[1])
+    extra = jnp.broadcast_to(param_flat, (row_count, 1, param_flat.shape[0]))
+    if param_flat.shape[0] == joined.shape[2]:
+        summed = row_scatter_sum(jnp.concatenate([joined, extra], axis=1))
+        param_flat = summed[-1]
+        summed = summed[:-1]
+    else:
+        summed = row_scatter_sum(joined)
+        param_flat = row_sum(param_flat)
+    grads_own = []
+    offset = 0
+    for part in partials:
+        grads_own.append(summed[:, offset : offset + part.shape[1]])
+        offset += part.shape[1]
+    down_weight_grad = grads_own[0].T
+    up_weight_grad = grads_own[1]
+    output_weight_grad = grads_own[2].T
+    qkv_grads = grads_own[3]
     param_totals = []
     offset = 0
     for part in param_parts:

time: 811 us -> 840 us (1.036)
  local copies, waits for them, and re-layouts: 59.8 us -> 102 us
  starting transfers between devices: 39.2 us -> 20.1 us
    all_gather x2 -> x0, waiting for transfers between devices: 67.8 us -> none  [rows_gathered_many(): pieces = lax.all_gather(flat, 'row', axis=0, tiled=False)]
    ppermute x7 -> x10, waiting for transfers between devices: 0.02 us -> 56.5 us  [row_gather(): lax.ppermute(values, axis, [(i, (i + shift) % count) for i in range(count)])]
    ppermute x28 -> x7, waiting for transfers between devices: 127 us -> 160 us  [row_scatter_sum(): lax.ppermute(outgoing, 'row', [(i, (i + shift) % count) for i in range(co...]
    another operation x0 -> x9, local copies, waits for them, and re-layouts: none -> 30.7 us  [row_gather(): stacked = jnp.stack(arrived)]
    all_gather x4, waiting for transfers between devices: 99.9 us -> 77.4 us  [feature_whole(): return lax.all_gather(blocked, 'col', axis=1, tiled=True)]
    ppermute x28 -> x7, starting transfers between devices: 26.6 us -> 7.86 us  [row_scatter_sum(): lax.ppermute(outgoing, 'row', [(i, (i + shift) % count) for i in range(co...]
    unnamed x1 -> x0, blocking collectives: 11.6 us -> none
    psum x3, blocking collectives: 30.9 us -> 41 us  [row_totals(): lax.psum((jnp.sum(first_term, axis=1), jnp.sum(second_term, axis=1)), 'col')]
  transfers between devices with their start and end apart: 45 -> 25, of which waited for: 26 -> 14; matrix products, arithmetic and copies ran while one was open for 10% -> 15% of each run, Pallas kernels for 6% -> 6%
where the time goes in v4:
time: 840 us; the launch traced here: 829 us
  waiting for transfers between devices  412 us (49%)
  Pallas kernels  116 us (14%)
  local copies, waits for them, and re-layouts  102 us (12%)
  matrix products  74 us (9%)
  other arithmetic  49.4 us (6%)
  blocking collectives  41 us (5%)
  starting transfers between devices  20.1 us (2%)
  between operations  15.1 us (2%)
    ppermute x7, waiting for transfers between devices, row_scatter_sum(): lax.ppermute(outgoing, 'row', [(i, (i + shift) % count) for i in range(co...  160 us
    reduce_scatter x3, waiting for transfers between devices, feature_sum(): lax.psum_scatter(partial_rows, 'col', scatter_dimension=1, tiled=True)  118 us
    all_gather x4, waiting for transfers between devices, feature_whole(): return lax.all_gather(blocked, 'col', axis=1, tiled=True)  77.4 us
    pallas_call x1, Pallas kernels, attention_backward(): pl.pallas_call(functools.partial(_bwd_kernel, scale), grid=grid, in_specs...  68.7 us
    ppermute x10, waiting for transfers between devices, row_gather(): lax.ppermute(values, axis, [(i, (i + shift) % count) for i in range(count)])  56.5 us
    pallas_call x1, Pallas kernels, attention_forward(): pl.pallas_call(functools.partial(_fwd_kernel, scale), grid=grid, in_specs...  46.9 us
    psum x3, blocking collectives, row_totals(): lax.psum((jnp.sum(first_term, axis=1), jnp.sum(second_term, axis=1)), 'col')  41 us
    another operation x9, local copies, waits for them, and re-layouts, row_gather(): stacked = jnp.stack(arrived)  30.7 us
  transfers between devices with their start and end apart: 25, of which 14 were waited for; matrix products, arithmetic and copies ran while one was open for 15% of the time, Pallas kernels for 6%

profile of v4, /device:TPU:12, one launch (start us, length us, event | category | flops | bytes accessed | tf_op | source)
XLA Modules:
  0.0 828.8 jit_solution(16597157123236236170)
XLA Ops:
  31.5 42.6 %collective-permute-done.1 = bf16[221184]{0:T(1024)(128)(2,1)S(1)} collective-permute-done((bf16[221184]{0:T(1024)(128)(2,1)}, bf16[221184]{0:T(1024)(128)(2,1)S(1)}, u32[]{:S(2)}, u32[]{:S(2)}) %collective-permute-start.1) | collective-permute-done | bytes 442400 | tf_op jit(solution)/shard_map/weights_in/ppermute | solution.py:208
  76.6 7.0 collective-permute-done.2
  85.0 6.9 collective-permute-done.3
  100.7 18.0 %stack.83 = bf16[8,221184]{1,0:T(8,128)(2,1)} concatenate(bf16[1,221184]{1,0:T(2,128)(2,1)S(1)} %stack.75, bf16[1,221184]{1,0:T(2,128)(2,1)S(1)} %stack.76, bf16[1,221184]{1,0:T(2,128)(2,1)S(1)} %stack.77, bf16[1,221184]{1,0:T(2,128)(2,1)S(1)} %stack.78, bf16[1,221184]{1,0:T(2,128)(2,1)} %stack.79, bf16[1,221184]{1,0:T(2,128)(2,1)} %stack.80, bf16[1,221184]{1,0:T(2,128)(2,1)} %stack.81, ...), dimensions={0} | concatenate | bytes 7077888 | tf_op jit(solution)/shard_map/weights_in/stack | solution.py:210
  138.7 3.9 convolution_bitcast_fusion.1
  149.2 4.6 fusion.27
  153.8 46.9 %shard_map.305 = (bf16[3,2048,64]{2,1,0:T(8,128)(2,1)S(1)}, f32[3,2048,1]{2,1,0:T(8,128)}, f32[3,2048,1]{2,1,0:T(8,128)}) custom-call(bf16[3,2048,64]{2,1,0:T(8,128)(2,1)S(1)} %get-tuple-element.132.q_ref, bf16[3,2048,64]{2,1,0:T(8,128)(2,1)S(1)} %bitcast.153, bf16[3,2048,64]{2,1,0:T(8,128)(2,1)} %get-tuple-element.133.v_ref, s32[2048,1]{1,0:T(8,128)S(1)} %copy-done.2, ...), custom_call_target="tpu_custom_call" | custom-call | flops 3221225472 | bytes 3145728 | tf_op jit(solution)/shard_map/pallas_call | solution.py:79
  213.7 19.2 %all-gather.8.cloned.1.call-done = bf16[2048,768]{0,1:T(8,128)(2,1)} async-done(((bf16[2048,192]{0,1:T(8,128)(2,1)}), bf16[2048,768]{0,1:T(8,128)(2,1)}) %all-gather.8.cloned.1.call-update) | async-done | bytes 3145744 | tf_op jit(solution)/shard_map/all_gather | solution.py:130
  232.9 6.9 fusion.71
  239.9 3.6 multiply_add_fusion
  243.5 17.9 %multiply_convert_fusion = (bf16[2048,768]{1,0:T(8,128)(2,1)S(1)}, f32[2048,768]{1,0:T(8,128)}, f32[2048,768]{1,0:T(8,128)}) fusion(f32[768]{0:T(1024)S(1)} %copy-done.28, bf16[768,768]{1,0:T(8,128)(2,1)S(1)} %copy-done.12, f32[2048,768]{0,1:T(8,128)S(1)} %get-tuple-element.93), kind=kOutput, calls=%fused_computation.24 | convolution fusion | flops 2521300992 | bytes 23202816 | tf_op jit(solution)/shard_map/dot_general | solution.py:322
  263.1 4.4 fusion.81
  267.6 58.9 %reduce-scatter.4.cloned.1.call-done = f32[2048,192]{0,1:T(8,128)} async-done(((f32[2048,768]{0,1:T(8,128)}), f32[2048,192]{0,1:T(8,128)}) %reduce-scatter.4.cloned.1.call-update) | async-done | bytes 1572880 | tf_op jit(solution)/shard_map/reduce_scatter | solution.py:134
  328.8 10.3 %all-reduce.2 = (f32[2048]{0:T(1024)S(1)}, f32[2048]{0:T(1024)S(1)}) all-reduce(f32[2048]{0:T(1024)S(1)} %get-tuple-element.72, f32[2048]{0:T(1024)S(1)} %get-tuple-element.71), channel_id=1, replica_groups=mesh['row'=8,'col'=4] {'col'}, use_global_device_ids=true, to_apply=%region_6.0 | all-reduce | flops 4096 | bytes 32768 | tf_op jit(solution)/shard_map/psum | solution.py:138
  341.2 20.4 %all-reduce.1 = (f32[2048]{0:T(1024)S(1)}, f32[2048]{0:T(1024)S(1)}) all-reduce(f32[2048]{0:T(1024)S(1)} %get-tuple-element.68, f32[2048]{0:T(1024)S(1)} %get-tuple-element.73), channel_id=1, replica_groups=mesh['row'=8,'col'=4] {'col'}, use_global_device_ids=true, to_apply=%region_10.0 | all-reduce | flops 4096 | bytes 32768 | tf_op jit(solution)/shard_map/psum | solution.py:138
  364.2 29.1 %all-gather.12.cloned.1.call-done = bf16[2048,768]{0,1:T(8,128)(2,1)} async-done(((bf16[2048,192]{0,1:T(8,128)(2,1)}), bf16[2048,768]{0,1:T(8,128)(2,1)}) %all-gather.12.cloned.1.call-update) | async-done | bytes 3145744 | tf_op jit(solution)/shard_map/all_gather | solution.py:130
  393.3 10.9 %convert_reduce_fusion = (f32[768]{0:T(1024)S(1)}, bf16[2048,768]{1,0:T(8,128)(2,1)S(1)}) fusion(f32[2048,768]{1,0:T(8,128)} %get-tuple-element.92, f32[2048,768]{1,0:T(8,128)} %get-tuple-element.131, f32[768]{0:T(1024)S(1)} %copy-done.28, bf16[2048,768]{0,1:T(8,128)(2,1)} %all-gather.12.cloned.1.call-done, bf16[768,768]{0,1:T(8,128)(2,1)} %bitcast.170), kind=kOutput, calls=%fused_computation.22 | convolution fusion | flops 2442657024 | bytes 20060160 | tf_op jit(solution)/shard_map/dot_general | solution.py:334
  405.8 4.5 fusion.82
  410.3 58.9 %reduce-scatter.6.cloned.1.call-done = f32[2048,192]{0,1:T(8,128)} async-done(((f32[2048,768]{0,1:T(8,128)}), f32[2048,192]{0,1:T(8,128)}) %reduce-scatter.6.cloned.1.call-update) | async-done | bytes 1572880 | tf_op jit(solution)/shard_map/reduce_scatter | solution.py:134
  469.3 4.7 multiply_reduce_fusion.1
  474.0 10.4 %all-reduce = (f32[2048]{0:T(1024)S(1)}, f32[2048]{0:T(1024)S(1)}) all-reduce(f32[2048]{0:T(1024)S(1)} %get-tuple-element.64, f32[2048]{0:T(1024)S(1)} %get-tuple-element.69), channel_id=1, replica_groups=mesh['row'=8,'col'=4] {'col'}, use_global_device_ids=true, to_apply=%region_15.0 | all-reduce | flops 4096 | bytes 32768 | tf_op jit(solution)/shard_map/psum | solution.py:138
  487.6 29.1 %all-gather.14.cloned.1.call-done = bf16[2048,768]{0,1:T(8,128)(2,1)} async-done(((bf16[2048,192]{0,1:T(8,128)(2,1)}), bf16[2048,768]{0,1:T(8,128)(2,1)}) %all-gather.14.cloned.1.call-update) | async-done | bytes 3145744 | tf_op jit(solution)/shard_map/all_gather | solution.py:130
  523.6 68.7 %shard_map.306 = (bf16[3,2048,64]{2,1,0:T(8,128)(2,1)S(1)}, f32[3,2048,64]{2,1,0:T(8,128)}, f32[3,2048,64]{2,1,0:T(8,128)}) custom-call(bf16[3,2048,64]{2,1,0:T(8,128)(2,1)S(1)} %copy-done.1, bf16[3,2048,64]{2,1,0:T(8,128)(2,1)S(1)} %bitcast.154, bf16[3,2048,64]{2,1,0:T(8,128)(2,1)} %get-tuple-element.133.v_ref, bf16[3,2048,64]{2,1,0:T(8,128)(2,1)} %bitcast.168, ...), custom_call_target="tpu_custom_call" | custom-call | flops 8053063680 | bytes 6291456 | tf_op jit(solution)/shard_map/pallas_call | solution.py:107
  600.3 6.9 convolution_bitcast_fusion
  608.6 5.8 fusion.83
  614.4 6.8 fusion.29
  627.9 8.3 %copy.62 = f32[768,2304]{1,0:T(8,128)} copy(f32[768,2304]{0,1:T(8,128)} %pad_maximum_fusion) | data formatting | bytes 14155776 | tf_op jit(solution)/shard_map/concatenate | solution.py:392
  636.9 4.3 fusion.49
  650.7 14.4 %collective-permute-done.10 = f32[97,2304]{1,0:T(8,128)} collective-permute-done((f32[97,2304]{1,0:T(8,128)}, f32[97,2304]{1,0:T(8,128)}, u32[]{:S(2)}, u32[]{:S(2)}) %collective-permute-start.10) | collective-permute-done | bytes 893984 | tf_op jit(solution)/shard_map/ppermute | solution.py:186
  665.6 101.6 %collective-permute-done.11 = f32[97,2304]{1,0:T(8,128)} collective-permute-done((f32[97,2304]{1,0:T(8,128)}, f32[97,2304]{1,0:T(8,128)}, u32[]{:S(2)}, u32[]{:S(2)}) %collective-permute-start.11) | collective-permute-done | bytes 893984 | tf_op jit(solution)/shard_map/ppermute | solution.py:186
  767.2 20.7 %collective-permute-done.12 = f32[97,2304]{1,0:T(8,128)} collective-permute-done((f32[97,2304]{1,0:T(8,128)}, f32[97,2304]{1,0:T(8,128)}, u32[]{:S(2)}, u32[]{:S(2)}) %collective-permute-start.12) | collective-permute-done | bytes 893984 | tf_op jit(solution)/shard_map/ppermute | solution.py:186
  787.9 19.8 %collective-permute-done.13 = f32[97,2304]{1,0:T(8,128)} collective-permute-done((f32[97,2304]{1,0:T(8,128)S(1)}, f32[97,2304]{1,0:T(8,128)}, u32[]{:S(2)}, u32[]{:S(2)}) %collective-permute-start.13) | collective-permute-done | bytes 893984 | tf_op jit(solution)/shard_map/ppermute | solution.py:186
  (199 shorter events, 137.3 us)
Async XLA Ops:
  7.2 131.5 %all-gather.6.cloned.1.call-start = ((), (), s32[]{:S(2)}) async-start(), calls=%async_computation.3 | async-start | bytes 3932160 | tf_op jit(solution)/shard_map/all_gather | solution.py:130
  14.3 15.9 %collective-permute-start = (bf16[221184]{0:T(1024)(128)(2,1)}, bf16[221184]{0:T(1024)(128)(2,1)S(1)}, u32[]{:S(2)}, u32[]{:S(2)}) collective-permute-start(bf16[221184]{0:T(1024)(128)(2,1)} %constant_dynamic-update-slice_fusion), channel_id=1, source_target_pairs={{0,4},{4,8},{8,12},{12,16},{16,20},{20,24},{24,28},{28,0},{1,5},{5... | collective-permute-start | bytes 1327112 | tf_op jit(solution)/shard_map/weights_in/ppermute | solution.py:208
  15.8 58.3 %collective-permute-start.1 = (bf16[221184]{0:T(1024)(128)(2,1)}, bf16[221184]{0:T(1024)(128)(2,1)S(1)}, u32[]{:S(2)}, u32[]{:S(2)}) collective-permute-start(bf16[221184]{0:T(1024)(128)(2,1)} %constant_dynamic-update-slice_fusion), channel_id=1, source_target_pairs={{0,8},{4,12},{8,16},{12,20},{16,24},{20,28},{24,0},{28,4},{1,9},{5... | collective-permute-start | bytes 1327112 | tf_op jit(solution)/shard_map/weights_in/ppermute | solution.py:208
  18.1 7.9 collective-permute-start.7
  18.2 9.0 %collective-permute-start.8 = (f32[3,192]{1,0:T(4,128)S(1)}, f32[3,192]{1,0:T(4,128)S(1)}, u32[]{:S(2)}, u32[]{:S(2)}) collective-permute-start(f32[3,192]{1,0:T(4,128)S(1)} %get-tuple-element.129), channel_id=1, source_target_pairs={{0,2},{1,3},{2,0},{3,1},{4,6},{5,7},{6,4},{7,5},{8,10},{9,11},{10,... | collective-permute-start | bytes 6920 | tf_op jit(solution)/shard_map/ppermute | solution.py:208
  19.8 9.1 %collective-permute-start.9 = (f32[3,192]{1,0:T(4,128)S(1)}, f32[3,192]{1,0:T(4,128)S(1)}, u32[]{:S(2)}, u32[]{:S(2)}) collective-permute-start(f32[3,192]{1,0:T(4,128)S(1)} %get-tuple-element.129), channel_id=1, source_target_pairs={{0,3},{1,0},{2,1},{3,2},{4,7},{5,4},{6,5},{7,6},{8,11},{9,8},{10,9... | collective-permute-start | bytes 6920 | tf_op jit(solution)/shard_map/ppermute | solution.py:208
  21.2 192.5 %all-gather.10.cloned.1.call-start = ((), (), s32[]{:S(2)}) async-start(), calls=%async_computation.5 | async-start | bytes 1474560 | tf_op jit(solution)/shard_map/weights_out/all_gather | solution.py:295
  26.0 57.6 %collective-permute-start.2 = (bf16[221184]{0:T(1024)(128)(2,1)}, bf16[221184]{0:T(1024)(128)(2,1)}, u32[]{:S(2)}, u32[]{:S(2)}) collective-permute-start(bf16[221184]{0:T(1024)(128)(2,1)} %constant_dynamic-update-slice_fusion), channel_id=1, source_target_pairs={{0,12},{4,16},{8,20},{12,24},{16,28},{20,0},{24,4},{28,8},{1,13},{... | collective-permute-start | bytes 1327112 | tf_op jit(solution)/shard_map/weights_in/ppermute | solution.py:208
  27.2 64.8 %collective-permute-start.3 = (bf16[221184]{0:T(1024)(128)(2,1)}, bf16[221184]{0:T(1024)(128)(2,1)}, u32[]{:S(2)}, u32[]{:S(2)}) collective-permute-start(bf16[221184]{0:T(1024)(128)(2,1)} %constant_dynamic-update-slice_fusion), channel_id=1, source_target_pairs={{0,16},{4,20},{8,24},{12,28},{16,0},{20,4},{24,8},{28,12},{1,17},{... | collective-permute-start | bytes 1327112 | tf_op jit(solution)/shard_map/weights_in/ppermute | solution.py:208
  28.9 65.3 %collective-permute-start.4 = (bf16[221184]{0:T(1024)(128)(2,1)}, bf16[221184]{0:T(1024)(128)(2,1)}, u32[]{:S(2)}, u32[]{:S(2)}) collective-permute-start(bf16[221184]{0:T(1024)(128)(2,1)} %constant_dynamic-update-slice_fusion), channel_id=1, source_target_pairs={{0,20},{4,24},{8,28},{12,0},{16,4},{20,8},{24,12},{28,16},{1,21},{... | collective-permute-start | bytes 1327112 | tf_op jit(solution)/shard_map/weights_in/ppermute | solution.py:208
  30.2 66.2 %collective-permute-start.5 = (bf16[221184]{0:T(1024)(128)(2,1)}, bf16[221184]{0:T(1024)(128)(2,1)}, u32[]{:S(2)}, u32[]{:S(2)}) collective-permute-start(bf16[221184]{0:T(1024)(128)(2,1)} %constant_dynamic-update-slice_fusion), channel_id=1, source_target_pairs={{0,24},{4,28},{8,0},{12,4},{16,8},{20,12},{24,16},{28,20},{1,25},{... | collective-permute-start | bytes 1327112 | tf_op jit(solution)/shard_map/weights_in/ppermute | solution.py:208
  74.1 24.4 %collective-permute-start.6 = (bf16[221184]{0:T(1024)(128)(2,1)}, bf16[221184]{0:T(1024)(128)(2,1)}, u32[]{:S(2)}, u32[]{:S(2)}) collective-permute-start(bf16[221184]{0:T(1024)(128)(2,1)} %constant_dynamic-update-slice_fusion), channel_id=1, source_target_pairs={{0,28},{4,0},{8,4},{12,8},{16,12},{20,16},{24,20},{28,24},{1,29},{... | collective-permute-start | bytes 1327112 | tf_op jit(solution)/shard_map/weights_in/ppermute | solution.py:208
  138.4 94.5 %all-gather.8.cloned.1.call-start = ((), (), s32[]{:S(2)}) async-start(), calls=%async_computation.4 | async-start | bytes 3932160 | tf_op jit(solution)/shard_map/all_gather | solution.py:130
  153.8 46.9 %copy-start = (bf16[3,2048,64]{2,1,0:T(8,128)(2,1)}, bf16[3,2048,64]{2,1,0:T(8,128)(2,1)S(1)}, u32[]{:S(2)}) copy-start(bf16[3,2048,64]{2,1,0:T(8,128)(2,1)S(1)} %get-tuple-element.132.q_ref) | copy-start | bytes 2359300
  202.2 124.3 %reduce-scatter.4.cloned.1.call-start = ((), (), s32[]{:S(2)}) async-start(), calls=%async_computation.6 | async-start | bytes 7864320 | tf_op jit(solution)/shard_map/reduce_scatter | solution.py:134
  209.4 23.5 %copy-start.22 = (f32[768]{0:T(1024)S(1)}, f32[768]{0:T(1024)}, u32[]{:S(2)}) copy-start(f32[768]{0:T(1024)} %add.229) | copy-start | bytes 9220
  267.5 59.0 %copy-start.25 = (f32[192]{0:T(256)S(1)}, f32[192]{0:T(256)}, u32[]{:S(2)}) copy-start(f32[192]{0:T(256)} %param.32) | copy-start | bytes 2308
  267.5 71.6 %copy-start.19 = (f32[192]{0:T(256)S(1)}, f32[192]{0:T(256)}, u32[]{:S(2)}) copy-start(f32[192]{0:T(256)} %param.33) | copy-start | bytes 2308
  267.5 125.8 %all-gather.12.cloned.1.call-start = ((), (), s32[]{:S(2)}) async-start(), calls=%async_computation.7 | async-start | bytes 3932160 | tf_op jit(solution)/shard_map/all_gather | solution.py:130
  364.2 105.1 %reduce-scatter.6.cloned.1.call-start = ((), (), s32[]{:S(2)}) async-start(), calls=%async_computation.8 | async-start | bytes 7864320 | tf_op jit(solution)/shard_map/reduce_scatter | solution.py:134
  410.2 59.0 %copy-start.18 = (f32[192]{0:T(256)S(1)}, f32[192]{0:T(256)}, u32[]{:S(2)}) copy-start(f32[192]{0:T(256)} %param.27) | copy-start | bytes 2308
  410.2 59.0 %copy-start.26 = (f32[192]{0:T(256)S(1)}, f32[192]{0:T(256)}, u32[]{:S(2)}) copy-start(f32[192]{0:T(256)} %param.34) | copy-start | bytes 2308
  410.3 106.4 %all-gather.14.cloned.1.call-start = ((), (), s32[]{:S(2)}) async-start(), calls=%async_computation.9 | async-start | bytes 3932160 | tf_op jit(solution)/shard_map/all_gather | solution.py:130
  474.0 42.7 %copy-start.11 = (bf16[192,768]{1,0:T(8,128)(2,1)S(1)}, bf16[192,768]{1,0:T(8,128)(2,1)}, u32[]{:S(2)}) copy-start(bf16[192,768]{1,0:T(8,128)(2,1)} %reshape.253) | copy-start | bytes 884740
  487.6 330.7 %reduce-scatter.8.cloned.1.call-start = ((), (), s32[]{:S(2)}) async-start(), calls=%async_computation.10 | async-start | bytes 7864320 | tf_op jit(solution)/shard_map/reduce_scatter | solution.py:134
  641.2 23.8 %collective-permute-start.10 = (f32[97,2304]{1,0:T(8,128)}, f32[97,2304]{1,0:T(8,128)}, u32[]{:S(2)}, u32[]{:S(2)}) collective-permute-start(f32[97,2304]{1,0:T(8,128)} %get-tuple-element.95), channel_id=1, source_target_pairs={{0,4},{4,8},{8,12},{12,16},{16,20},{20,24},{24,28},{28,0},{1,5},{5... | collective-permute-start | bytes 2681864 | tf_op jit(solution)/shard_map/ppermute | solution.py:186
  642.7 124.5 %collective-permute-start.11 = (f32[97,2304]{1,0:T(8,128)}, f32[97,2304]{1,0:T(8,128)}, u32[]{:S(2)}, u32[]{:S(2)}) collective-permute-start(f32[97,2304]{1,0:T(8,128)} %get-tuple-element.96), channel_id=1, source_target_pairs={{0,8},{4,12},{8,16},{12,20},{16,24},{20,28},{24,0},{28,4},{1,9},{5... | collective-permute-start | bytes 2681864 | tf_op jit(solution)/shard_map/ppermute | solution.py:186
  644.2 143.7 %collective-permute-start.12 = (f32[97,2304]{1,0:T(8,128)}, f32[97,2304]{1,0:T(8,128)}, u32[]{:S(2)}, u32[]{:S(2)}) collective-permute-start(f32[97,2304]{1,0:T(8,128)} %get-tuple-element.97), channel_id=1, source_target_pairs={{0,12},{4,16},{8,20},{12,24},{16,28},{20,0},{24,4},{28,8},{1,13},{... | collective-permute-start | bytes 2681864 | tf_op jit(solution)/shard_map/ppermute | solution.py:186
  645.6 162.1 %collective-permute-start.13 = (f32[97,2304]{1,0:T(8,128)S(1)}, f32[97,2304]{1,0:T(8,128)}, u32[]{:S(2)}, u32[]{:S(2)}) collective-permute-start(f32[97,2304]{1,0:T(8,128)S(1)} %get-tuple-element.98), channel_id=1, source_target_pairs={{0,16},{4,20},{8,24},{12,28},{16,0},{20,4},{24,8},{28,12},{1,17},{... | collective-permute-start | bytes 2681864 | tf_op jit(solution)/shard_map/ppermute | solution.py:186
  647.1 160.6 %collective-permute-start.14 = (f32[97,2304]{1,0:T(8,128)S(1)}, f32[97,2304]{1,0:T(8,128)}, u32[]{:S(2)}, u32[]{:S(2)}) collective-permute-start(f32[97,2304]{1,0:T(8,128)S(1)} %get-tuple-element.99), channel_id=1, source_target_pairs={{0,20},{4,24},{8,28},{12,0},{16,4},{20,8},{24,12},{28,16},{1,21},{... | collective-permute-start | bytes 2681864 | tf_op jit(solution)/shard_map/ppermute | solution.py:186
  665.0 145.2 %collective-permute-start.15 = (f32[97,2304]{1,0:T(8,128)S(1)}, f32[97,2304]{1,0:T(8,128)}, u32[]{:S(2)}, u32[]{:S(2)}) collective-permute-start(f32[97,2304]{1,0:T(8,128)S(1)} %get-tuple-element.100), channel_id=1, source_target_pairs={{0,24},{4,28},{8,0},{12,4},{16,8},{20,12},{24,16},{28,20},{1,25},{... | collective-permute-start | bytes 2681864 | tf_op jit(solution)/shard_map/ppermute | solution.py:186
  767.2 43.8 %collective-permute-start.16 = (f32[97,2304]{1,0:T(8,128)}, f32[97,2304]{1,0:T(8,128)}, u32[]{:S(2)}, u32[]{:S(2)}) collective-permute-start(f32[97,2304]{1,0:T(8,128)} %fusion.58), channel_id=1, source_target_pairs={{0,28},{4,0},{8,4},{12,8},{16,12},{20,16},{24,20},{28,24},{1,29},{... | collective-permute-start | bytes 2681864 | tf_op jit(solution)/shard_map/ppermute | solution.py:186
  (26 other events, 172.6 us)
Sparse Core Ops, SparseCore 0:
  21.3 27.3 all-gather.5
  138.5 19.3 all-gather.9
  202.3 30.5 all-gather.7
  267.7 58.8 reduce-scatter.3
  364.3 28.9 all-gather.11
  410.4 58.8 reduce-scatter.5
  487.7 28.9 all-gather.13
  607.4 58.8 reduce-scatter.7

commit v5 on v3

--- a/solution.py
+++ b/solution.py
@@ -154,29 +154,6 @@
     return (back_rows, jnp.sum(grad_rows * normed, axis=0), jnp.sum(grad_rows, axis=0))
 
 
-def project_in(gathered, stacked):
-    complete = lax.all_gather(stacked, "row", axis=1, tiled=True)
-    return (
-        jnp.einsum("td,kdc->ktc", gathered, complete, preferred_element_type=jnp.float32),
-        complete,
-    )
-
-
-def project_in_back(grad_stack, stacked, complete):
-    complete = lax.all_gather(stacked, "row", axis=1, tiled=True)
-    return jnp.einsum("ktc,kdc->td", grad_stack, complete, preferred_element_type=jnp.float32)
-
-
-def columns_whole(weight_block):
-    return lax.all_gather(weight_block, "row", axis=1, tiled=True)
-
-
-def project_out_back(grad_full, weight_block, complete):
-    contract = (((1,), (1,)), ((), ()))
-    complete = lax.all_gather(weight_block, "row", axis=1, tiled=True)
-    return lax.dot_general(grad_full, complete, contract, preferred_element_type=jnp.float32)
-
-
 def row_scatter_sum(partial_rows):
     count = lax.axis_size("row")
     me = lax.axis_index("row")
@@ -198,6 +175,24 @@
             values, "row", [(i, (i + shift) % count) for i in range(count)]
         )
     return total
+
+
+def axis_gather(values, axis):
+    count = lax.axis_size(axis)
+    me = lax.axis_index(axis)
+    arrived = [values]
+    for shift in range(1, count):
+        arrived.append(
+            lax.ppermute(values, axis, [(i, (i + shift) % count) for i in range(count)])
+        )
+    order = lax.rem(me - jnp.arange(count) + count, count)
+    return jnp.stack(arrived)[order]
+
+
+def weight_partial(gathered, local_grad):
+    return lax.dot_general(
+        gathered, local_grad, (((0,), (0,)), ((), ())), preferred_element_type=jnp.float32
+    )
 
 
 def weight_grad(gathered, local_grad):
@@ -239,7 +234,7 @@
     return (normed * gain_full + shift_full, normed, inverse)
 
 
-def body(
+def layer(
     inputs,
     segments,
     query_weight,
@@ -264,17 +259,13 @@
     labels = segments[0]
     token_rows = inputs.T
     out_grad = cotangent.T.astype(jnp.float32)
-    token_count = token_rows.shape[0]
     own_features = token_rows.shape[1]
     own_start = lax.axis_index("col") * own_features
     inputs_full = feature_whole(token_rows)
     qkv_stack = jnp.stack([query_weight, key_weight, value_weight])
-    with jax.named_scope("weights_in"):
-        qkv_complete, output_rows = rows_gathered_many(((qkv_stack, 1), (output_weight, 1)))
-    with jax.named_scope("weights_out"):
-        output_complete = lax.all_gather(output_rows, "col", axis=0, tiled=True)
-    with jax.named_scope("weights_ffn"):
-        up_complete, down_complete = rows_gathered_many(((up_weight, 0), (down_weight, 1)))
+    qkv_complete, output_rows = rows_gathered_many(((qkv_stack, 1), (output_weight, 1)))
+    output_complete = lax.all_gather(output_rows, "col", axis=0, tiled=True)
+    up_complete, down_complete = rows_gathered_many(((up_weight, 0), (down_weight, 1)))
     projected = jnp.einsum(
         "td,kdc->ktc", inputs_full, qkv_complete, preferred_element_type=jnp.float32
     )
@@ -286,9 +277,10 @@
     )
     attended = heads_beside(attended_h)
     attended_full = feature_whole(attended)
-    output_bias_full = lax.all_gather(output_bias, "col", axis=0, tiled=True)
-    gain_one_full = lax.all_gather(attn_gain, "col", axis=0, tiled=True)
-    shift_one_full = lax.all_gather(attn_shift, "col", axis=0, tiled=True)
+    vectors_full = axis_gather(jnp.stack([output_bias, attn_gain, attn_shift]), "col")
+    output_bias_full, gain_one_full, shift_one_full = (
+        vectors_full[:, which].reshape(-1) for which in range(3)
+    )
     first_sum_full = (
         inputs_full.astype(jnp.float32)
         + jnp.dot(attended_full, output_complete, preferred_element_type=jnp.float32)
@@ -311,12 +303,15 @@
     )
     branch_grad = second_grad.astype(jnp.bfloat16)
     branch_full = feature_whole(branch_grad)
-    down_weight_grad = weight_grad(branch_full, acted).T
+    down_partial = weight_partial(branch_full, acted)
     acted_grad = lax.dot_general(
         branch_full, down_complete, (((1,), (1,)), ((), ())), preferred_element_type=jnp.float32
     )
     upped_grad = gelu_pull(acted_grad)[0].astype(jnp.bfloat16)
-    up_weight_grad = weight_grad(hidden_full, upped_grad)
+    up_partial = weight_partial(hidden_full, upped_grad)
+    ffn_grads = row_scatter_sum(jnp.concatenate([down_partial, up_partial], axis=1))
+    down_weight_grad = ffn_grads[:, : down_partial.shape[1]].T
+    up_weight_grad = ffn_grads[:, down_partial.shape[1] :]
     hidden_grad = second_grad + feature_sum(
         lax.dot_general(
             upped_grad, up_complete, (((1,), (1,)), ((), ())), preferred_element_type=jnp.float32
@@ -416,7 +411,7 @@
         P("col", "row"),
     )
     return jax.shard_map(
-        body,
+        layer,
         mesh=mesh,
         in_specs=placed,
         out_specs=(

time: 811 us -> 841 us (1.037)
  waiting for transfers between devices: 413 us -> 432 us
  local copies, waits for them, and re-layouts: 59.8 us -> 70.5 us
    unnamed x1 -> x0, blocking collectives: 11.6 us -> none
    dot_general x8 -> x10, matrix products: 58.8 us -> 70.2 us  [the longest x1 18 us: layer(): jnp.dot(hidden_full, up_complete, preferred_element_type=jnp.float32)]
    dot_general x4 -> x2, matrix products: 18.6 us -> 8.31 us  [weight_grad(): lax.dot_general(gathered, local_grad, (((0,), (0,)), ((), ())), preferred...]
    psum x3, blocking collectives: 30.9 us -> 41.1 us  [row_totals(): lax.psum((jnp.sum(first_term, axis=1), jnp.sum(second_term, axis=1)), 'col')]
    ppermute x28 -> x21, waiting for transfers between devices: 127 us -> 136 us  [row_scatter_sum(): lax.ppermute(outgoing, 'row', [(i, (i + shift) % count) for i in range(co...]
    all_gather x2, waiting for transfers between devices: 67.8 us -> 76.6 us  [rows_gathered_many(): pieces = lax.all_gather(flat, 'row', axis=0, tiled=False)]
    ppermute x28 -> x21, starting transfers between devices: 26.6 us -> 26.1 us  [row_scatter_sum(): lax.ppermute(outgoing, 'row', [(i, (i + shift) % count) for i in range(co...]
  transfers between devices with their start and end apart: 45 -> 41, of which waited for: 26 -> 21; matrix products, arithmetic and copies ran while one was open for 10% -> 11% of each run, Pallas kernels for 6% -> 6%
where the time goes in v5:
time: 841 us; the launch traced here: 835 us
  waiting for transfers between devices  432 us (51%)
  Pallas kernels  116 us (14%)
  matrix products  78.6 us (9%)
  local copies, waits for them, and re-layouts  70.5 us (8%)
  other arithmetic  41.9 us (5%)
  blocking collectives  41.1 us (5%)
  starting transfers between devices  39.6 us (5%)
  between operations  15.3 us (2%)
    ppermute x21, waiting for transfers between devices, row_scatter_sum(): lax.ppermute(outgoing, 'row', [(i, (i + shift) % count) for i in range(co...  136 us
    reduce_scatter x3, waiting for transfers between devices, feature_sum(): lax.psum_scatter(partial_rows, 'col', scatter_dimension=1, tiled=True)  118 us
    all_gather x4, waiting for transfers between devices, feature_whole(): return lax.all_gather(blocked, 'col', axis=1, tiled=True)  100 us
    all_gather x2, waiting for transfers between devices, rows_gathered_many(): pieces = lax.all_gather(flat, 'row', axis=0, tiled=False)  76.6 us
    pallas_call x1, Pallas kernels, attention_backward(): pl.pallas_call(functools.partial(_bwd_kernel, scale), grid=grid, in_specs...  68.9 us
    pallas_call x1, Pallas kernels, attention_forward(): pl.pallas_call(functools.partial(_fwd_kernel, scale), grid=grid, in_specs...  46.9 us
    psum x3, blocking collectives, row_totals(): lax.psum((jnp.sum(first_term, axis=1), jnp.sum(second_term, axis=1)), 'col')  41.1 us
    ppermute x21, starting transfers between devices, row_scatter_sum(): lax.ppermute(outgoing, 'row', [(i, (i + shift) % count) for i in range(co...  26.1 us
  transfers between devices with their start and end apart: 41, of which 21 were waited for; matrix products, arithmetic and copies ran while one was open for 11% of the time, Pallas kernels for 6%

profile of v5, /device:TPU:12, one launch (start us, length us, event | category | flops | bytes accessed | tf_op | source)
XLA Modules:
  0.0 834.7 jit_solution(14438091037228113461)
XLA Ops:
  21.3 30.2 %all-gather.20.cloned.1.call-done = bf16[589824]{0:T(1024)(128)(2,1)} async-done(((bf16[73728]{0:T(1024)(128)(2,1)}), bf16[589824]{0:T(1024)(128)(2,1)}) %all-gather.20.cloned.1.call-update) | async-done | bytes 1179664 | tf_op jit(solution)/shard_map/all_gather | solution.py:208
  59.0 46.4 %all-gather.22.cloned.1.call-done = bf16[1179648]{0:T(1024)(128)(2,1)} async-done(((bf16[147456]{0:T(1024)(128)(2,1)}), bf16[1179648]{0:T(1024)(128)(2,1)}) %all-gather.22.cloned.1.call-update) | async-done | bytes 2359312 | tf_op jit(solution)/shard_map/all_gather | solution.py:208
  109.6 25.4 %all-gather.10.cloned.1.call-done = bf16[2048,768]{0,1:T(8,128)(2,1)} async-done(((bf16[2048,192]{0,1:T(8,128)(2,1)}), bf16[2048,768]{0,1:T(8,128)(2,1)}) %all-gather.10.cloned.1.call-update) | async-done | bytes 3145744 | tf_op jit(solution)/shard_map/all_gather | solution.py:130
  145.6 4.6 fusion.27
  150.2 46.9 %shard_map.305 = (bf16[3,2048,64]{2,1,0:T(8,128)(2,1)S(1)}, f32[3,2048,1]{2,1,0:T(8,128)}, f32[3,2048,1]{2,1,0:T(8,128)}) custom-call(bf16[3,2048,64]{2,1,0:T(8,128)(2,1)S(1)} %get-tuple-element.161.q_ref, bf16[3,2048,64]{2,1,0:T(8,128)(2,1)S(1)} %bitcast.203, bf16[3,2048,64]{2,1,0:T(8,128)(2,1)} %get-tuple-element.162.v_ref, s32[2048,1]{1,0:T(8,128)S(1)} %copy-done.2, ...), custom_call_target="tpu_custom_call" | custom-call | flops 3221225472 | bytes 3145728 | tf_op jit(solution)/shard_map/pallas_call | solution.py:79
  210.5 16.7 %all-gather.12.cloned.1.call-done = bf16[2048,768]{0,1:T(8,128)(2,1)} async-done(((bf16[2048,192]{0,1:T(8,128)(2,1)}), bf16[2048,768]{0,1:T(8,128)(2,1)}) %all-gather.12.cloned.1.call-update) | async-done | bytes 3145744 | tf_op jit(solution)/shard_map/all_gather | solution.py:130
  227.2 6.9 fusion.65
  237.9 18.0 %multiply_convert_fusion = (bf16[2048,768]{1,0:T(8,128)(2,1)S(1)}, f32[2048,768]{1,0:T(8,128)}, f32[2048,768]{1,0:T(8,128)}) fusion(f32[768]{0:T(1024)S(1)} %copy-done.37, bf16[768,768]{1,0:T(8,128)(2,1)S(1)} %copy-done.11, f32[2048,768]{0,1:T(8,128)S(1)} %get-tuple-element.110), kind=kOutput, calls=%fused_computation.5 | convolution fusion | flops 2521300992 | bytes 23202816 | tf_op jit(solution)/shard_map/dot_general | solution.py:295
  257.6 4.6 fusion.75
  262.3 59.0 %reduce-scatter.4.cloned.1.call-done = f32[2048,192]{0,1:T(8,128)} async-done(((f32[2048,768]{0,1:T(8,128)}), f32[2048,192]{0,1:T(8,128)}) %reduce-scatter.4.cloned.1.call-update) | async-done | bytes 1572880 | tf_op jit(solution)/shard_map/reduce_scatter | solution.py:134
  323.5 10.3 %all-reduce.2 = (f32[2048]{0:T(1024)S(1)}, f32[2048]{0:T(1024)S(1)}) all-reduce(f32[2048]{0:T(1024)S(1)} %get-tuple-element.89, f32[2048]{0:T(1024)S(1)} %get-tuple-element.88), channel_id=1, replica_groups=mesh['row'=8,'col'=4] {'col'}, use_global_device_ids=true, to_apply=%region_6.0 | all-reduce | flops 4096 | bytes 32768 | tf_op jit(solution)/shard_map/psum | solution.py:138
  335.9 20.4 %all-reduce.1 = (f32[2048]{0:T(1024)S(1)}, f32[2048]{0:T(1024)S(1)}) all-reduce(f32[2048]{0:T(1024)S(1)} %get-tuple-element.85, f32[2048]{0:T(1024)S(1)} %get-tuple-element.90), channel_id=1, replica_groups=mesh['row'=8,'col'=4] {'col'}, use_global_device_ids=true, to_apply=%region_10.0 | all-reduce | flops 4096 | bytes 32768 | tf_op jit(solution)/shard_map/psum | solution.py:138
  359.0 29.1 %all-gather.16.cloned.1.call-done = bf16[2048,768]{0,1:T(8,128)(2,1)} async-done(((bf16[2048,192]{0,1:T(8,128)(2,1)}), bf16[2048,768]{0,1:T(8,128)(2,1)}) %all-gather.16.cloned.1.call-update) | async-done | bytes 3145744 | tf_op jit(solution)/shard_map/all_gather | solution.py:130
  388.1 10.9 %convert_reduce_fusion = (f32[768]{0:T(1024)S(1)}, bf16[2048,768]{1,0:T(8,128)(2,1)S(1)}) fusion(f32[2048,768]{1,0:T(8,128)} %get-tuple-element.109, f32[2048,768]{1,0:T(8,128)} %get-tuple-element.160, f32[768]{0:T(1024)S(1)} %copy-done.37, bf16[2048,768]{0,1:T(8,128)(2,1)} %all-gather.16.cloned.1.call-done, bf16[768,768]{0,1:T(8,128)(2,1)} %bitcast.222), kind=kOutput, calls=%fused_computation.3 | convolution fusion | flops 2442657024 | bytes 20060160 | tf_op jit(solution)/shard_map/dot_general | solution.py:307
  400.7 4.6 fusion.76
  405.3 58.9 %reduce-scatter.6.cloned.1.call-done = f32[2048,192]{0,1:T(8,128)} async-done(((f32[2048,768]{0,1:T(8,128)}), f32[2048,192]{0,1:T(8,128)}) %reduce-scatter.6.cloned.1.call-update) | async-done | bytes 1572880 | tf_op jit(solution)/shard_map/reduce_scatter | solution.py:134
  464.3 4.7 multiply_reduce_fusion.1
  468.9 10.4 %all-reduce = (f32[2048]{0:T(1024)S(1)}, f32[2048]{0:T(1024)S(1)}) all-reduce(f32[2048]{0:T(1024)S(1)} %get-tuple-element.81, f32[2048]{0:T(1024)S(1)} %get-tuple-element.86), channel_id=1, replica_groups=mesh['row'=8,'col'=4] {'col'}, use_global_device_ids=true, to_apply=%region_15.0 | all-reduce | flops 4096 | bytes 32768 | tf_op jit(solution)/shard_map/psum | solution.py:138
  482.6 29.1 %all-gather.18.cloned.1.call-done = bf16[2048,768]{0,1:T(8,128)(2,1)} async-done(((bf16[2048,192]{0,1:T(8,128)(2,1)}), bf16[2048,768]{0,1:T(8,128)(2,1)}) %all-gather.18.cloned.1.call-update) | async-done | bytes 3145744 | tf_op jit(solution)/shard_map/all_gather | solution.py:130
  518.6 68.9 %shard_map.306 = (bf16[3,2048,64]{2,1,0:T(8,128)(2,1)S(1)}, f32[3,2048,64]{2,1,0:T(8,128)}, f32[3,2048,64]{2,1,0:T(8,128)}) custom-call(bf16[3,2048,64]{2,1,0:T(8,128)(2,1)S(1)} %copy-done.1, bf16[3,2048,64]{2,1,0:T(8,128)(2,1)S(1)} %bitcast.204, bf16[3,2048,64]{2,1,0:T(8,128)(2,1)} %get-tuple-element.162.v_ref, bf16[3,2048,64]{2,1,0:T(8,128)(2,1)} %bitcast.220, ...), custom_call_target="tpu_custom_call" | custom-call | flops 8053063680 | bytes 6291456 | tf_op jit(solution)/shard_map/pallas_call | solution.py:107
  595.5 7.3 convolution_bitcast_fusion
  602.9 5.6 fusion.78
  608.5 5.7 fusion.29
  616.7 6.1 copy.108
  622.9 4.4 dynamic-slice_bitcast_fusion.6
  634.6 8.0 collective-permute-done.24
  643.0 62.6 %collective-permute-done.25 = f32[96,1536]{1,0:T(8,128)S(1)} collective-permute-done((f32[96,1536]{1,0:T(8,128)S(1)}, f32[96,1536]{1,0:T(8,128)S(1)}, u32[]{:S(2)}, u32[]{:S(2)}) %collective-permute-start.25) | collective-permute-done | bytes 589856 | tf_op jit(solution)/shard_map/ppermute | solution.py:164
  706.7 11.7 %collective-permute-done.26 = f32[96,1536]{1,0:T(8,128)} collective-permute-done((f32[96,1536]{1,0:T(8,128)}, f32[96,1536]{1,0:T(8,128)}, u32[]{:S(2)}, u32[]{:S(2)}) %collective-permute-start.26) | collective-permute-done | bytes 589856 | tf_op jit(solution)/shard_map/ppermute | solution.py:164
  718.4 11.7 %collective-permute-done.27 = f32[96,1536]{1,0:T(8,128)} collective-permute-done((f32[96,1536]{1,0:T(8,128)}, f32[96,1536]{1,0:T(8,128)}, u32[]{:S(2)}, u32[]{:S(2)}) %collective-permute-start.27) | collective-permute-done | bytes 589856 | tf_op jit(solution)/shard_map/ppermute | solution.py:164
  743.5 5.4 fusion.33
  781.9 10.7 %collective-permute-done.22 = f32[96,192]{1,0:T(8,128)S(1)} collective-permute-done((f32[96,192]{1,0:T(8,128)S(1)}, f32[96,192]{1,0:T(8,128)S(1)}, u32[]{:S(2)}, u32[]{:S(2)}) %collective-permute-start.22) | collective-permute-done | bytes 73760 | tf_op jit(solution)/shard_map/ppermute | solution.py:164
  800.7 13.7 %collective-permute-done.5 = f32[96,576]{1,0:T(8,128)} collective-permute-done((f32[96,576]{1,0:T(8,128)}, f32[96,576]{1,0:T(8,128)}, u32[]{:S(2)}, u32[]{:S(2)}) %collective-permute-start.5) | collective-permute-done | bytes 221216 | tf_op jit(solution)/shard_map/ppermute | solution.py:164
  (240 shorter events, 160.7 us)
Async XLA Ops:
  7.3 44.2 %all-gather.20.cloned.1.call-start = ((), (), s32[]{:S(2)}) async-start(), calls=%async_computation.11 | async-start | bytes 1327104 | tf_op jit(solution)/shard_map/all_gather | solution.py:208
  10.0 95.4 %all-gather.22.cloned.1.call-start = ((), (), s32[]{:S(2)}) async-start(), calls=%async_computation.12 | async-start | bytes 2654208 | tf_op jit(solution)/shard_map/all_gather | solution.py:208
  13.3 121.8 %all-gather.10.cloned.1.call-start = ((), (), s32[]{:S(2)}) async-start(), calls=%async_computation.3 | async-start | bytes 3932160 | tf_op jit(solution)/shard_map/all_gather | solution.py:130
  14.0 196.5 %all-gather.14.cloned.1.call-start = ((), (), s32[]{:S(2)}) async-start(), calls=%async_computation.5 | async-start | bytes 1474560 | tf_op jit(solution)/shard_map/all_gather | solution.py:267
  58.8 168.4 %all-gather.12.cloned.1.call-start = ((), (), s32[]{:S(2)}) async-start(), calls=%async_computation.4 | async-start | bytes 3932160 | tf_op jit(solution)/shard_map/all_gather | solution.py:130
  198.5 122.7 %reduce-scatter.4.cloned.1.call-start = ((), (), s32[]{:S(2)}) async-start(), calls=%async_computation.6 | async-start | bytes 7864320 | tf_op jit(solution)/shard_map/reduce_scatter | solution.py:134
  262.2 125.8 %all-gather.16.cloned.1.call-start = ((), (), s32[]{:S(2)}) async-start(), calls=%async_computation.7 | async-start | bytes 3932160 | tf_op jit(solution)/shard_map/all_gather | solution.py:130
  358.9 105.4 %reduce-scatter.6.cloned.1.call-start = ((), (), s32[]{:S(2)}) async-start(), calls=%async_computation.8 | async-start | bytes 7864320 | tf_op jit(solution)/shard_map/reduce_scatter | solution.py:134
  405.3 106.4 %all-gather.18.cloned.1.call-start = ((), (), s32[]{:S(2)}) async-start(), calls=%async_computation.9 | async-start | bytes 3932160 | tf_op jit(solution)/shard_map/all_gather | solution.py:130
  482.6 341.6 %reduce-scatter.8.cloned.1.call-start = ((), (), s32[]{:S(2)}) async-start(), calls=%async_computation.10 | async-start | bytes 7864320 | tf_op jit(solution)/shard_map/reduce_scatter | solution.py:134
  627.2 15.3 %collective-permute-start.24 = (f32[96,1536]{1,0:T(8,128)S(1)}, f32[96,1536]{1,0:T(8,128)S(1)}, u32[]{:S(2)}, u32[]{:S(2)}) collective-permute-start(f32[96,1536]{1,0:T(8,128)S(1)} %get-tuple-element.112), channel_id=1, source_target_pairs={{0,4},{4,8},{8,12},{12,16},{16,20},{20,24},{24,28},{28,0},{1,5},{5... | collective-permute-start | bytes 1769480 | tf_op jit(solution)/shard_map/ppermute | solution.py:164
  628.7 76.9 %collective-permute-start.25 = (f32[96,1536]{1,0:T(8,128)S(1)}, f32[96,1536]{1,0:T(8,128)S(1)}, u32[]{:S(2)}, u32[]{:S(2)}) collective-permute-start(f32[96,1536]{1,0:T(8,128)S(1)} %get-tuple-element.118), channel_id=1, source_target_pairs={{0,8},{4,12},{8,16},{12,20},{16,24},{20,28},{24,0},{28,4},{1,9},{5... | collective-permute-start | bytes 1769480 | tf_op jit(solution)/shard_map/ppermute | solution.py:164
  630.2 88.2 %collective-permute-start.26 = (f32[96,1536]{1,0:T(8,128)}, f32[96,1536]{1,0:T(8,128)}, u32[]{:S(2)}, u32[]{:S(2)}) collective-permute-start(f32[96,1536]{1,0:T(8,128)} %get-tuple-element.117), channel_id=1, source_target_pairs={{0,12},{4,16},{8,20},{12,24},{16,28},{20,0},{24,4},{28,8},{1,13},{... | collective-permute-start | bytes 1769480 | tf_op jit(solution)/shard_map/ppermute | solution.py:164
  631.6 98.4 %collective-permute-start.27 = (f32[96,1536]{1,0:T(8,128)}, f32[96,1536]{1,0:T(8,128)}, u32[]{:S(2)}, u32[]{:S(2)}) collective-permute-start(f32[96,1536]{1,0:T(8,128)} %get-tuple-element.116), channel_id=1, source_target_pairs={{0,16},{4,20},{8,24},{12,28},{16,0},{20,4},{24,8},{28,12},{1,17},{... | collective-permute-start | bytes 1769480 | tf_op jit(solution)/shard_map/ppermute | solution.py:164
  633.1 96.9 %collective-permute-start.28 = (f32[96,1536]{1,0:T(8,128)}, f32[96,1536]{1,0:T(8,128)}, u32[]{:S(2)}, u32[]{:S(2)}) collective-permute-start(f32[96,1536]{1,0:T(8,128)} %get-tuple-element.115), channel_id=1, source_target_pairs={{0,20},{4,24},{8,28},{12,0},{16,4},{20,8},{24,12},{28,16},{1,21},{... | collective-permute-start | bytes 1769480 | tf_op jit(solution)/shard_map/ppermute | solution.py:164
  642.5 89.7 %collective-permute-start.29 = (f32[96,1536]{1,0:T(8,128)}, f32[96,1536]{1,0:T(8,128)}, u32[]{:S(2)}, u32[]{:S(2)}) collective-permute-start(f32[96,1536]{1,0:T(8,128)} %get-tuple-element.114), channel_id=1, source_target_pairs={{0,24},{4,28},{8,0},{12,4},{16,8},{20,12},{24,16},{28,20},{1,25},{... | collective-permute-start | bytes 1769480 | tf_op jit(solution)/shard_map/ppermute | solution.py:164
  706.5 26.7 %collective-permute-start.30 = (f32[96,1536]{1,0:T(8,128)}, f32[96,1536]{1,0:T(8,128)}, u32[]{:S(2)}, u32[]{:S(2)}) collective-permute-start(f32[96,1536]{1,0:T(8,128)} %get-tuple-element.113), channel_id=1, source_target_pairs={{0,28},{4,0},{8,4},{12,8},{16,12},{20,16},{24,20},{28,24},{1,29},{... | collective-permute-start | bytes 1769480 | tf_op jit(solution)/shard_map/ppermute | solution.py:164
  737.9 17.0 %collective-permute-start.10 = (f32[2304]{0:T(1024)}, f32[2304]{0:T(1024)}, u32[]{:S(2)}, u32[]{:S(2)}) collective-permute-start(f32[2304]{0:T(1024)} %concatenate.18), channel_id=1, source_target_pairs={{0,4},{4,8},{8,12},{12,16},{16,20},{20,24},{24,28},{28,0},{1,5},{5... | collective-permute-start | bytes 27656 | tf_op jit(solution)/shard_map/ppermute | solution.py:174
  737.9 18.9 %collective-permute-start.11 = (f32[2304]{0:T(1024)}, f32[2304]{0:T(1024)}, u32[]{:S(2)}, u32[]{:S(2)}) collective-permute-start(f32[2304]{0:T(1024)} %concatenate.18), channel_id=1, source_target_pairs={{0,8},{4,12},{8,16},{12,20},{16,24},{20,28},{24,0},{28,4},{1,9},{5... | collective-permute-start | bytes 27656 | tf_op jit(solution)/shard_map/ppermute | solution.py:174
  737.9 21.0 %collective-permute-start.12 = (f32[2304]{0:T(1024)}, f32[2304]{0:T(1024)}, u32[]{:S(2)}, u32[]{:S(2)}) collective-permute-start(f32[2304]{0:T(1024)} %concatenate.18), channel_id=1, source_target_pairs={{0,12},{4,16},{8,20},{12,24},{16,28},{20,0},{24,4},{28,8},{1,13},{... | collective-permute-start | bytes 27656 | tf_op jit(solution)/shard_map/ppermute | solution.py:174
  740.8 19.1 %collective-permute-start.13 = (f32[2304]{0:T(1024)}, f32[2304]{0:T(1024)}, u32[]{:S(2)}, u32[]{:S(2)}) collective-permute-start(f32[2304]{0:T(1024)} %concatenate.18), channel_id=1, source_target_pairs={{0,16},{4,20},{8,24},{12,28},{16,0},{20,4},{24,8},{28,12},{1,17},{... | collective-permute-start | bytes 27656 | tf_op jit(solution)/shard_map/ppermute | solution.py:174
  742.3 18.2 %collective-permute-start.14 = (f32[2304]{0:T(1024)}, f32[2304]{0:T(1024)}, u32[]{:S(2)}, u32[]{:S(2)}) collective-permute-start(f32[2304]{0:T(1024)} %concatenate.18), channel_id=1, source_target_pairs={{0,20},{4,24},{8,28},{12,0},{16,4},{20,8},{24,12},{28,16},{1,21},{... | collective-permute-start | bytes 27656 | tf_op jit(solution)/shard_map/ppermute | solution.py:174
  763.7 17.8 %collective-permute-start.21 = (f32[96,192]{1,0:T(8,128)S(1)}, f32[96,192]{1,0:T(8,128)S(1)}, u32[]{:S(2)}, u32[]{:S(2)}) collective-permute-start(f32[96,192]{1,0:T(8,128)S(1)} %get-tuple-element.136), channel_id=1, source_target_pairs={{0,20},{4,24},{8,28},{12,0},{16,4},{20,8},{24,12},{28,16},{1,21},{... | collective-permute-start | bytes 221192 | tf_op jit(solution)/shard_map/ppermute | solution.py:164
  766.9 25.7 %collective-permute-start.22 = (f32[96,192]{1,0:T(8,128)S(1)}, f32[96,192]{1,0:T(8,128)S(1)}, u32[]{:S(2)}, u32[]{:S(2)}) collective-permute-start(f32[96,192]{1,0:T(8,128)S(1)} %get-tuple-element.135), channel_id=1, source_target_pairs={{0,24},{4,28},{8,0},{12,4},{16,8},{20,12},{24,16},{28,20},{1,25},{... | collective-permute-start | bytes 221192 | tf_op jit(solution)/shard_map/ppermute | solution.py:164
  772.3 22.1 %collective-permute-start.23 = (f32[96,192]{1,0:T(8,128)S(1)}, f32[96,192]{1,0:T(8,128)S(1)}, u32[]{:S(2)}, u32[]{:S(2)}) collective-permute-start(f32[96,192]{1,0:T(8,128)S(1)} %get-tuple-element.134), channel_id=1, source_target_pairs={{0,28},{4,0},{8,4},{12,8},{16,12},{20,16},{24,20},{28,24},{1,29},{... | collective-permute-start | bytes 221192 | tf_op jit(solution)/shard_map/ppermute | solution.py:164
  775.4 19.0 %collective-permute-start.3 = (f32[96,576]{1,0:T(8,128)S(1)}, f32[96,576]{1,0:T(8,128)S(1)}, u32[]{:S(2)}, u32[]{:S(2)}) collective-permute-start(f32[96,576]{1,0:T(8,128)S(1)} %get-tuple-element.125), channel_id=1, source_target_pairs={{0,4},{4,8},{8,12},{12,16},{16,20},{20,24},{24,28},{28,0},{1,5},{5... | collective-permute-start | bytes 663560 | tf_op jit(solution)/shard_map/ppermute | solution.py:164
  777.5 18.4 %collective-permute-start.4 = (f32[96,576]{1,0:T(8,128)S(1)}, f32[96,576]{1,0:T(8,128)S(1)}, u32[]{:S(2)}, u32[]{:S(2)}) collective-permute-start(f32[96,576]{1,0:T(8,128)S(1)} %get-tuple-element.131), channel_id=1, source_target_pairs={{0,8},{4,12},{8,16},{12,20},{16,24},{20,28},{24,0},{28,4},{1,9},{5... | collective-permute-start | bytes 663560 | tf_op jit(solution)/shard_map/ppermute | solution.py:164
  781.5 32.9 %collective-permute-start.5 = (f32[96,576]{1,0:T(8,128)}, f32[96,576]{1,0:T(8,128)}, u32[]{:S(2)}, u32[]{:S(2)}) collective-permute-start(f32[96,576]{1,0:T(8,128)} %get-tuple-element.130), channel_id=1, source_target_pairs={{0,12},{4,16},{8,20},{12,24},{16,28},{20,0},{24,4},{28,8},{1,13},{... | collective-permute-start | bytes 663560 | tf_op jit(solution)/shard_map/ppermute | solution.py:164
  792.6 25.3 %collective-permute-start.6 = (f32[96,576]{1,0:T(8,128)}, f32[96,576]{1,0:T(8,128)}, u32[]{:S(2)}, u32[]{:S(2)}) collective-permute-start(f32[96,576]{1,0:T(8,128)} %get-tuple-element.129), channel_id=1, source_target_pairs={{0,16},{4,20},{8,24},{12,28},{16,0},{20,4},{24,8},{28,12},{1,17},{... | collective-permute-start | bytes 663560 | tf_op jit(solution)/shard_map/ppermute | solution.py:164
  794.4 23.6 %collective-permute-start.7 = (f32[96,576]{1,0:T(8,128)}, f32[96,576]{1,0:T(8,128)}, u32[]{:S(2)}, u32[]{:S(2)}) collective-permute-start(f32[96,576]{1,0:T(8,128)} %get-tuple-element.128), channel_id=1, source_target_pairs={{0,20},{4,24},{8,28},{12,0},{16,4},{20,8},{24,12},{28,16},{1,21},{... | collective-permute-start | bytes 663560 | tf_op jit(solution)/shard_map/ppermute | solution.py:164
  794.4 27.3 %collective-permute-start.8 = (f32[96,576]{1,0:T(8,128)}, f32[96,576]{1,0:T(8,128)}, u32[]{:S(2)}, u32[]{:S(2)}) collective-permute-start(f32[96,576]{1,0:T(8,128)} %get-tuple-element.127), channel_id=1, source_target_pairs={{0,24},{4,28},{8,0},{12,4},{16,8},{20,12},{24,16},{28,20},{1,25},{... | collective-permute-start | bytes 663560 | tf_op jit(solution)/shard_map/ppermute | solution.py:164
  796.5 25.2 %collective-permute-start.9 = (f32[96,576]{1,0:T(8,128)}, f32[96,576]{1,0:T(8,128)}, u32[]{:S(2)}, u32[]{:S(2)}) collective-permute-start(f32[96,576]{1,0:T(8,128)} %get-tuple-element.126), channel_id=1, source_target_pairs={{0,28},{4,0},{8,4},{12,8},{16,12},{20,16},{24,20},{28,24},{1,29},{... | collective-permute-start | bytes 663560 | tf_op jit(solution)/shard_map/ppermute | solution.py:164
  (50 other events, 1066.2 us)
Sparse Core Ops, SparseCore 0:
  10.8 40.5 all-gather.19
  54.2 51.1 all-gather.21
  107.0 27.9 all-gather.9
  137.0 17.4 all-gather.13
  198.6 28.5 all-gather.11
  262.3 58.8 reduce-scatter.3
  359.0 28.9 all-gather.15
  405.4 58.8 reduce-scatter.5
  482.7 28.9 all-gather.17
  602.9 58.8 reduce-scatter.7

commit v6 on v5

--- a/solution.py
+++ b/solution.py
@@ -126,8 +126,9 @@
 NORM_EPS = 1e-06
 
 
-def feature_whole(blocked):
-    return lax.all_gather(blocked, "col", axis=1, tiled=True)
+def feature_whole_sent(blocked):
+    pieces = axis_gather(blocked, "col")
+    return jnp.moveaxis(pieces, 0, 1).reshape(blocked.shape[0], -1)
 
 
 def feature_sum(partial_rows):
@@ -203,9 +204,12 @@
     )
 
 
-def rows_gathered_many(blocks_and_axes):
+def rows_gathered_many(blocks_and_axes, sent=False):
     flat = jnp.concatenate([block.reshape(-1) for block, _ in blocks_and_axes])
-    pieces = lax.all_gather(flat, "row", axis=0, tiled=False)
+    if sent:
+        pieces = axis_gather(flat, "row")
+    else:
+        pieces = lax.all_gather(flat, "row", axis=0, tiled=False)
     wholes = []
     offset = 0
     for block, axis in blocks_and_axes:
@@ -261,9 +265,9 @@
     out_grad = cotangent.T.astype(jnp.float32)
     own_features = token_rows.shape[1]
     own_start = lax.axis_index("col") * own_features
-    inputs_full = feature_whole(token_rows)
+    inputs_full = axis_gather(inputs, "col").reshape(-1, inputs.shape[1]).T
     qkv_stack = jnp.stack([query_weight, key_weight, value_weight])
-    qkv_complete, output_rows = rows_gathered_many(((qkv_stack, 1), (output_weight, 1)))
+    qkv_complete, output_rows = rows_gathered_many(((qkv_stack, 1), (output_weight, 1)), sent=True)
     output_complete = lax.all_gather(output_rows, "col", axis=0, tiled=True)
     up_complete, down_complete = rows_gathered_many(((up_weight, 0), (down_weight, 1)))
     projected = jnp.einsum(
@@ -276,7 +280,7 @@
         queries, key_all, value_all, labels, score_scale
     )
     attended = heads_beside(attended_h)
-    attended_full = feature_whole(attended)
+    attended_full = feature_whole_sent(attended)
     vectors_full = axis_gather(jnp.stack([output_bias, attn_gain, attn_shift]), "col")
     output_bias_full, gain_one_full, shift_one_full = (
         vectors_full[:, which].reshape(-1) for which in range(3)
@@ -302,7 +306,7 @@
         out_grad, normed_two, inverse_two, final_gain
     )
     branch_grad = second_grad.astype(jnp.bfloat16)
-    branch_full = feature_whole(branch_grad)
+    branch_full = feature_whole_sent(branch_grad)
     down_partial = weight_partial(branch_full, acted)
     acted_grad = lax.dot_general(
         branch_full, down_complete, (((1,), (1,)), ((), ())), preferred_element_type=jnp.float32
@@ -321,7 +325,7 @@
         hidden_grad, normed_one, inverse_one, attn_gain
     )
     attn_branch_grad = first_grad.astype(jnp.bfloat16)
-    attn_branch_full = feature_whole(attn_branch_grad)
+    attn_branch_full = feature_whole_sent(attn_branch_grad)
     output_weight_grad = weight_grad(attn_branch_full, attended).T
     attended_grad = lax.dot_general(
         attn_branch_full, output_rows, (((1,), (1,)), ((), ())), preferred_element_type=jnp.float32

time: 841 us -> 841 us (level)
  waiting for transfers between devices: 432 us -> 400 us
  local copies, waits for them, and re-layouts: 70.5 us -> 89.1 us
  starting transfers between devices: 39.6 us -> 55.5 us
  blocking collectives: 41.1 us -> 30.7 us
    ppermute x3 -> x22, waiting for transfers between devices: 0.01 us -> 137 us  [axis_gather(): lax.ppermute(values, axis, [(i, (i + shift) % count) for i in range(count)])]
    all_gather x4 -> x0, waiting for transfers between devices: 100 us -> none  [feature_whole(): return lax.all_gather(blocked, 'col', axis=1, tiled=True)]
    all_gather x2 -> x1, waiting for transfers between devices: 76.6 us -> 0.01 us  [rows_gathered_many(): pieces = lax.all_gather(flat, 'row', axis=0, tiled=False)]
    gather x1 -> x6, local copies, waits for them, and re-layouts: 0.57 us -> 17.8 us  [axis_gather(): return jnp.stack(arrived)[order]]
    ppermute x3 -> x22, starting transfers between devices: 3 us -> 19.9 us  [axis_gather(): lax.ppermute(values, axis, [(i, (i + shift) % count) for i in range(count)])]
    psum x3, blocking collectives: 41.1 us -> 30.7 us  [row_totals(): lax.psum((jnp.sum(first_term, axis=1), jnp.sum(second_term, axis=1)), 'col')]
    another operation x2 -> x6, other arithmetic: 0.02 us -> 10.3 us  [axis_gather(): return jnp.stack(arrived)[order]]
  transfers between devices with their start and end apart: 41 -> 55, of which waited for: 21 -> 30; matrix products, arithmetic and copies ran while one was open for 11% -> 12% of each run, Pallas kernels for 6% -> 6%
where the time goes in v6:
time: 841 us; the launch traced here: 836 us
  waiting for transfers between devices  400 us (48%)
  Pallas kernels  116 us (14%)
  local copies, waits for them, and re-layouts  89.1 us (11%)
  matrix products  78.8 us (9%)
  starting transfers between devices  55.5 us (7%)
  other arithmetic  50.2 us (6%)
  blocking collectives  30.7 us (4%)
  between operations  15.1 us (2%)
    ppermute x21, waiting for transfers between devices, row_scatter_sum(): lax.ppermute(outgoing, 'row', [(i, (i + shift) % count) for i in range(co...  141 us
    ppermute x22, waiting for transfers between devices, axis_gather(): lax.ppermute(values, axis, [(i, (i + shift) % count) for i in range(count)])  137 us
    reduce_scatter x3, waiting for transfers between devices, feature_sum(): lax.psum_scatter(partial_rows, 'col', scatter_dimension=1, tiled=True)  122 us
    pallas_call x1, Pallas kernels, attention_backward(): pl.pallas_call(functools.partial(_bwd_kernel, scale), grid=grid, in_specs...  68.7 us
    pallas_call x1, Pallas kernels, attention_forward(): pl.pallas_call(functools.partial(_fwd_kernel, scale), grid=grid, in_specs...  47.2 us
    psum x3, blocking collectives, row_totals(): lax.psum((jnp.sum(first_term, axis=1), jnp.sum(second_term, axis=1)), 'col')  30.7 us
    ppermute x21, starting transfers between devices, row_scatter_sum(): lax.ppermute(outgoing, 'row', [(i, (i + shift) % count) for i in range(co...  25.4 us
    ppermute x22, starting transfers between devices, axis_gather(): lax.ppermute(values, axis, [(i, (i + shift) % count) for i in range(count)])  19.9 us
  transfers between devices with their start and end apart: 55, of which 30 were waited for; matrix products, arithmetic and copies ran while one was open for 12% of the time, Pallas kernels for 6%

profile of v6, /device:TPU:12, one launch (start us, length us, event | category | flops | bytes accessed | tf_op | source)
XLA Modules:
  0.0 835.6 jit_solution(5487274246435116716)
XLA Ops:
  17.8 13.0 %collective-permute-done.4 = bf16[73728]{0:T(1024)(128)(2,1)S(1)} collective-permute-done((bf16[73728]{0:T(1024)(128)(2,1)S(1)}, bf16[73728]{0:T(1024)(128)(2,1)S(1)}, u32[]{:S(2)}, u32[]{:S(2)}) %collective-permute-start.4) | collective-permute-done | bytes 147488 | tf_op jit(solution)/shard_map/ppermute | solution.py:187
  56.8 20.7 %collective-permute-done.2 = bf16[192,2048]{1,0:T(8,128)(2,1)} collective-permute-done((bf16[192,2048]{1,0:T(8,128)(2,1)}, bf16[192,2048]{1,0:T(8,128)(2,1)}, u32[]{:S(2)}, u32[]{:S(2)}) %collective-permute-start.2) | collective-permute-done | bytes 786464 | tf_op jit(solution)/shard_map/ppermute | solution.py:187
  95.9 4.6 fusion.26
  100.4 47.2 %shard_map.305 = (bf16[3,2048,64]{2,1,0:T(8,128)(2,1)S(1)}, f32[3,2048,1]{2,1,0:T(8,128)}, f32[3,2048,1]{2,1,0:T(8,128)}) custom-call(bf16[3,2048,64]{2,1,0:T(8,128)(2,1)S(1)} %get-tuple-element.144.q_ref, bf16[3,2048,64]{2,1,0:T(8,128)(2,1)S(1)} %bitcast.253, bf16[3,2048,64]{2,1,0:T(8,128)(2,1)} %get-tuple-element.145.v_ref, s32[2048,1]{1,0:T(8,128)S(1)} %copy-done.2, ...), custom_call_target="tpu_custom_call" | custom-call | flops 3221225472 | bytes 3145728 | tf_op jit(solution)/shard_map/pallas_call | solution.py:79
  152.6 32.0 %collective-permute-done.13 = f32[3,192]{1,0:T(4,128)S(1)} collective-permute-done((f32[3,192]{1,0:T(4,128)S(1)}, f32[3,192]{1,0:T(4,128)S(1)}, u32[]{:S(2)}, u32[]{:S(2)}) %collective-permute-start.13) | collective-permute-done | bytes 2336 | tf_op jit(solution)/shard_map/ppermute | solution.py:187
  194.4 7.0 fusion.63
  201.4 5.6 multiply_add_fusion
  222.5 19.9 %multiply_convert_fusion = (bf16[2048,768]{1,0:T(8,128)(2,1)S(1)}, f32[2048,768]{1,0:T(8,128)}, f32[2048,768]{1,0:T(8,128)}) fusion(f32[768]{0:T(1024)S(1)} %copy-done.31, bf16[768,768]{1,0:T(8,128)(2,1)} %reshape_reshape.3, f32[2048,768]{0,1:T(8,128)} %get-tuple-element.93), kind=kOutput, calls=%fused_computation.12 | convolution fusion | flops 2521300992 | bytes 23202816 | tf_op jit(solution)/shard_map/dot_general | solution.py:299
  244.0 4.6 fusion.73
  248.7 62.1 %reduce-scatter.4.cloned.1.call-done = f32[2048,192]{0,1:T(8,128)} async-done(((f32[2048,768]{0,1:T(8,128)}), f32[2048,192]{0,1:T(8,128)}) %reduce-scatter.4.cloned.1.call-update) | async-done | bytes 1572880 | tf_op jit(solution)/shard_map/reduce_scatter | solution.py:135
  313.1 10.3 %all-reduce.2 = (f32[2048]{0:T(1024)S(1)}, f32[2048]{0:T(1024)S(1)}) all-reduce(f32[2048]{0:T(1024)S(1)} %get-tuple-element.72, f32[2048]{0:T(1024)S(1)} %get-tuple-element.71), channel_id=1, replica_groups=mesh['row'=8,'col'=4] {'col'}, use_global_device_ids=true, to_apply=%region_6.0 | all-reduce | flops 4096 | bytes 32768 | tf_op jit(solution)/shard_map/psum | solution.py:139
  325.5 10.1 %all-reduce.1 = (f32[2048]{0:T(1024)S(1)}, f32[2048]{0:T(1024)S(1)}) all-reduce(f32[2048]{0:T(1024)S(1)} %get-tuple-element.68, f32[2048]{0:T(1024)S(1)} %get-tuple-element.73), channel_id=1, replica_groups=mesh['row'=8,'col'=4] {'col'}, use_global_device_ids=true, to_apply=%region_10.0 | all-reduce | flops 4096 | bytes 32768 | tf_op jit(solution)/shard_map/psum | solution.py:139
  339.9 16.7 %collective-permute-done.16 = bf16[2048,192]{0,1:T(8,128)(2,1)S(1)} collective-permute-done((bf16[2048,192]{0,1:T(8,128)(2,1)S(1)}, bf16[2048,192]{0,1:T(8,128)(2,1)S(1)}, u32[]{:S(2)}, u32[]{:S(2)}) %collective-permute-start.16) | collective-permute-done | bytes 786464 | tf_op jit(solution)/shard_map/ppermute | solution.py:187
  357.9 14.7 %collective-permute-done.18 = bf16[2048,192]{0,1:T(8,128)(2,1)S(1)} collective-permute-done((bf16[2048,192]{0,1:T(8,128)(2,1)S(1)}, bf16[2048,192]{0,1:T(8,128)(2,1)S(1)}, u32[]{:S(2)}, u32[]{:S(2)}) %collective-permute-start.18) | collective-permute-done | bytes 786464 | tf_op jit(solution)/shard_map/ppermute | solution.py:187
  379.2 10.9 %convert_reduce_fusion = (f32[768]{0:T(1024)S(1)}, bf16[2048,768]{1,0:T(8,128)(2,1)S(1)}) fusion(f32[2048,768]{1,0:T(8,128)} %get-tuple-element.92, f32[2048,768]{1,0:T(8,128)} %get-tuple-element.143, f32[768]{0:T(1024)S(1)} %copy-done.31, bf16[2048,768]{0,1:T(8,128)(2,1)} %bitcast.266, bf16[768,768]{0,1:T(8,128)(2,1)} %bitcast.281), kind=kOutput, calls=%fused_computation.10 | convolution fusion | flops 2442657024 | bytes 20060160 | tf_op jit(solution)/shard_map/dot_general | solution.py:311
  391.9 4.6 fusion.74
  396.5 60.3 %reduce-scatter.6.cloned.1.call-done = f32[2048,192]{0,1:T(8,128)} async-done(((f32[2048,768]{0,1:T(8,128)}), f32[2048,192]{0,1:T(8,128)}) %reduce-scatter.6.cloned.1.call-update) | async-done | bytes 1572880 | tf_op jit(solution)/shard_map/reduce_scatter | solution.py:135
  456.9 4.7 multiply_reduce_fusion.1
  461.5 10.2 %all-reduce = (f32[2048]{0:T(1024)S(1)}, f32[2048]{0:T(1024)S(1)}) all-reduce(f32[2048]{0:T(1024)S(1)} %get-tuple-element.66, f32[2048]{0:T(1024)S(1)} %get-tuple-element.69), channel_id=1, replica_groups=mesh['row'=8,'col'=4] {'col'}, use_global_device_ids=true, to_apply=%region_15.0 | all-reduce | flops 4096 | bytes 32768 | tf_op jit(solution)/shard_map/psum | solution.py:139
  476.7 16.7 %collective-permute-done.19 = bf16[2048,192]{0,1:T(8,128)(2,1)S(1)} collective-permute-done((bf16[2048,192]{0,1:T(8,128)(2,1)S(1)}, bf16[2048,192]{0,1:T(8,128)(2,1)S(1)}, u32[]{:S(2)}, u32[]{:S(2)}) %collective-permute-start.19) | collective-permute-done | bytes 786464 | tf_op jit(solution)/shard_map/ppermute | solution.py:187
  494.7 14.7 %collective-permute-done.21 = bf16[2048,192]{0,1:T(8,128)(2,1)S(1)} collective-permute-done((bf16[2048,192]{0,1:T(8,128)(2,1)S(1)}, bf16[2048,192]{0,1:T(8,128)(2,1)S(1)}, u32[]{:S(2)}, u32[]{:S(2)}) %collective-permute-start.21) | collective-permute-done | bytes 786464 | tf_op jit(solution)/shard_map/ppermute | solution.py:187
  522.8 68.7 %shard_map.306 = (bf16[3,2048,64]{2,1,0:T(8,128)(2,1)S(1)}, f32[3,2048,64]{2,1,0:T(8,128)}, f32[3,2048,64]{2,1,0:T(8,128)}) custom-call(bf16[3,2048,64]{2,1,0:T(8,128)(2,1)S(1)} %copy-done.1, bf16[3,2048,64]{2,1,0:T(8,128)(2,1)S(1)} %bitcast.254, bf16[3,2048,64]{2,1,0:T(8,128)(2,1)} %get-tuple-element.145.v_ref, bf16[3,2048,64]{2,1,0:T(8,128)(2,1)} %bitcast.279, ...), custom_call_target="tpu_custom_call" | custom-call | flops 8053063680 | bytes 6291456 | tf_op jit(solution)/shard_map/pallas_call | solution.py:107
  599.5 7.2 convolution_bitcast_fusion
  606.8 5.8 fusion.76
  612.6 6.7 fusion.28
  621.8 6.2 copy.82
  639.3 8.9 %collective-permute-done.43 = f32[96,1536]{1,0:T(8,128)S(1)} collective-permute-done((f32[96,1536]{1,0:T(8,128)S(1)}, f32[96,1536]{1,0:T(8,128)S(1)}, u32[]{:S(2)}, u32[]{:S(2)}) %collective-permute-start.43) | collective-permute-done | bytes 589856 | tf_op jit(solution)/shard_map/ppermute | solution.py:165
  648.7 12.1 %collective-permute-done.44 = f32[96,1536]{1,0:T(8,128)S(1)} collective-permute-done((f32[96,1536]{1,0:T(8,128)S(1)}, f32[96,1536]{1,0:T(8,128)S(1)}, u32[]{:S(2)}, u32[]{:S(2)}) %collective-permute-start.44) | collective-permute-done | bytes 589856 | tf_op jit(solution)/shard_map/ppermute | solution.py:165
  661.9 61.3 %collective-permute-done.45 = f32[96,1536]{1,0:T(8,128)} collective-permute-done((f32[96,1536]{1,0:T(8,128)}, f32[96,1536]{1,0:T(8,128)}, u32[]{:S(2)}, u32[]{:S(2)}) %collective-permute-start.45) | collective-permute-done | bytes 589856 | tf_op jit(solution)/shard_map/ppermute | solution.py:165
  723.2 12.5 %collective-permute-done.46 = f32[96,1536]{1,0:T(8,128)} collective-permute-done((f32[96,1536]{1,0:T(8,128)}, f32[96,1536]{1,0:T(8,128)}, u32[]{:S(2)}, u32[]{:S(2)}) %collective-permute-start.46) | collective-permute-done | bytes 589856 | tf_op jit(solution)/shard_map/ppermute | solution.py:165
  783.1 13.3 %collective-permute-done.41 = f32[96,192]{1,0:T(8,128)S(1)} collective-permute-done((f32[96,192]{1,0:T(8,128)S(1)}, f32[96,192]{1,0:T(8,128)S(1)}, u32[]{:S(2)}, u32[]{:S(2)}) %collective-permute-start.41) | collective-permute-done | bytes 73760 | tf_op jit(solution)/shard_map/ppermute | solution.py:165
  801.7 13.3 %collective-permute-done.24 = f32[96,576]{1,0:T(8,128)} collective-permute-done((f32[96,576]{1,0:T(8,128)S(1)}, f32[96,576]{1,0:T(8,128)}, u32[]{:S(2)}, u32[]{:S(2)}) %collective-permute-start.24) | collective-permute-done | bytes 221216 | tf_op jit(solution)/shard_map/ppermute | solution.py:165
  (270 shorter events, 213.9 us)
Async XLA Ops:
  7.2 187.2 %all-gather.4.cloned.1.call-start = ((), (), s32[]{:S(2)}) async-start(), calls=%async_computation.3 | async-start | bytes 1474560 | tf_op jit(solution)/shard_map/all_gather | solution.py:271
  12.4 22.7 %collective-permute-start.5 = (bf16[73728]{0:T(1024)(128)(2,1)S(1)}, bf16[73728]{0:T(1024)(128)(2,1)S(1)}, u32[]{:S(2)}, u32[]{:S(2)}) collective-permute-start(bf16[73728]{0:T(1024)(128)(2,1)S(1)} %constant_dynamic-update-slice_fusion), channel_id=1, source_target_pairs={{0,12},{4,16},{8,20},{12,24},{16,28},{20,0},{24,4},{28,8},{1,13},{... | collective-permute-start | bytes 442376 | tf_op jit(solution)/shard_map/ppermute | solution.py:187
  13.6 22.5 %collective-permute-start.6 = (bf16[73728]{0:T(1024)(128)(2,1)S(1)}, bf16[73728]{0:T(1024)(128)(2,1)S(1)}, u32[]{:S(2)}, u32[]{:S(2)}) collective-permute-start(bf16[73728]{0:T(1024)(128)(2,1)S(1)} %constant_dynamic-update-slice_fusion), channel_id=1, source_target_pairs={{0,16},{4,20},{8,24},{12,28},{16,0},{20,4},{24,8},{28,12},{1,17},{... | collective-permute-start | bytes 442376 | tf_op jit(solution)/shard_map/ppermute | solution.py:187
  15.3 22.4 %collective-permute-start.7 = (bf16[73728]{0:T(1024)(128)(2,1)S(1)}, bf16[73728]{0:T(1024)(128)(2,1)S(1)}, u32[]{:S(2)}, u32[]{:S(2)}) collective-permute-start(bf16[73728]{0:T(1024)(128)(2,1)S(1)} %constant_dynamic-update-slice_fusion), channel_id=1, source_target_pairs={{0,20},{4,24},{8,28},{12,0},{16,4},{20,8},{24,12},{28,16},{1,21},{... | collective-permute-start | bytes 442376 | tf_op jit(solution)/shard_map/ppermute | solution.py:187
  16.6 22.2 %collective-permute-start.8 = (bf16[73728]{0:T(1024)(128)(2,1)S(1)}, bf16[73728]{0:T(1024)(128)(2,1)S(1)}, u32[]{:S(2)}, u32[]{:S(2)}) collective-permute-start(bf16[73728]{0:T(1024)(128)(2,1)S(1)} %constant_dynamic-update-slice_fusion), channel_id=1, source_target_pairs={{0,24},{4,28},{8,0},{12,4},{16,8},{20,12},{24,16},{28,20},{1,25},{... | collective-permute-start | bytes 442376 | tf_op jit(solution)/shard_map/ppermute | solution.py:187
  36.1 20.7 %collective-permute-start.1 = (bf16[192,2048]{1,0:T(8,128)(2,1)}, bf16[192,2048]{1,0:T(8,128)(2,1)}, u32[]{:S(2)}, u32[]{:S(2)}) collective-permute-start(bf16[192,2048]{1,0:T(8,128)(2,1)} %param.18), channel_id=1, source_target_pairs={{0,2},{1,3},{2,0},{3,1},{4,6},{5,7},{6,4},{7,5},{8,10},{9,11},{10,... | collective-permute-start | bytes 2359304 | tf_op jit(solution)/shard_map/ppermute | solution.py:187
  37.7 39.8 %collective-permute-start.2 = (bf16[192,2048]{1,0:T(8,128)(2,1)}, bf16[192,2048]{1,0:T(8,128)(2,1)}, u32[]{:S(2)}, u32[]{:S(2)}) collective-permute-start(bf16[192,2048]{1,0:T(8,128)(2,1)} %param.18), channel_id=1, source_target_pairs={{0,3},{1,0},{2,1},{3,2},{4,7},{5,4},{6,5},{7,6},{8,11},{9,8},{10,9... | collective-permute-start | bytes 2359304 | tf_op jit(solution)/shard_map/ppermute | solution.py:187
  45.9 161.0 %all-gather.6.cloned.1.call-start = ((), (), s32[]{:S(2)}) async-start(), calls=%async_computation.7 | async-start | bytes 2654208 | tf_op jit(solution)/shard_map/all_gather | solution.py:212
  46.8 264.1 %reduce-scatter.4.cloned.1.call-start = ((), (), s32[]{:S(2)}) async-start(), calls=%async_computation.4 | async-start | bytes 7864320 | tf_op jit(solution)/shard_map/reduce_scatter | solution.py:135
  149.0 38.1 %collective-permute-start.10 = (bf16[2048,192]{0,1:T(8,128)(2,1)}, bf16[2048,192]{0,1:T(8,128)(2,1)S(1)}, u32[]{:S(2)}, u32[]{:S(2)}) collective-permute-start(bf16[2048,192]{0,1:T(8,128)(2,1)} %bitcast.270), channel_id=1, source_target_pairs={{0,1},{1,2},{2,3},{3,0},{4,5},{5,6},{6,7},{7,4},{8,9},{9,10},{10,1... | collective-permute-start | bytes 2359304 | tf_op jit(solution)/shard_map/ppermute | solution.py:187
  149.7 37.4 %collective-permute-start.11 = (bf16[2048,192]{0,1:T(8,128)(2,1)}, bf16[2048,192]{0,1:T(8,128)(2,1)S(1)}, u32[]{:S(2)}, u32[]{:S(2)}) collective-permute-start(bf16[2048,192]{0,1:T(8,128)(2,1)} %bitcast.271), channel_id=1, source_target_pairs={{0,2},{1,3},{2,0},{3,1},{4,6},{5,7},{6,4},{7,5},{8,10},{9,11},{10,... | collective-permute-start | bytes 2359304 | tf_op jit(solution)/shard_map/ppermute | solution.py:187
  151.1 36.0 %collective-permute-start.12 = (bf16[2048,192]{0,1:T(8,128)(2,1)}, bf16[2048,192]{0,1:T(8,128)(2,1)}, u32[]{:S(2)}, u32[]{:S(2)}) collective-permute-start(bf16[2048,192]{0,1:T(8,128)(2,1)} %bitcast.272), channel_id=1, source_target_pairs={{0,3},{1,0},{2,1},{3,2},{4,7},{5,4},{6,5},{7,6},{8,11},{9,8},{10,9... | collective-permute-start | bytes 2359304 | tf_op jit(solution)/shard_map/ppermute | solution.py:187
  151.2 33.5 %collective-permute-start.13 = (f32[3,192]{1,0:T(4,128)S(1)}, f32[3,192]{1,0:T(4,128)S(1)}, u32[]{:S(2)}, u32[]{:S(2)}) collective-permute-start(f32[3,192]{1,0:T(4,128)S(1)} %get-tuple-element.141), channel_id=1, source_target_pairs={{0,1},{1,2},{2,3},{3,0},{4,5},{5,6},{6,7},{7,4},{8,9},{9,10},{10,1... | collective-permute-start | bytes 6920 | tf_op jit(solution)/shard_map/ppermute | solution.py:187
  151.7 34.3 %collective-permute-start.14 = (f32[3,192]{1,0:T(4,128)S(1)}, f32[3,192]{1,0:T(4,128)S(1)}, u32[]{:S(2)}, u32[]{:S(2)}) collective-permute-start(f32[3,192]{1,0:T(4,128)S(1)} %get-tuple-element.141), channel_id=1, source_target_pairs={{0,2},{1,3},{2,0},{3,1},{4,6},{5,7},{6,4},{7,5},{8,10},{9,11},{10,... | collective-permute-start | bytes 6920 | tf_op jit(solution)/shard_map/ppermute | solution.py:187
  248.6 208.2 %reduce-scatter.6.cloned.1.call-start = ((), (), s32[]{:S(2)}) async-start(), calls=%async_computation.5 | async-start | bytes 7864320 | tf_op jit(solution)/shard_map/reduce_scatter | solution.py:135
  337.5 20.5 %collective-permute-start.17 = (bf16[2048,192]{0,1:T(8,128)(2,1)S(1)}, bf16[2048,192]{0,1:T(8,128)(2,1)S(1)}, u32[]{:S(2)}, u32[]{:S(2)}) collective-permute-start(bf16[2048,192]{0,1:T(8,128)(2,1)S(1)} %get-tuple-element.84), channel_id=1, source_target_pairs={{0,2},{1,3},{2,0},{3,1},{4,6},{5,7},{6,4},{7,5},{8,10},{9,11},{10,... | collective-permute-start | bytes 2359304 | tf_op jit(solution)/shard_map/ppermute | solution.py:187
  338.5 34.1 %collective-permute-start.18 = (bf16[2048,192]{0,1:T(8,128)(2,1)S(1)}, bf16[2048,192]{0,1:T(8,128)(2,1)S(1)}, u32[]{:S(2)}, u32[]{:S(2)}) collective-permute-start(bf16[2048,192]{0,1:T(8,128)(2,1)S(1)} %get-tuple-element.84), channel_id=1, source_target_pairs={{0,3},{1,0},{2,1},{3,2},{4,7},{5,4},{6,5},{7,6},{8,11},{9,8},{10,9... | collective-permute-start | bytes 2359304 | tf_op jit(solution)/shard_map/ppermute | solution.py:187
  396.5 428.8 %reduce-scatter.8.cloned.1.call-start = ((), (), s32[]{:S(2)}) async-start(), calls=%async_computation.6 | async-start | bytes 7864320 | tf_op jit(solution)/shard_map/reduce_scatter | solution.py:135
  475.3 34.1 %collective-permute-start.21 = (bf16[2048,192]{0,1:T(8,128)(2,1)S(1)}, bf16[2048,192]{0,1:T(8,128)(2,1)S(1)}, u32[]{:S(2)}, u32[]{:S(2)}) collective-permute-start(bf16[2048,192]{0,1:T(8,128)(2,1)S(1)} %get-tuple-element.88), channel_id=1, source_target_pairs={{0,3},{1,0},{2,1},{3,2},{4,7},{5,4},{6,5},{7,6},{8,11},{9,8},{10,9... | collective-permute-start | bytes 2359304 | tf_op jit(solution)/shard_map/ppermute | solution.py:187
  633.5 27.3 %collective-permute-start.44 = (f32[96,1536]{1,0:T(8,128)S(1)}, f32[96,1536]{1,0:T(8,128)S(1)}, u32[]{:S(2)}, u32[]{:S(2)}) collective-permute-start(f32[96,1536]{1,0:T(8,128)S(1)} %get-tuple-element.101), channel_id=1, source_target_pairs={{0,8},{4,12},{8,16},{12,20},{16,24},{20,28},{24,0},{28,4},{1,9},{5... | collective-permute-start | bytes 1769480 | tf_op jit(solution)/shard_map/ppermute | solution.py:165
  635.0 88.2 %collective-permute-start.45 = (f32[96,1536]{1,0:T(8,128)}, f32[96,1536]{1,0:T(8,128)}, u32[]{:S(2)}, u32[]{:S(2)}) collective-permute-start(f32[96,1536]{1,0:T(8,128)} %get-tuple-element.100), channel_id=1, source_target_pairs={{0,12},{4,16},{8,20},{12,24},{16,28},{20,0},{24,4},{28,8},{1,13},{... | collective-permute-start | bytes 1769480 | tf_op jit(solution)/shard_map/ppermute | solution.py:165
  636.4 99.3 %collective-permute-start.46 = (f32[96,1536]{1,0:T(8,128)}, f32[96,1536]{1,0:T(8,128)}, u32[]{:S(2)}, u32[]{:S(2)}) collective-permute-start(f32[96,1536]{1,0:T(8,128)} %get-tuple-element.99), channel_id=1, source_target_pairs={{0,16},{4,20},{8,24},{12,28},{16,0},{20,4},{24,8},{28,12},{1,17},{... | collective-permute-start | bytes 1769480 | tf_op jit(solution)/shard_map/ppermute | solution.py:165
  637.9 97.8 %collective-permute-start.47 = (f32[96,1536]{1,0:T(8,128)}, f32[96,1536]{1,0:T(8,128)}, u32[]{:S(2)}, u32[]{:S(2)}) collective-permute-start(f32[96,1536]{1,0:T(8,128)} %get-tuple-element.98), channel_id=1, source_target_pairs={{0,20},{4,24},{8,28},{12,0},{16,4},{20,8},{24,12},{28,16},{1,21},{... | collective-permute-start | bytes 1769480 | tf_op jit(solution)/shard_map/ppermute | solution.py:165
  648.2 89.4 %collective-permute-start.48 = (f32[96,1536]{1,0:T(8,128)}, f32[96,1536]{1,0:T(8,128)}, u32[]{:S(2)}, u32[]{:S(2)}) collective-permute-start(f32[96,1536]{1,0:T(8,128)} %get-tuple-element.97), channel_id=1, source_target_pairs={{0,24},{4,28},{8,0},{12,4},{16,8},{20,12},{24,16},{28,20},{1,25},{... | collective-permute-start | bytes 1769480 | tf_op jit(solution)/shard_map/ppermute | solution.py:165
  661.7 77.2 %collective-permute-start.49 = (f32[96,1536]{1,0:T(8,128)S(1)}, f32[96,1536]{1,0:T(8,128)}, u32[]{:S(2)}, u32[]{:S(2)}) collective-permute-start(f32[96,1536]{1,0:T(8,128)S(1)} %get-tuple-element.96), channel_id=1, source_target_pairs={{0,28},{4,0},{8,4},{12,8},{16,12},{20,16},{24,20},{28,24},{1,29},{... | collective-permute-start | bytes 1769480 | tf_op jit(solution)/shard_map/ppermute | solution.py:165
  767.4 29.1 %collective-permute-start.41 = (f32[96,192]{1,0:T(8,128)S(1)}, f32[96,192]{1,0:T(8,128)S(1)}, u32[]{:S(2)}, u32[]{:S(2)}) collective-permute-start(f32[96,192]{1,0:T(8,128)S(1)} %get-tuple-element.118), channel_id=1, source_target_pairs={{0,24},{4,28},{8,0},{12,4},{16,8},{20,12},{24,16},{28,20},{1,25},{... | collective-permute-start | bytes 221192 | tf_op jit(solution)/shard_map/ppermute | solution.py:165
  773.7 22.8 %collective-permute-start.42 = (f32[96,192]{1,0:T(8,128)S(1)}, f32[96,192]{1,0:T(8,128)S(1)}, u32[]{:S(2)}, u32[]{:S(2)}) collective-permute-start(f32[96,192]{1,0:T(8,128)S(1)} %get-tuple-element.117), channel_id=1, source_target_pairs={{0,28},{4,0},{8,4},{12,8},{16,12},{20,16},{24,20},{28,24},{1,29},{... | collective-permute-start | bytes 221192 | tf_op jit(solution)/shard_map/ppermute | solution.py:165
  782.8 32.2 %collective-permute-start.24 = (f32[96,576]{1,0:T(8,128)S(1)}, f32[96,576]{1,0:T(8,128)}, u32[]{:S(2)}, u32[]{:S(2)}) collective-permute-start(f32[96,576]{1,0:T(8,128)S(1)} %get-tuple-element.113), channel_id=1, source_target_pairs={{0,12},{4,16},{8,20},{12,24},{16,28},{20,0},{24,4},{28,8},{1,13},{... | collective-permute-start | bytes 663560 | tf_op jit(solution)/shard_map/ppermute | solution.py:165
  796.5 22.6 %collective-permute-start.25 = (f32[96,576]{1,0:T(8,128)S(1)}, f32[96,576]{1,0:T(8,128)}, u32[]{:S(2)}, u32[]{:S(2)}) collective-permute-start(f32[96,576]{1,0:T(8,128)S(1)} %get-tuple-element.112), channel_id=1, source_target_pairs={{0,16},{4,20},{8,24},{12,28},{16,0},{20,4},{24,8},{28,12},{1,17},{... | collective-permute-start | bytes 663560 | tf_op jit(solution)/shard_map/ppermute | solution.py:165
  796.5 22.6 %collective-permute-start.26 = (f32[96,576]{1,0:T(8,128)S(1)}, f32[96,576]{1,0:T(8,128)}, u32[]{:S(2)}, u32[]{:S(2)}) collective-permute-start(f32[96,576]{1,0:T(8,128)S(1)} %get-tuple-element.111), channel_id=1, source_target_pairs={{0,20},{4,24},{8,28},{12,0},{16,4},{20,8},{24,12},{28,16},{1,21},{... | collective-permute-start | bytes 663560 | tf_op jit(solution)/shard_map/ppermute | solution.py:165
  796.5 26.4 %collective-permute-start.27 = (f32[96,576]{1,0:T(8,128)S(1)}, f32[96,576]{1,0:T(8,128)}, u32[]{:S(2)}, u32[]{:S(2)}) collective-permute-start(f32[96,576]{1,0:T(8,128)S(1)} %get-tuple-element.110), channel_id=1, source_target_pairs={{0,24},{4,28},{8,0},{12,4},{16,8},{20,12},{24,16},{28,20},{1,25},{... | collective-permute-start | bytes 663560 | tf_op jit(solution)/shard_map/ppermute | solution.py:165
  797.5 25.4 %collective-permute-start.28 = (f32[96,576]{1,0:T(8,128)S(1)}, f32[96,576]{1,0:T(8,128)}, u32[]{:S(2)}, u32[]{:S(2)}) collective-permute-start(f32[96,576]{1,0:T(8,128)S(1)} %get-tuple-element.109), channel_id=1, source_target_pairs={{0,28},{4,0},{8,4},{12,8},{16,12},{20,16},{24,20},{28,24},{1,29},{... | collective-permute-start | bytes 663560 | tf_op jit(solution)/shard_map/ppermute | solution.py:165
  (58 other events, 969.7 us)
Sparse Core Ops, SparseCore 0:
  46.0 25.2 all-gather.3
  74.1 49.9 all-gather.5
  248.7 62.0 reduce-scatter.3
  396.6 60.2 reduce-scatter.5
  606.9 60.2 reduce-scatter.7

commit v7 on v6

--- a/solution.py
+++ b/solution.py
@@ -126,13 +126,14 @@
 NORM_EPS = 1e-06
 
 
-def feature_whole_sent(blocked):
-    pieces = axis_gather(blocked, "col")
-    return jnp.moveaxis(pieces, 0, 1).reshape(blocked.shape[0], -1)
+def feature_whole(blocked):
+    return lax.all_gather(blocked, "col", axis=1, tiled=True)
 
 
 def feature_sum(partial_rows):
-    return lax.psum_scatter(partial_rows, "col", scatter_dimension=1, tiled=True)
+    return lax.psum_scatter(
+        partial_rows.astype(jnp.bfloat16), "col", scatter_dimension=1, tiled=True
+    ).astype(jnp.float32)
 
 
 def row_totals(first_term, second_term):
@@ -280,7 +281,7 @@
         queries, key_all, value_all, labels, score_scale
     )
     attended = heads_beside(attended_h)
-    attended_full = feature_whole_sent(attended)
+    attended_full = feature_whole(attended)
     vectors_full = axis_gather(jnp.stack([output_bias, attn_gain, attn_shift]), "col")
     output_bias_full, gain_one_full, shift_one_full = (
         vectors_full[:, which].reshape(-1) for which in range(3)
@@ -306,7 +307,7 @@
         out_grad, normed_two, inverse_two, final_gain
     )
     branch_grad = second_grad.astype(jnp.bfloat16)
-    branch_full = feature_whole_sent(branch_grad)
+    branch_full = feature_whole(branch_grad)
     down_partial = weight_partial(branch_full, acted)
     acted_grad = lax.dot_general(
         branch_full, down_complete, (((1,), (1,)), ((), ())), preferred_element_type=jnp.float32
@@ -325,7 +326,7 @@
         hidden_grad, normed_one, inverse_one, attn_gain
     )
     attn_branch_grad = first_grad.astype(jnp.bfloat16)
-    attn_branch_full = feature_whole_sent(attn_branch_grad)
+    attn_branch_full = feature_whole(attn_branch_grad)
     output_weight_grad = weight_grad(attn_branch_full, attended).T
     attended_grad = lax.dot_general(
         attn_branch_full, output_rows, (((1,), (1,)), ((), ())), preferred_element_type=jnp.float32

time: 841 us -> 765 us (0.910)
  waiting for transfers between devices: 400 us -> 342 us
  local copies, waits for them, and re-layouts: 89.1 us -> 74.2 us
  blocking collectives: 30.7 us -> 41.8 us
    ppermute x22 -> x13, waiting for transfers between devices: 137 us -> 53.1 us  [axis_gather(): lax.ppermute(values, axis, [(i, (i + shift) % count) for i in range(count)])]
    all_gather x0 -> x3, waiting for transfers between devices: none -> 72.7 us  [feature_whole(): return lax.all_gather(blocked, 'col', axis=1, tiled=True)]
    reduce_scatter x3, waiting for transfers between devices: 122 us -> 76 us  [feature_sum(): lax.psum_scatter(partial_rows.astype(jnp.bfloat16), 'col', scatter_dimens...]
    gather x6 -> x3, local copies, waits for them, and re-layouts: 17.8 us -> 4.78 us  [axis_gather(): return jnp.stack(arrived)[order]]
    psum x3, blocking collectives: 30.7 us -> 41.8 us  [row_totals(): lax.psum((jnp.sum(first_term, axis=1), jnp.sum(second_term, axis=1)), 'col')]
    ppermute x22 -> x13, starting transfers between devices: 19.9 us -> 14.8 us  [axis_gather(): lax.ppermute(values, axis, [(i, (i + shift) % count) for i in range(count)])]
  transfers between devices with their start and end apart: 55 -> 49, of which waited for: 30 -> 26; matrix products, arithmetic and copies ran while one was open for 12% -> 13% of each run, Pallas kernels for 6% -> 6%
where the time goes in v7:
time: 765 us; the launch traced here: 757 us
  waiting for transfers between devices  342 us (45%)
  Pallas kernels  116 us (15%)
  local copies, waits for them, and re-layouts  74.2 us (10%)
  matrix products  73.8 us (10%)
  starting transfers between devices  50.9 us (7%)
  other arithmetic  43.3 us (6%)
  blocking collectives  41.8 us (5%)
  between operations  15.4 us (2%)
    ppermute x21, waiting for transfers between devices, row_scatter_sum(): lax.ppermute(outgoing, 'row', [(i, (i + shift) % count) for i in range(co...  140 us
    reduce_scatter x3, waiting for transfers between devices, feature_sum(): lax.psum_scatter(partial_rows.astype(jnp.bfloat16), 'col', scatter_dimens...  76 us
    all_gather x3, waiting for transfers between devices, feature_whole(): return lax.all_gather(blocked, 'col', axis=1, tiled=True)  72.7 us
    pallas_call x1, Pallas kernels, attention_backward(): pl.pallas_call(functools.partial(_bwd_kernel, scale), grid=grid, in_specs...  68.9 us
    ppermute x13, waiting for transfers between devices, axis_gather(): lax.ppermute(values, axis, [(i, (i + shift) % count) for i in range(count)])  53.1 us
    pallas_call x1, Pallas kernels, attention_forward(): pl.pallas_call(functools.partial(_fwd_kernel, scale), grid=grid, in_specs...  46.9 us
    psum x3, blocking collectives, row_totals(): lax.psum((jnp.sum(first_term, axis=1), jnp.sum(second_term, axis=1)), 'col')  41.8 us
    ppermute x21, starting transfers between devices, row_scatter_sum(): lax.ppermute(outgoing, 'row', [(i, (i + shift) % count) for i in range(co...  25.5 us
  transfers between devices with their start and end apart: 49, of which 26 were waited for; matrix products, arithmetic and copies ran while one was open for 13% of the time, Pallas kernels for 6%

profile of v7, /device:TPU:12, one launch (start us, length us, event | category | flops | bytes accessed | tf_op | source)
XLA Modules:
  0.0 757.4 jit_solution(14963331758374725861)
XLA Ops:
  16.7 32.3 %collective-permute-done.10 = f32[3,192]{1,0:T(4,128)S(1)} collective-permute-done((f32[3,192]{1,0:T(4,128)S(1)}, f32[3,192]{1,0:T(4,128)S(1)}, u32[]{:S(2)}, u32[]{:S(2)}) %collective-permute-start.10) | collective-permute-done | bytes 2336 | tf_op jit(solution)/shard_map/ppermute | solution.py:188
  59.1 6.1 collective-permute-done.8
  79.2 5.3 collective-permute-done.5
  115.4 4.6 fusion.26
  119.9 46.9 %shard_map.305 = (bf16[3,2048,64]{2,1,0:T(8,128)(2,1)S(1)}, f32[3,2048,1]{2,1,0:T(8,128)}, f32[3,2048,1]{2,1,0:T(8,128)}) custom-call(bf16[3,2048,64]{2,1,0:T(8,128)(2,1)S(1)} %get-tuple-element.144.q_ref, bf16[3,2048,64]{2,1,0:T(8,128)(2,1)S(1)} %bitcast.231, bf16[3,2048,64]{2,1,0:T(8,128)(2,1)} %get-tuple-element.145.v_ref, s32[2048,1]{1,0:T(8,128)S(1)} %copy-done.2, ...), custom_call_target="tpu_custom_call" | custom-call | flops 3221225472 | bytes 3145728 | tf_op jit(solution)/shard_map/pallas_call | solution.py:79
  168.7 4.1 reshape.280
  184.3 14.7 %all-gather.7.cloned.1.call-done = bf16[2048,768]{0,1:T(8,128)(2,1)} async-done(((bf16[2048,192]{0,1:T(8,128)(2,1)}), bf16[2048,768]{0,1:T(8,128)(2,1)}) %all-gather.7.cloned.1.call-update) | async-done | bytes 3145744 | tf_op jit(solution)/shard_map/all_gather | solution.py:130
  199.0 6.8 fusion.62
  209.5 18.0 %multiply_convert_fusion = (bf16[2048,768]{1,0:T(8,128)(2,1)S(1)}, f32[2048,768]{1,0:T(8,128)}, f32[2048,768]{1,0:T(8,128)}) fusion(f32[768]{0:T(1024)S(1)} %copy-done.34, bf16[768,768]{1,0:T(8,128)(2,1)S(1)} %copy-done.14, f32[2048,768]{0,1:T(8,128)S(1)} %get-tuple-element.93), kind=kOutput, calls=%fused_computation.10 | convolution fusion | flops 2521300992 | bytes 23202816 | tf_op jit(solution)/shard_map/dot_general | solution.py:300
  229.2 4.1 convolution_convert_fusion.1
  233.4 38.0 %reduce-scatter.4.cloned.1.call-done = bf16[2048,192]{0,1:T(8,128)(2,1)} async-done(((bf16[2048,768]{0,1:T(8,128)(2,1)}), bf16[2048,192]{0,1:T(8,128)(2,1)}) %reduce-scatter.4.cloned.1.call-update) | async-done | bytes 786448 | tf_op jit(solution)/shard_map/reduce_scatter | solution.py:134
  273.4 21.3 %all-reduce.2 = (f32[2048]{0:T(1024)S(1)}, f32[2048]{0:T(1024)S(1)}) all-reduce(f32[2048]{0:T(1024)S(1)} %get-tuple-element.72, f32[2048]{0:T(1024)S(1)} %get-tuple-element.71), channel_id=1, replica_groups=mesh['row'=8,'col'=4] {'col'}, use_global_device_ids=true, to_apply=%region_6.0 | all-reduce | flops 4096 | bytes 32768 | tf_op jit(solution)/shard_map/psum | solution.py:140
  296.8 10.1 %all-reduce.1 = (f32[2048]{0:T(1024)S(1)}, f32[2048]{0:T(1024)S(1)}) all-reduce(f32[2048]{0:T(1024)S(1)} %get-tuple-element.68, f32[2048]{0:T(1024)S(1)} %get-tuple-element.73), channel_id=1, replica_groups=mesh['row'=8,'col'=4] {'col'}, use_global_device_ids=true, to_apply=%region_10.0 | all-reduce | flops 4096 | bytes 32768 | tf_op jit(solution)/shard_map/psum | solution.py:140
  309.6 29.0 %all-gather.11.cloned.1.call-done = bf16[2048,768]{0,1:T(8,128)(2,1)} async-done(((bf16[2048,192]{0,1:T(8,128)(2,1)}), bf16[2048,768]{0,1:T(8,128)(2,1)}) %all-gather.11.cloned.1.call-update) | async-done | bytes 3145744 | tf_op jit(solution)/shard_map/all_gather | solution.py:130
  338.7 10.9 %convert_reduce_fusion = (f32[768]{0:T(1024)S(1)}, bf16[2048,768]{1,0:T(8,128)(2,1)S(1)}) fusion(f32[2048,768]{1,0:T(8,128)} %get-tuple-element.92, f32[2048,768]{1,0:T(8,128)} %get-tuple-element.143, f32[768]{0:T(1024)S(1)} %copy-done.34, bf16[2048,768]{0,1:T(8,128)(2,1)} %all-gather.11.cloned.1.call-done, bf16[768,768]{0,1:T(8,128)(2,1)} %bitcast.250), kind=kOutput, calls=%fused_computation.8 | convolution fusion | flops 2442657024 | bytes 20060160 | tf_op jit(solution)/shard_map/dot_general | solution.py:312
  351.2 4.0 convolution_convert_fusion
  355.3 38.0 %reduce-scatter.6.cloned.1.call-done = bf16[2048,192]{0,1:T(8,128)(2,1)} async-done(((bf16[2048,768]{0,1:T(8,128)(2,1)}), bf16[2048,192]{0,1:T(8,128)(2,1)}) %reduce-scatter.6.cloned.1.call-update) | async-done | bytes 786448 | tf_op jit(solution)/shard_map/reduce_scatter | solution.py:134
  393.3 4.5 multiply_reduce_fusion.1
  397.7 10.4 %all-reduce = (f32[2048]{0:T(1024)S(1)}, f32[2048]{0:T(1024)S(1)}) all-reduce(f32[2048]{0:T(1024)S(1)} %get-tuple-element.66, f32[2048]{0:T(1024)S(1)} %get-tuple-element.69), channel_id=1, replica_groups=mesh['row'=8,'col'=4] {'col'}, use_global_device_ids=true, to_apply=%region_15.0 | all-reduce | flops 4096 | bytes 32768 | tf_op jit(solution)/shard_map/psum | solution.py:140
  411.4 29.0 %all-gather.13.cloned.1.call-done = bf16[2048,768]{0,1:T(8,128)(2,1)} async-done(((bf16[2048,192]{0,1:T(8,128)(2,1)}), bf16[2048,768]{0,1:T(8,128)(2,1)}) %all-gather.13.cloned.1.call-update) | async-done | bytes 3145744 | tf_op jit(solution)/shard_map/all_gather | solution.py:130
  447.4 68.9 %shard_map.306 = (bf16[3,2048,64]{2,1,0:T(8,128)(2,1)S(1)}, f32[3,2048,64]{2,1,0:T(8,128)}, f32[3,2048,64]{2,1,0:T(8,128)}) custom-call(bf16[3,2048,64]{2,1,0:T(8,128)(2,1)S(1)} %copy-done.1, bf16[3,2048,64]{2,1,0:T(8,128)(2,1)S(1)} %bitcast.232, bf16[3,2048,64]{2,1,0:T(8,128)(2,1)} %get-tuple-element.145.v_ref, bf16[3,2048,64]{2,1,0:T(8,128)(2,1)} %bitcast.248, ...), custom_call_target="tpu_custom_call" | custom-call | flops 8053063680 | bytes 6291456 | tf_op jit(solution)/shard_map/pallas_call | solution.py:107
  524.4 6.2 bitcast_convert_fusion
  530.7 5.6 fusion.72
  536.3 5.9 fusion.28
  544.6 6.1 copy.80
  561.9 8.2 %collective-permute-done.34 = f32[96,1536]{1,0:T(8,128)S(1)} collective-permute-done((f32[96,1536]{1,0:T(8,128)S(1)}, f32[96,1536]{1,0:T(8,128)S(1)}, u32[]{:S(2)}, u32[]{:S(2)}) %collective-permute-start.34) | collective-permute-done | bytes 589856 | tf_op jit(solution)/shard_map/ppermute | solution.py:166
  570.6 62.2 %collective-permute-done.35 = f32[96,1536]{1,0:T(8,128)S(1)} collective-permute-done((f32[96,1536]{1,0:T(8,128)S(1)}, f32[96,1536]{1,0:T(8,128)S(1)}, u32[]{:S(2)}, u32[]{:S(2)}) %collective-permute-start.35) | collective-permute-done | bytes 589856 | tf_op jit(solution)/shard_map/ppermute | solution.py:166
  633.8 11.9 %collective-permute-done.36 = f32[96,1536]{1,0:T(8,128)} collective-permute-done((f32[96,1536]{1,0:T(8,128)}, f32[96,1536]{1,0:T(8,128)}, u32[]{:S(2)}, u32[]{:S(2)}) %collective-permute-start.36) | collective-permute-done | bytes 589856 | tf_op jit(solution)/shard_map/ppermute | solution.py:166
  645.7 11.9 %collective-permute-done.37 = f32[96,1536]{1,0:T(8,128)} collective-permute-done((f32[96,1536]{1,0:T(8,128)}, f32[96,1536]{1,0:T(8,128)}, u32[]{:S(2)}, u32[]{:S(2)}) %collective-permute-start.37) | collective-permute-done | bytes 589856 | tf_op jit(solution)/shard_map/ppermute | solution.py:166
  704.9 13.3 %collective-permute-done.32 = f32[96,192]{1,0:T(8,128)S(1)} collective-permute-done((f32[96,192]{1,0:T(8,128)S(1)}, f32[96,192]{1,0:T(8,128)S(1)}, u32[]{:S(2)}, u32[]{:S(2)}) %collective-permute-start.32) | collective-permute-done | bytes 73760 | tf_op jit(solution)/shard_map/ppermute | solution.py:166
  723.5 13.3 %collective-permute-done.15 = f32[96,576]{1,0:T(8,128)} collective-permute-done((f32[96,576]{1,0:T(8,128)S(1)}, f32[96,576]{1,0:T(8,128)}, u32[]{:S(2)}, u32[]{:S(2)}) %collective-permute-start.15) | collective-permute-done | bytes 221216 | tf_op jit(solution)/shard_map/ppermute | solution.py:166
  736.8 4.1 collective-permute-done.16
  (261 shorter events, 186.4 us)
Async XLA Ops:
  7.2 161.4 %all-gather.15.cloned.1.call-start = ((), (), s32[]{:S(2)}) async-start(), calls=%async_computation.10 | async-start | bytes 2654208 | tf_op jit(solution)/shard_map/all_gather | solution.py:213
  10.5 173.9 %all-gather.9.cloned.1.call-start = ((), (), s32[]{:S(2)}) async-start(), calls=%async_computation.4 | async-start | bytes 1474560 | tf_op jit(solution)/shard_map/all_gather | solution.py:272
  12.5 45.4 %collective-permute-start.7 = (bf16[73728]{0:T(1024)(128)(2,1)S(1)}, bf16[73728]{0:T(1024)(128)(2,1)S(1)}, u32[]{:S(2)}, u32[]{:S(2)}) collective-permute-start(bf16[73728]{0:T(1024)(128)(2,1)S(1)} %constant_dynamic-update-slice_fusion), channel_id=1, source_target_pairs={{0,20},{4,24},{8,28},{12,0},{16,4},{20,8},{24,12},{28,16},{1,21},{... | collective-permute-start | bytes 442376 | tf_op jit(solution)/shard_map/ppermute | solution.py:188
  12.6 86.4 %collective-permute-start = (bf16[192,2048]{1,0:T(8,128)(2,1)}, bf16[192,2048]{1,0:T(8,128)(2,1)}, u32[]{:S(2)}, u32[]{:S(2)}) collective-permute-start(bf16[192,2048]{1,0:T(8,128)(2,1)} %param.18), channel_id=1, source_target_pairs={{0,1},{1,2},{2,3},{3,0},{4,5},{5,6},{6,7},{7,4},{8,9},{9,10},{10,1... | collective-permute-start | bytes 2359304 | tf_op jit(solution)/shard_map/ppermute | solution.py:188
  12.7 86.4 %collective-permute-start.1 = (bf16[192,2048]{1,0:T(8,128)(2,1)}, bf16[192,2048]{1,0:T(8,128)(2,1)}, u32[]{:S(2)}, u32[]{:S(2)}) collective-permute-start(bf16[192,2048]{1,0:T(8,128)(2,1)} %param.18), channel_id=1, source_target_pairs={{0,2},{1,3},{2,0},{3,1},{4,6},{5,7},{6,4},{7,5},{8,10},{9,11},{10,... | collective-permute-start | bytes 2359304 | tf_op jit(solution)/shard_map/ppermute | solution.py:188
  14.5 84.6 %collective-permute-start.2 = (bf16[192,2048]{1,0:T(8,128)(2,1)}, bf16[192,2048]{1,0:T(8,128)(2,1)}, u32[]{:S(2)}, u32[]{:S(2)}) collective-permute-start(bf16[192,2048]{1,0:T(8,128)(2,1)} %param.18), channel_id=1, source_target_pairs={{0,3},{1,0},{2,1},{3,2},{4,7},{5,4},{6,5},{7,6},{8,11},{9,8},{10,9... | collective-permute-start | bytes 2359304 | tf_op jit(solution)/shard_map/ppermute | solution.py:188
  16.7 32.3 %collective-permute-start.10 = (f32[3,192]{1,0:T(4,128)S(1)}, f32[3,192]{1,0:T(4,128)S(1)}, u32[]{:S(2)}, u32[]{:S(2)}) collective-permute-start(f32[3,192]{1,0:T(4,128)S(1)} %get-tuple-element.141), channel_id=1, source_target_pairs={{0,1},{1,2},{2,3},{3,0},{4,5},{5,6},{6,7},{7,4},{8,9},{9,10},{10,1... | collective-permute-start | bytes 6920 | tf_op jit(solution)/shard_map/ppermute | solution.py:188
  98.8 100.3 %all-gather.7.cloned.1.call-start = ((), (), s32[]{:S(2)}) async-start(), calls=%async_computation.3 | async-start | bytes 3932160 | tf_op jit(solution)/shard_map/all_gather | solution.py:130
  168.3 103.1 %reduce-scatter.4.cloned.1.call-start = ((), (), s32[]{:S(2)}) async-start(), calls=%async_computation.5 | async-start | bytes 3932160 | tf_op jit(solution)/shard_map/reduce_scatter | solution.py:134
  233.4 105.3 %all-gather.11.cloned.1.call-start = ((), (), s32[]{:S(2)}) async-start(), calls=%async_computation.6 | async-start | bytes 3932160 | tf_op jit(solution)/shard_map/all_gather | solution.py:130
  309.6 83.7 %reduce-scatter.6.cloned.1.call-start = ((), (), s32[]{:S(2)}) async-start(), calls=%async_computation.7 | async-start | bytes 3932160 | tf_op jit(solution)/shard_map/reduce_scatter | solution.py:134
  355.2 85.2 %all-gather.13.cloned.1.call-start = ((), (), s32[]{:S(2)}) async-start(), calls=%async_computation.8 | async-start | bytes 3932160 | tf_op jit(solution)/shard_map/all_gather | solution.py:130
  411.3 335.7 %reduce-scatter.8.cloned.1.call-start = ((), (), s32[]{:S(2)}) async-start(), calls=%async_computation.9 | async-start | bytes 3932160 | tf_op jit(solution)/shard_map/reduce_scatter | solution.py:134
  554.6 15.5 %collective-permute-start.34 = (f32[96,1536]{1,0:T(8,128)S(1)}, f32[96,1536]{1,0:T(8,128)S(1)}, u32[]{:S(2)}, u32[]{:S(2)}) collective-permute-start(f32[96,1536]{1,0:T(8,128)S(1)} %get-tuple-element.95), channel_id=1, source_target_pairs={{0,4},{4,8},{8,12},{12,16},{16,20},{20,24},{24,28},{28,0},{1,5},{5... | collective-permute-start | bytes 1769480 | tf_op jit(solution)/shard_map/ppermute | solution.py:166
  556.0 76.8 %collective-permute-start.35 = (f32[96,1536]{1,0:T(8,128)S(1)}, f32[96,1536]{1,0:T(8,128)S(1)}, u32[]{:S(2)}, u32[]{:S(2)}) collective-permute-start(f32[96,1536]{1,0:T(8,128)S(1)} %get-tuple-element.101), channel_id=1, source_target_pairs={{0,8},{4,12},{8,16},{12,20},{16,24},{20,28},{24,0},{28,4},{1,9},{5... | collective-permute-start | bytes 1769480 | tf_op jit(solution)/shard_map/ppermute | solution.py:166
  557.5 88.2 %collective-permute-start.36 = (f32[96,1536]{1,0:T(8,128)}, f32[96,1536]{1,0:T(8,128)}, u32[]{:S(2)}, u32[]{:S(2)}) collective-permute-start(f32[96,1536]{1,0:T(8,128)} %get-tuple-element.100), channel_id=1, source_target_pairs={{0,12},{4,16},{8,20},{12,24},{16,28},{20,0},{24,4},{28,8},{1,13},{... | collective-permute-start | bytes 1769480 | tf_op jit(solution)/shard_map/ppermute | solution.py:166
  558.9 98.7 %collective-permute-start.37 = (f32[96,1536]{1,0:T(8,128)}, f32[96,1536]{1,0:T(8,128)}, u32[]{:S(2)}, u32[]{:S(2)}) collective-permute-start(f32[96,1536]{1,0:T(8,128)} %get-tuple-element.99), channel_id=1, source_target_pairs={{0,16},{4,20},{8,24},{12,28},{16,0},{20,4},{24,8},{28,12},{1,17},{... | collective-permute-start | bytes 1769480 | tf_op jit(solution)/shard_map/ppermute | solution.py:166
  560.4 97.2 %collective-permute-start.38 = (f32[96,1536]{1,0:T(8,128)}, f32[96,1536]{1,0:T(8,128)}, u32[]{:S(2)}, u32[]{:S(2)}) collective-permute-start(f32[96,1536]{1,0:T(8,128)} %get-tuple-element.98), channel_id=1, source_target_pairs={{0,20},{4,24},{8,28},{12,0},{16,4},{20,8},{24,12},{28,16},{1,21},{... | collective-permute-start | bytes 1769480 | tf_op jit(solution)/shard_map/ppermute | solution.py:166
  570.0 89.7 %collective-permute-start.39 = (f32[96,1536]{1,0:T(8,128)}, f32[96,1536]{1,0:T(8,128)}, u32[]{:S(2)}, u32[]{:S(2)}) collective-permute-start(f32[96,1536]{1,0:T(8,128)} %get-tuple-element.97), channel_id=1, source_target_pairs={{0,24},{4,28},{8,0},{12,4},{16,8},{20,12},{24,16},{28,20},{1,25},{... | collective-permute-start | bytes 1769480 | tf_op jit(solution)/shard_map/ppermute | solution.py:166
  633.6 27.1 %collective-permute-start.40 = (f32[96,1536]{1,0:T(8,128)S(1)}, f32[96,1536]{1,0:T(8,128)}, u32[]{:S(2)}, u32[]{:S(2)}) collective-permute-start(f32[96,1536]{1,0:T(8,128)S(1)} %get-tuple-element.96), channel_id=1, source_target_pairs={{0,28},{4,0},{8,4},{12,8},{16,12},{20,16},{24,20},{28,24},{1,29},{... | collective-permute-start | bytes 1769480 | tf_op jit(solution)/shard_map/ppermute | solution.py:166
  665.0 16.9 %collective-permute-start.22 = (f32[2304]{0:T(1024)S(1)}, f32[2304]{0:T(1024)S(1)}, u32[]{:S(2)}, u32[]{:S(2)}) collective-permute-start(f32[2304]{0:T(1024)S(1)} %concatenate.18), channel_id=1, source_target_pairs={{0,12},{4,16},{8,20},{12,24},{16,28},{20,0},{24,4},{28,8},{1,13},{... | collective-permute-start | bytes 27656 | tf_op jit(solution)/shard_map/ppermute | solution.py:176
  667.9 15.0 %collective-permute-start.23 = (f32[2304]{0:T(1024)S(1)}, f32[2304]{0:T(1024)S(1)}, u32[]{:S(2)}, u32[]{:S(2)}) collective-permute-start(f32[2304]{0:T(1024)S(1)} %concatenate.18), channel_id=1, source_target_pairs={{0,16},{4,20},{8,24},{12,28},{16,0},{20,4},{24,8},{28,12},{1,17},{... | collective-permute-start | bytes 27656 | tf_op jit(solution)/shard_map/ppermute | solution.py:176
  686.7 17.9 %collective-permute-start.31 = (f32[96,192]{1,0:T(8,128)S(1)}, f32[96,192]{1,0:T(8,128)S(1)}, u32[]{:S(2)}, u32[]{:S(2)}) collective-permute-start(f32[96,192]{1,0:T(8,128)S(1)} %get-tuple-element.119), channel_id=1, source_target_pairs={{0,20},{4,24},{8,28},{12,0},{16,4},{20,8},{24,12},{28,16},{1,21},{... | collective-permute-start | bytes 221192 | tf_op jit(solution)/shard_map/ppermute | solution.py:166
  689.2 29.1 %collective-permute-start.32 = (f32[96,192]{1,0:T(8,128)S(1)}, f32[96,192]{1,0:T(8,128)S(1)}, u32[]{:S(2)}, u32[]{:S(2)}) collective-permute-start(f32[96,192]{1,0:T(8,128)S(1)} %get-tuple-element.118), channel_id=1, source_target_pairs={{0,24},{4,28},{8,0},{12,4},{16,8},{20,12},{24,16},{28,20},{1,25},{... | collective-permute-start | bytes 221192 | tf_op jit(solution)/shard_map/ppermute | solution.py:166
  695.4 22.8 %collective-permute-start.33 = (f32[96,192]{1,0:T(8,128)S(1)}, f32[96,192]{1,0:T(8,128)S(1)}, u32[]{:S(2)}, u32[]{:S(2)}) collective-permute-start(f32[96,192]{1,0:T(8,128)S(1)} %get-tuple-element.117), channel_id=1, source_target_pairs={{0,28},{4,0},{8,4},{12,8},{16,12},{20,16},{24,20},{28,24},{1,29},{... | collective-permute-start | bytes 221192 | tf_op jit(solution)/shard_map/ppermute | solution.py:166
  698.4 19.8 %collective-permute-start.13 = (f32[96,576]{1,0:T(8,128)S(1)}, f32[96,576]{1,0:T(8,128)S(1)}, u32[]{:S(2)}, u32[]{:S(2)}) collective-permute-start(f32[96,576]{1,0:T(8,128)S(1)} %get-tuple-element.108), channel_id=1, source_target_pairs={{0,4},{4,8},{8,12},{12,16},{16,20},{20,24},{24,28},{28,0},{1,5},{5... | collective-permute-start | bytes 663560 | tf_op jit(solution)/shard_map/ppermute | solution.py:166
  700.5 18.8 %collective-permute-start.14 = (f32[96,576]{1,0:T(8,128)S(1)}, f32[96,576]{1,0:T(8,128)S(1)}, u32[]{:S(2)}, u32[]{:S(2)}) collective-permute-start(f32[96,576]{1,0:T(8,128)S(1)} %get-tuple-element.114), channel_id=1, source_target_pairs={{0,8},{4,12},{8,16},{12,20},{16,24},{20,28},{24,0},{28,4},{1,9},{5... | collective-permute-start | bytes 663560 | tf_op jit(solution)/shard_map/ppermute | solution.py:166
  704.6 32.2 %collective-permute-start.15 = (f32[96,576]{1,0:T(8,128)S(1)}, f32[96,576]{1,0:T(8,128)}, u32[]{:S(2)}, u32[]{:S(2)}) collective-permute-start(f32[96,576]{1,0:T(8,128)S(1)} %get-tuple-element.113), channel_id=1, source_target_pairs={{0,12},{4,16},{8,20},{12,24},{16,28},{20,0},{24,4},{28,8},{1,13},{... | collective-permute-start | bytes 663560 | tf_op jit(solution)/shard_map/ppermute | solution.py:166
  718.3 22.6 %collective-permute-start.16 = (f32[96,576]{1,0:T(8,128)S(1)}, f32[96,576]{1,0:T(8,128)}, u32[]{:S(2)}, u32[]{:S(2)}) collective-permute-start(f32[96,576]{1,0:T(8,128)S(1)} %get-tuple-element.112), channel_id=1, source_target_pairs={{0,16},{4,20},{8,24},{12,28},{16,0},{20,4},{24,8},{28,12},{1,17},{... | collective-permute-start | bytes 663560 | tf_op jit(solution)/shard_map/ppermute | solution.py:166
  718.3 22.6 %collective-permute-start.17 = (f32[96,576]{1,0:T(8,128)S(1)}, f32[96,576]{1,0:T(8,128)}, u32[]{:S(2)}, u32[]{:S(2)}) collective-permute-start(f32[96,576]{1,0:T(8,128)S(1)} %get-tuple-element.111), channel_id=1, source_target_pairs={{0,20},{4,24},{8,28},{12,0},{16,4},{20,8},{24,12},{28,16},{1,21},{... | collective-permute-start | bytes 663560 | tf_op jit(solution)/shard_map/ppermute | solution.py:166
  718.3 26.4 %collective-permute-start.18 = (f32[96,576]{1,0:T(8,128)S(1)}, f32[96,576]{1,0:T(8,128)}, u32[]{:S(2)}, u32[]{:S(2)}) collective-permute-start(f32[96,576]{1,0:T(8,128)S(1)} %get-tuple-element.110), channel_id=1, source_target_pairs={{0,24},{4,28},{8,0},{12,4},{16,8},{20,12},{24,16},{28,20},{1,25},{... | collective-permute-start | bytes 663560 | tf_op jit(solution)/shard_map/ppermute | solution.py:166
  719.3 25.4 %collective-permute-start.19 = (f32[96,576]{1,0:T(8,128)S(1)}, f32[96,576]{1,0:T(8,128)}, u32[]{:S(2)}, u32[]{:S(2)}) collective-permute-start(f32[96,576]{1,0:T(8,128)S(1)} %get-tuple-element.109), channel_id=1, source_target_pairs={{0,28},{4,0},{8,4},{12,8},{16,12},{20,16},{24,20},{28,24},{1,29},{... | collective-permute-start | bytes 663560 | tf_op jit(solution)/shard_map/ppermute | solution.py:166
  (55 other events, 1012.8 us)
Sparse Core Ops, SparseCore 0:
  10.8 55.9 all-gather.14
  98.9 19.5 all-gather.8
  168.4 30.5 all-gather.6
  233.5 37.8 reduce-scatter.3
  309.7 28.8 all-gather.10
  355.3 37.8 reduce-scatter.5
  411.5 28.9 all-gather.12
  530.8 37.8 reduce-scatter.7

commit v8 on v7

--- a/solution.py
+++ b/solution.py
@@ -194,14 +194,6 @@
 def weight_partial(gathered, local_grad):
     return lax.dot_general(
         gathered, local_grad, (((0,), (0,)), ((), ())), preferred_element_type=jnp.float32
-    )
-
-
-def weight_grad(gathered, local_grad):
-    return row_scatter_sum(
-        lax.dot_general(
-            gathered, local_grad, (((0,), (0,)), ((), ())), preferred_element_type=jnp.float32
-        )
     )
 
 
@@ -314,9 +306,6 @@
     )
     upped_grad = gelu_pull(acted_grad)[0].astype(jnp.bfloat16)
     up_partial = weight_partial(hidden_full, upped_grad)
-    ffn_grads = row_scatter_sum(jnp.concatenate([down_partial, up_partial], axis=1))
-    down_weight_grad = ffn_grads[:, : down_partial.shape[1]].T
-    up_weight_grad = ffn_grads[:, down_partial.shape[1] :]
     hidden_grad = second_grad + feature_sum(
         lax.dot_general(
             upped_grad, up_complete, (((1,), (1,)), ((), ())), preferred_element_type=jnp.float32
@@ -327,7 +316,15 @@
     )
     attn_branch_grad = first_grad.astype(jnp.bfloat16)
     attn_branch_full = feature_whole(attn_branch_grad)
-    output_weight_grad = weight_grad(attn_branch_full, attended).T
+    output_partial = weight_partial(attn_branch_full, attended)
+    early_grads = row_scatter_sum(
+        jnp.concatenate([down_partial, up_partial, output_partial], axis=1)
+    )
+    down_end = down_partial.shape[1]
+    up_end = down_end + up_partial.shape[1]
+    down_weight_grad = early_grads[:, :down_end].T
+    up_weight_grad = early_grads[:, down_end:up_end]
+    output_weight_grad = early_grads[:, up_end:].T
     attended_grad = lax.dot_general(
         attn_branch_full, output_rows, (((1,), (1,)), ((), ())), preferred_element_type=jnp.float32
     ).astype(jnp.bfloat16)
@@ -345,7 +342,7 @@
     key_grad = heads_beside(key_grad_h).astype(jnp.bfloat16)
     value_grad = heads_beside(value_grad_h).astype(jnp.bfloat16)
     column_count = query_weight.shape[1]
-    qkv_grads = weight_grad(
+    qkv_partial = weight_partial(
         inputs_full, jnp.concatenate([query_grad, key_grad, value_grad], axis=1)
     )
     input_grad = first_grad + feature_sum(
@@ -367,7 +364,21 @@
         final_gain_grad,
         final_shift_grad,
     )
-    param_flat = row_sum(jnp.concatenate(param_parts))
+    param_flat = jnp.concatenate(param_parts)
+    row_count = lax.axis_size("row")
+    width = qkv_partial.shape[1]
+    if param_flat.shape[0] % width == 0:
+        extra_rows = param_flat.shape[0] // width
+        blocks = qkv_partial.reshape(row_count, -1, width)
+        extra = jnp.broadcast_to(
+            param_flat.reshape(1, extra_rows, width), (row_count, extra_rows, width)
+        )
+        summed = row_scatter_sum(jnp.concatenate([blocks, extra], axis=1).reshape(-1, width))
+        qkv_grads = summed[:-extra_rows]
+        param_flat = summed[-extra_rows:].reshape(-1)
+    else:
+        qkv_grads = row_scatter_sum(qkv_partial)
+        param_flat = row_sum(param_flat)
     param_totals = []
     offset = 0
     for part in param_parts:

time: 765 us -> 764 us (level)
  waiting for transfers between devices: 342 us -> 370 us
  starting transfers between devices: 50.9 us -> 29.9 us
  blocking collectives: 41.8 us -> 31.1 us
    ppermute x21 -> x14, waiting for transfers between devices: 140 us -> 169 us  [row_scatter_sum(): lax.ppermute(outgoing, 'row', [(i, (i + shift) % count) for i in range(co...]
    ppermute x21 -> x14, starting transfers between devices: 25.5 us -> 13.4 us  [row_scatter_sum(): lax.ppermute(outgoing, 'row', [(i, (i + shift) % count) for i in range(co...]
    psum x3, blocking collectives: 41.8 us -> 31.1 us  [row_totals(): lax.psum((jnp.sum(first_term, axis=1), jnp.sum(second_term, axis=1)), 'col')]
    ppermute x7 -> x0, starting transfers between devices: 9.68 us -> none  [row_sum(): lax.ppermute(values, 'row', [(i, (i + shift) % count) for i in range(coun...]
    dot_general x2 -> x4, matrix products: 11.5 us -> 18.7 us  [weight_partial(): lax.dot_general(gathered, local_grad, (((0,), (0,)), ((), ())), preferred...]
  transfers between devices with their start and end apart: 49 -> 35, of which waited for: 26 -> 22; matrix products, arithmetic and copies ran while one was open for 13% -> 13% of each run, Pallas kernels for 6% -> 6%
where the time goes in v8:
time: 764 us; the launch traced here: 754 us
  waiting for transfers between devices  370 us (48%)
  Pallas kernels  116 us (15%)
  matrix products  75.2 us (10%)
  local copies, waits for them, and re-layouts  72.2 us (9%)
  other arithmetic  45.1 us (6%)
  blocking collectives  31.1 us (4%)
  starting transfers between devices  29.9 us (4%)
  between operations  15.3 us (2%)
    ppermute x14, waiting for transfers between devices, row_scatter_sum(): lax.ppermute(outgoing, 'row', [(i, (i + shift) % count) for i in range(co...  169 us
    reduce_scatter x3, waiting for transfers between devices, feature_sum(): lax.psum_scatter(partial_rows.astype(jnp.bfloat16), 'col', scatter_dimens...  76 us
    all_gather x3, waiting for transfers between devices, feature_whole(): return lax.all_gather(blocked, 'col', axis=1, tiled=True)  72.5 us
    pallas_call x1, Pallas kernels, attention_backward(): pl.pallas_call(functools.partial(_bwd_kernel, scale), grid=grid, in_specs...  68.9 us
    ppermute x13, waiting for transfers between devices, axis_gather(): lax.ppermute(values, axis, [(i, (i + shift) % count) for i in range(count)])  52.5 us
    pallas_call x1, Pallas kernels, attention_forward(): pl.pallas_call(functools.partial(_fwd_kernel, scale), grid=grid, in_specs...  46.9 us
    psum x3, blocking collectives, row_totals(): lax.psum((jnp.sum(first_term, axis=1), jnp.sum(second_term, axis=1)), 'col')  31.1 us
    dot_general x4, matrix products, weight_partial(): lax.dot_general(gathered, local_grad, (((0,), (0,)), ((), ())), preferred...  18.7 us
  transfers between devices with their start and end apart: 35, of which 22 were waited for; matrix products, arithmetic and copies ran while one was open for 13% of the time, Pallas kernels for 6%

profile of v8, /device:TPU:12, one launch (start us, length us, event | category | flops | bytes accessed | tf_op | source)
XLA Modules:
  0.0 754.5 jit_solution(4362054273876560845)
XLA Ops:
  16.7 32.3 %collective-permute-done.10 = f32[3,192]{1,0:T(4,128)S(1)} collective-permute-done((f32[3,192]{1,0:T(4,128)S(1)}, f32[3,192]{1,0:T(4,128)S(1)}, u32[]{:S(2)}, u32[]{:S(2)}) %collective-permute-start.10) | collective-permute-done | bytes 2336 | tf_op jit(solution)/shard_map/ppermute | solution.py:188
  59.1 6.1 collective-permute-done.8
  79.8 4.7 collective-permute-done.5
  115.4 4.6 fusion.26
  120.0 46.9 %shard_map.305 = (bf16[3,2048,64]{2,1,0:T(8,128)(2,1)S(1)}, f32[3,2048,1]{2,1,0:T(8,128)}, f32[3,2048,1]{2,1,0:T(8,128)}) custom-call(bf16[3,2048,64]{2,1,0:T(8,128)(2,1)S(1)} %get-tuple-element.153.q_ref, bf16[3,2048,64]{2,1,0:T(8,128)(2,1)S(1)} %bitcast.198, bf16[3,2048,64]{2,1,0:T(8,128)(2,1)} %get-tuple-element.154.v_ref, s32[2048,1]{1,0:T(8,128)S(1)} %copy-done.2, ...), custom_call_target="tpu_custom_call" | custom-call | flops 3221225472 | bytes 3145728 | tf_op jit(solution)/shard_map/pallas_call | solution.py:79
  168.9 4.1 reshape.284
  184.5 14.6 %all-gather.7.cloned.1.call-done = bf16[2048,768]{0,1:T(8,128)(2,1)} async-done(((bf16[2048,192]{0,1:T(8,128)(2,1)}), bf16[2048,768]{0,1:T(8,128)(2,1)}) %all-gather.7.cloned.1.call-update) | async-done | bytes 3145744 | tf_op jit(solution)/shard_map/all_gather | solution.py:130
  199.1 6.8 fusion.72
  209.6 18.0 %multiply_convert_fusion = (bf16[2048,768]{1,0:T(8,128)(2,1)S(1)}, f32[2048,768]{1,0:T(8,128)}, f32[2048,768]{1,0:T(8,128)}) fusion(f32[768]{0:T(1024)S(1)} %copy-done.34, bf16[768,768]{1,0:T(8,128)(2,1)S(1)} %copy-done.14, f32[2048,768]{0,1:T(8,128)S(1)} %get-tuple-element.110), kind=kOutput, calls=%fused_computation.18 | convolution fusion | flops 2521300992 | bytes 23202816 | tf_op jit(solution)/shard_map/dot_general | solution.py:292
  233.4 38.0 %reduce-scatter.4.cloned.1.call-done = bf16[2048,192]{0,1:T(8,128)(2,1)} async-done(((bf16[2048,768]{0,1:T(8,128)(2,1)}), bf16[2048,192]{0,1:T(8,128)(2,1)}) %reduce-scatter.4.cloned.1.call-update) | async-done | bytes 786448 | tf_op jit(solution)/shard_map/reduce_scatter | solution.py:134
  273.4 10.5 %all-reduce.2 = (f32[2048]{0:T(1024)S(1)}, f32[2048]{0:T(1024)S(1)}) all-reduce(f32[2048]{0:T(1024)S(1)} %get-tuple-element.89, f32[2048]{0:T(1024)S(1)} %get-tuple-element.88), channel_id=1, replica_groups=mesh['row'=8,'col'=4] {'col'}, use_global_device_ids=true, to_apply=%region_6.0 | all-reduce | flops 4096 | bytes 32768 | tf_op jit(solution)/shard_map/psum | solution.py:140
  286.0 10.1 %all-reduce.1 = (f32[2048]{0:T(1024)S(1)}, f32[2048]{0:T(1024)S(1)}) all-reduce(f32[2048]{0:T(1024)S(1)} %get-tuple-element.85, f32[2048]{0:T(1024)S(1)} %get-tuple-element.90), channel_id=1, replica_groups=mesh['row'=8,'col'=4] {'col'}, use_global_device_ids=true, to_apply=%region_10.0 | all-reduce | flops 4096 | bytes 32768 | tf_op jit(solution)/shard_map/psum | solution.py:140
  298.9 29.1 %all-gather.11.cloned.1.call-done = bf16[2048,768]{0,1:T(8,128)(2,1)} async-done(((bf16[2048,192]{0,1:T(8,128)(2,1)}), bf16[2048,768]{0,1:T(8,128)(2,1)}) %all-gather.11.cloned.1.call-update) | async-done | bytes 3145744 | tf_op jit(solution)/shard_map/all_gather | solution.py:130
  327.9 10.9 %convert_reduce_fusion = (f32[768]{0:T(1024)S(1)}, bf16[2048,768]{1,0:T(8,128)(2,1)S(1)}) fusion(f32[2048,768]{1,0:T(8,128)} %get-tuple-element.109, f32[2048,768]{1,0:T(8,128)} %get-tuple-element.152, f32[768]{0:T(1024)S(1)} %copy-done.34, bf16[2048,768]{0,1:T(8,128)(2,1)} %all-gather.11.cloned.1.call-done, bf16[768,768]{0,1:T(8,128)(2,1)} %bitcast.218), kind=kOutput, calls=%fused_computation.16 | convolution fusion | flops 2442657024 | bytes 20060160 | tf_op jit(solution)/shard_map/dot_general | solution.py:304
  340.5 4.1 convolution_convert_fusion
  344.7 38.0 %reduce-scatter.6.cloned.1.call-done = bf16[2048,192]{0,1:T(8,128)(2,1)} async-done(((bf16[2048,768]{0,1:T(8,128)(2,1)}), bf16[2048,192]{0,1:T(8,128)(2,1)}) %reduce-scatter.6.cloned.1.call-update) | async-done | bytes 786448 | tf_op jit(solution)/shard_map/reduce_scatter | solution.py:134
  382.7 4.5 multiply_reduce_fusion.1
  387.1 10.4 %all-reduce = (f32[2048]{0:T(1024)S(1)}, f32[2048]{0:T(1024)S(1)}) all-reduce(f32[2048]{0:T(1024)S(1)} %get-tuple-element.83, f32[2048]{0:T(1024)S(1)} %get-tuple-element.86), channel_id=1, replica_groups=mesh['row'=8,'col'=4] {'col'}, use_global_device_ids=true, to_apply=%region_15.0 | all-reduce | flops 4096 | bytes 32768 | tf_op jit(solution)/shard_map/psum | solution.py:140
  401.0 28.8 %all-gather.13.cloned.1.call-done = bf16[2048,768]{0,1:T(8,128)(2,1)} async-done(((bf16[2048,192]{0,1:T(8,128)(2,1)}), bf16[2048,768]{0,1:T(8,128)(2,1)}) %all-gather.13.cloned.1.call-update) | async-done | bytes 3145744 | tf_op jit(solution)/shard_map/all_gather | solution.py:130
  436.8 68.9 %shard_map.306 = (bf16[3,2048,64]{2,1,0:T(8,128)(2,1)S(1)}, f32[3,2048,64]{2,1,0:T(8,128)}, f32[3,2048,64]{2,1,0:T(8,128)}) custom-call(bf16[3,2048,64]{2,1,0:T(8,128)(2,1)S(1)} %copy-done.1, bf16[3,2048,64]{2,1,0:T(8,128)(2,1)S(1)} %bitcast.199, bf16[3,2048,64]{2,1,0:T(8,128)(2,1)} %get-tuple-element.154.v_ref, bf16[3,2048,64]{2,1,0:T(8,128)(2,1)} %bitcast.216, ...), custom_call_target="tpu_custom_call" | custom-call | flops 8053063680 | bytes 6291456 | tf_op jit(solution)/shard_map/pallas_call | solution.py:107
  513.6 6.2 bitcast_convert_fusion
  521.2 5.6 fusion.81
  526.8 6.5 fusion.28
  537.2 6.7 copy.81
  544.6 5.4 fusion.12
  562.6 54.5 %collective-permute-done.14 = f32[100,576]{1,0:T(8,128)S(1)} collective-permute-done((f32[100,576]{1,0:T(8,128)S(1)}, f32[100,576]{1,0:T(8,128)S(1)}, u32[]{:S(2)}, u32[]{:S(2)}) %collective-permute-start.14) | collective-permute-done | bytes 230432 | tf_op jit(solution)/shard_map/ppermute | solution.py:166
  617.1 5.8 collective-permute-done.15
  623.7 4.2 collective-permute-done.16
  631.5 16.7 %collective-permute-done.19 = f32[100,576]{1,0:T(8,128)} collective-permute-done((f32[100,576]{1,0:T(8,128)}, f32[100,576]{1,0:T(8,128)}, u32[]{:S(2)}, u32[]{:S(2)}) %collective-permute-start.19) | collective-permute-done | bytes 230432 | tf_op jit(solution)/shard_map/ppermute | solution.py:166
  654.4 48.8 %collective-permute-done.22 = f32[96,1728]{1,0:T(8,128)} collective-permute-done((f32[96,1728]{1,0:T(8,128)}, f32[96,1728]{1,0:T(8,128)}, u32[]{:S(2)}, u32[]{:S(2)}) %collective-permute-start.22) | collective-permute-done | bytes 663584 | tf_op jit(solution)/shard_map/ppermute | solution.py:166
  703.2 13.2 %collective-permute-done.23 = f32[96,1728]{1,0:T(8,128)} collective-permute-done((f32[96,1728]{1,0:T(8,128)}, f32[96,1728]{1,0:T(8,128)}, u32[]{:S(2)}, u32[]{:S(2)}) %collective-permute-start.23) | collective-permute-done | bytes 663584 | tf_op jit(solution)/shard_map/ppermute | solution.py:166
  720.3 19.5 %collective-permute-done.26 = f32[96,1728]{1,0:T(8,128)} collective-permute-done((f32[96,1728]{1,0:T(8,128)}, f32[96,1728]{1,0:T(8,128)}, u32[]{:S(2)}, u32[]{:S(2)}) %collective-permute-start.26) | collective-permute-done | bytes 663584 | tf_op jit(solution)/shard_map/ppermute | solution.py:166
  (241 shorter events, 154.6 us)
Async XLA Ops:
  7.2 161.6 %all-gather.15.cloned.1.call-start = ((), (), s32[]{:S(2)}) async-start(), calls=%async_computation.10 | async-start | bytes 2654208 | tf_op jit(solution)/shard_map/all_gather | solution.py:205
  10.5 174.1 %all-gather.9.cloned.1.call-start = ((), (), s32[]{:S(2)}) async-start(), calls=%async_computation.4 | async-start | bytes 1474560 | tf_op jit(solution)/shard_map/all_gather | solution.py:264
  12.5 45.4 %collective-permute-start.7 = (bf16[73728]{0:T(1024)(128)(2,1)S(1)}, bf16[73728]{0:T(1024)(128)(2,1)S(1)}, u32[]{:S(2)}, u32[]{:S(2)}) collective-permute-start(bf16[73728]{0:T(1024)(128)(2,1)S(1)} %constant_dynamic-update-slice_fusion), channel_id=1, source_target_pairs={{0,20},{4,24},{8,28},{12,0},{16,4},{20,8},{24,12},{28,16},{1,21},{... | collective-permute-start | bytes 442376 | tf_op jit(solution)/shard_map/ppermute | solution.py:188
  12.6 86.4 %collective-permute-start = (bf16[192,2048]{1,0:T(8,128)(2,1)}, bf16[192,2048]{1,0:T(8,128)(2,1)}, u32[]{:S(2)}, u32[]{:S(2)}) collective-permute-start(bf16[192,2048]{1,0:T(8,128)(2,1)} %param.18), channel_id=1, source_target_pairs={{0,1},{1,2},{2,3},{3,0},{4,5},{5,6},{6,7},{7,4},{8,9},{9,10},{10,1... | collective-permute-start | bytes 2359304 | tf_op jit(solution)/shard_map/ppermute | solution.py:188
  12.7 86.3 %collective-permute-start.1 = (bf16[192,2048]{1,0:T(8,128)(2,1)}, bf16[192,2048]{1,0:T(8,128)(2,1)}, u32[]{:S(2)}, u32[]{:S(2)}) collective-permute-start(bf16[192,2048]{1,0:T(8,128)(2,1)} %param.18), channel_id=1, source_target_pairs={{0,2},{1,3},{2,0},{3,1},{4,6},{5,7},{6,4},{7,5},{8,10},{9,11},{10,... | collective-permute-start | bytes 2359304 | tf_op jit(solution)/shard_map/ppermute | solution.py:188
  14.5 84.5 %collective-permute-start.2 = (bf16[192,2048]{1,0:T(8,128)(2,1)}, bf16[192,2048]{1,0:T(8,128)(2,1)}, u32[]{:S(2)}, u32[]{:S(2)}) collective-permute-start(bf16[192,2048]{1,0:T(8,128)(2,1)} %param.18), channel_id=1, source_target_pairs={{0,3},{1,0},{2,1},{3,2},{4,7},{5,4},{6,5},{7,6},{8,11},{9,8},{10,9... | collective-permute-start | bytes 2359304 | tf_op jit(solution)/shard_map/ppermute | solution.py:188
  16.7 32.3 %collective-permute-start.10 = (f32[3,192]{1,0:T(4,128)S(1)}, f32[3,192]{1,0:T(4,128)S(1)}, u32[]{:S(2)}, u32[]{:S(2)}) collective-permute-start(f32[3,192]{1,0:T(4,128)S(1)} %get-tuple-element.150), channel_id=1, source_target_pairs={{0,1},{1,2},{2,3},{3,0},{4,5},{5,6},{6,7},{7,4},{8,9},{9,10},{10,1... | collective-permute-start | bytes 6920 | tf_op jit(solution)/shard_map/ppermute | solution.py:188
  53.9 11.2 %collective-permute-start.8 = (bf16[73728]{0:T(1024)(128)(2,1)S(1)}, bf16[73728]{0:T(1024)(128)(2,1)S(1)}, u32[]{:S(2)}, u32[]{:S(2)}) collective-permute-start(bf16[73728]{0:T(1024)(128)(2,1)S(1)} %constant_dynamic-update-slice_fusion), channel_id=1, source_target_pairs={{0,24},{4,28},{8,0},{12,4},{16,8},{20,12},{24,16},{28,20},{1,25},{... | collective-permute-start | bytes 442376 | tf_op jit(solution)/shard_map/ppermute | solution.py:188
  58.0 11.7 %collective-permute-start.9 = (bf16[73728]{0:T(1024)(128)(2,1)S(1)}, bf16[73728]{0:T(1024)(128)(2,1)S(1)}, u32[]{:S(2)}, u32[]{:S(2)}) collective-permute-start(bf16[73728]{0:T(1024)(128)(2,1)S(1)} %constant_dynamic-update-slice_fusion), channel_id=1, source_target_pairs={{0,28},{4,0},{8,4},{12,8},{16,12},{20,16},{24,20},{28,24},{1,29},{... | collective-permute-start | bytes 442376 | tf_op jit(solution)/shard_map/ppermute | solution.py:188
  65.2 8.2 %collective-permute-start.3 = (bf16[73728]{0:T(1024)(128)(2,1)S(1)}, bf16[73728]{0:T(1024)(128)(2,1)S(1)}, u32[]{:S(2)}, u32[]{:S(2)}) collective-permute-start(bf16[73728]{0:T(1024)(128)(2,1)S(1)} %constant_dynamic-update-slice_fusion), channel_id=1, source_target_pairs={{0,4},{4,8},{8,12},{12,16},{16,20},{20,24},{24,28},{28,0},{1,5},{5... | collective-permute-start | bytes 442376 | tf_op jit(solution)/shard_map/ppermute | solution.py:188
  73.4 11.1 %collective-permute-start.5 = (bf16[73728]{0:T(1024)(128)(2,1)S(1)}, bf16[73728]{0:T(1024)(128)(2,1)S(1)}, u32[]{:S(2)}, u32[]{:S(2)}) collective-permute-start(bf16[73728]{0:T(1024)(128)(2,1)S(1)} %constant_dynamic-update-slice_fusion), channel_id=1, source_target_pairs={{0,12},{4,16},{8,20},{12,24},{16,28},{20,0},{24,4},{28,8},{1,13},{... | collective-permute-start | bytes 442376 | tf_op jit(solution)/shard_map/ppermute | solution.py:188
  75.5 11.6 %collective-permute-start.6 = (bf16[73728]{0:T(1024)(128)(2,1)S(1)}, bf16[73728]{0:T(1024)(128)(2,1)S(1)}, u32[]{:S(2)}, u32[]{:S(2)}) collective-permute-start(bf16[73728]{0:T(1024)(128)(2,1)S(1)} %constant_dynamic-update-slice_fusion), channel_id=1, source_target_pairs={{0,16},{4,20},{8,24},{12,28},{16,0},{20,4},{24,8},{28,12},{1,17},{... | collective-permute-start | bytes 442376 | tf_op jit(solution)/shard_map/ppermute | solution.py:188
  98.7 100.4 %all-gather.7.cloned.1.call-start = ((), (), s32[]{:S(2)}) async-start(), calls=%async_computation.3 | async-start | bytes 3932160 | tf_op jit(solution)/shard_map/all_gather | solution.py:130
  168.4 103.0 %reduce-scatter.4.cloned.1.call-start = ((), (), s32[]{:S(2)}) async-start(), calls=%async_computation.5 | async-start | bytes 3932160 | tf_op jit(solution)/shard_map/reduce_scatter | solution.py:134
  233.3 94.6 %all-gather.11.cloned.1.call-start = ((), (), s32[]{:S(2)}) async-start(), calls=%async_computation.6 | async-start | bytes 3932160 | tf_op jit(solution)/shard_map/all_gather | solution.py:130
  298.8 83.8 %reduce-scatter.6.cloned.1.call-start = ((), (), s32[]{:S(2)}) async-start(), calls=%async_computation.7 | async-start | bytes 3932160 | tf_op jit(solution)/shard_map/reduce_scatter | solution.py:134
  344.6 85.3 %all-gather.13.cloned.1.call-start = ((), (), s32[]{:S(2)}) async-start(), calls=%async_computation.8 | async-start | bytes 3932160 | tf_op jit(solution)/shard_map/all_gather | solution.py:130
  400.8 343.3 %reduce-scatter.8.cloned.1.call-start = ((), (), s32[]{:S(2)}) async-start(), calls=%async_computation.9 | async-start | bytes 3932160 | tf_op jit(solution)/shard_map/reduce_scatter | solution.py:134
  551.0 9.7 %collective-permute-start.13 = (f32[100,576]{1,0:T(8,128)S(1)}, f32[100,576]{1,0:T(8,128)S(1)}, u32[]{:S(2)}, u32[]{:S(2)}) collective-permute-start(f32[100,576]{1,0:T(8,128)S(1)} %get-tuple-element.125), channel_id=1, source_target_pairs={{0,4},{4,8},{8,12},{12,16},{16,20},{20,24},{24,28},{28,0},{1,5},{5... | collective-permute-start | bytes 691208 | tf_op jit(solution)/shard_map/ppermute | solution.py:166
  554.8 93.5 %collective-permute-start.20 = (f32[96,1728]{1,0:T(8,128)}, f32[96,1728]{1,0:T(8,128)S(1)}, u32[]{:S(2)}, u32[]{:S(2)}) collective-permute-start(f32[96,1728]{1,0:T(8,128)} %get-tuple-element.112), channel_id=1, source_target_pairs={{0,4},{4,8},{8,12},{12,16},{16,20},{20,24},{24,28},{28,0},{1,5},{5... | collective-permute-start | bytes 1990664 | tf_op jit(solution)/shard_map/ppermute | solution.py:166
  556.2 92.0 %collective-permute-start.21 = (f32[96,1728]{1,0:T(8,128)}, f32[96,1728]{1,0:T(8,128)}, u32[]{:S(2)}, u32[]{:S(2)}) collective-permute-start(f32[96,1728]{1,0:T(8,128)} %get-tuple-element.118), channel_id=1, source_target_pairs={{0,8},{4,12},{8,16},{12,20},{16,24},{20,28},{24,0},{28,4},{1,9},{5... | collective-permute-start | bytes 1990664 | tf_op jit(solution)/shard_map/ppermute | solution.py:166
  557.7 59.4 %collective-permute-start.14 = (f32[100,576]{1,0:T(8,128)S(1)}, f32[100,576]{1,0:T(8,128)S(1)}, u32[]{:S(2)}, u32[]{:S(2)}) collective-permute-start(f32[100,576]{1,0:T(8,128)S(1)} %get-tuple-element.126), channel_id=1, source_target_pairs={{0,8},{4,12},{8,16},{12,20},{16,24},{20,28},{24,0},{28,4},{1,9},{5... | collective-permute-start | bytes 691208 | tf_op jit(solution)/shard_map/ppermute | solution.py:166
  558.2 64.7 %collective-permute-start.15 = (f32[100,576]{1,0:T(8,128)S(1)}, f32[100,576]{1,0:T(8,128)S(1)}, u32[]{:S(2)}, u32[]{:S(2)}) collective-permute-start(f32[100,576]{1,0:T(8,128)S(1)} %get-tuple-element.127), channel_id=1, source_target_pairs={{0,12},{4,16},{8,20},{12,24},{16,28},{20,0},{24,4},{28,8},{1,13},{... | collective-permute-start | bytes 691208 | tf_op jit(solution)/shard_map/ppermute | solution.py:166
  560.6 67.3 %collective-permute-start.16 = (f32[100,576]{1,0:T(8,128)S(1)}, f32[100,576]{1,0:T(8,128)}, u32[]{:S(2)}, u32[]{:S(2)}) collective-permute-start(f32[100,576]{1,0:T(8,128)S(1)} %get-tuple-element.128), channel_id=1, source_target_pairs={{0,16},{4,20},{8,24},{12,28},{16,0},{20,4},{24,8},{28,12},{1,17},{... | collective-permute-start | bytes 691208 | tf_op jit(solution)/shard_map/ppermute | solution.py:166
  617.1 10.8 %collective-permute-start.17 = (f32[100,576]{1,0:T(8,128)}, f32[100,576]{1,0:T(8,128)}, u32[]{:S(2)}, u32[]{:S(2)}) collective-permute-start(f32[100,576]{1,0:T(8,128)} %get-tuple-element.129), channel_id=1, source_target_pairs={{0,20},{4,24},{8,28},{12,0},{16,4},{20,8},{24,12},{28,16},{1,21},{... | collective-permute-start | bytes 691208 | tf_op jit(solution)/shard_map/ppermute | solution.py:166
  623.0 7.2 collective-permute-start.18
  627.9 20.3 %collective-permute-start.19 = (f32[100,576]{1,0:T(8,128)}, f32[100,576]{1,0:T(8,128)}, u32[]{:S(2)}, u32[]{:S(2)}) collective-permute-start(f32[100,576]{1,0:T(8,128)} %fusion.62), channel_id=1, source_target_pairs={{0,28},{4,0},{8,4},{12,8},{16,12},{20,16},{24,20},{28,24},{1,29},{... | collective-permute-start | bytes 691208 | tf_op jit(solution)/shard_map/ppermute | solution.py:166
  627.9 75.3 %collective-permute-start.22 = (f32[96,1728]{1,0:T(8,128)}, f32[96,1728]{1,0:T(8,128)}, u32[]{:S(2)}, u32[]{:S(2)}) collective-permute-start(f32[96,1728]{1,0:T(8,128)} %get-tuple-element.117), channel_id=1, source_target_pairs={{0,12},{4,16},{8,20},{12,24},{16,28},{20,0},{24,4},{28,8},{1,13},{... | collective-permute-start | bytes 1990664 | tf_op jit(solution)/shard_map/ppermute | solution.py:166
  630.1 86.3 %collective-permute-start.23 = (f32[96,1728]{1,0:T(8,128)}, f32[96,1728]{1,0:T(8,128)}, u32[]{:S(2)}, u32[]{:S(2)}) collective-permute-start(f32[96,1728]{1,0:T(8,128)} %get-tuple-element.116), channel_id=1, source_target_pairs={{0,16},{4,20},{8,24},{12,28},{16,0},{20,4},{24,8},{28,12},{1,17},{... | collective-permute-start | bytes 1990664 | tf_op jit(solution)/shard_map/ppermute | solution.py:166
  648.3 68.2 %collective-permute-start.24 = (f32[96,1728]{1,0:T(8,128)}, f32[96,1728]{1,0:T(8,128)}, u32[]{:S(2)}, u32[]{:S(2)}) collective-permute-start(f32[96,1728]{1,0:T(8,128)} %get-tuple-element.115), channel_id=1, source_target_pairs={{0,20},{4,24},{8,28},{12,0},{16,4},{20,8},{24,12},{28,16},{1,21},{... | collective-permute-start | bytes 1990664 | tf_op jit(solution)/shard_map/ppermute | solution.py:166
  648.3 72.1 %collective-permute-start.25 = (f32[96,1728]{1,0:T(8,128)}, f32[96,1728]{1,0:T(8,128)}, u32[]{:S(2)}, u32[]{:S(2)}) collective-permute-start(f32[96,1728]{1,0:T(8,128)} %get-tuple-element.114), channel_id=1, source_target_pairs={{0,24},{4,28},{8,0},{12,4},{16,8},{20,12},{24,16},{28,20},{1,25},{... | collective-permute-start | bytes 1990664 | tf_op jit(solution)/shard_map/ppermute | solution.py:166
  648.3 91.5 %collective-permute-start.26 = (f32[96,1728]{1,0:T(8,128)}, f32[96,1728]{1,0:T(8,128)}, u32[]{:S(2)}, u32[]{:S(2)}) collective-permute-start(f32[96,1728]{1,0:T(8,128)} %get-tuple-element.113), channel_id=1, source_target_pairs={{0,28},{4,0},{8,4},{12,8},{16,12},{20,16},{24,20},{28,24},{1,29},{... | collective-permute-start | bytes 1990664 | tf_op jit(solution)/shard_map/ppermute | solution.py:166
  (43 other events, 938.8 us)
Sparse Core Ops, SparseCore 0:
  10.8 55.9 all-gather.14
  98.9 19.5 all-gather.8
  168.5 30.5 all-gather.6
  233.4 37.8 reduce-scatter.3
  298.9 28.9 all-gather.10
  344.7 37.8 reduce-scatter.5
  400.9 28.9 all-gather.12
  520.0 37.8 reduce-scatter.7

commit v9 on v7

--- a/solution.py
+++ b/solution.py
@@ -140,13 +140,31 @@
     return lax.psum((jnp.sum(first_term, axis=1), jnp.sum(second_term, axis=1)), "col")
 
 
-def norm_forward(row_values, gain_row, shift_row):
-    totals, squares = row_totals(row_values, row_values * row_values)
+def norm_both(row_values, gain_row, shift_row, grad_rows):
+    scaled = grad_rows * gain_row
+    totals, squares, grad_totals, grad_along = lax.psum(
+        jnp.stack(
+            [
+                jnp.sum(row_values, axis=1),
+                jnp.sum(row_values * row_values, axis=1),
+                jnp.sum(scaled, axis=1),
+                jnp.sum(scaled * row_values, axis=1),
+            ]
+        ),
+        "col",
+    )
     mean_row = (totals / D)[:, None]
     var_row = (squares / D)[:, None] - mean_row * mean_row
     inverse = lax.rsqrt(var_row + NORM_EPS)
     normed = (row_values - mean_row) * inverse
-    return (normed * gain_row + shift_row, normed, inverse)
+    along = inverse * (grad_along[:, None] - mean_row * grad_totals[:, None])
+    back_rows = inverse * (scaled - (grad_totals / D)[:, None] - normed * (along / D))
+    return (
+        normed * gain_row + shift_row,
+        back_rows,
+        jnp.sum(grad_rows * normed, axis=0),
+        jnp.sum(grad_rows, axis=0),
+    )
 
 
 def norm_backward(grad_rows, normed, inverse, gain_row):
@@ -302,9 +320,8 @@
     acted = acted_f.astype(jnp.bfloat16)
     ffn_partial = jnp.dot(acted, down_complete, preferred_element_type=jnp.float32)
     second_sum = hidden + feature_sum(ffn_partial) + down_bias
-    result, normed_two, inverse_two = norm_forward(second_sum, final_gain, final_shift)
-    second_grad, final_gain_grad, final_shift_grad = norm_backward(
-        out_grad, normed_two, inverse_two, final_gain
+    result, second_grad, final_gain_grad, final_shift_grad = norm_both(
+        second_sum, final_gain, final_shift, out_grad
     )
     branch_grad = second_grad.astype(jnp.bfloat16)
     branch_full = feature_whole(branch_grad)

time: 765 us -> 755 us (0.987)
  blocking collectives: 41.8 us -> 31.2 us
    psum x3 -> x1, blocking collectives: 41.8 us -> 10.4 us  [row_totals(): lax.psum((jnp.sum(first_term, axis=1), jnp.sum(second_term, axis=1)), 'col')]
    psum x0 -> x1, blocking collectives: none -> 20.8 us  [norm_both(): lax.psum(jnp.stack([jnp.sum(row_values, axis=1), jnp.sum(row_values * row...]
where the time goes in v9:
time: 755 us; the launch traced here: 747 us
  waiting for transfers between devices  340 us (45%)
  Pallas kernels  116 us (15%)
  local copies, waits for them, and re-layouts  74.3 us (10%)
  matrix products  73.8 us (10%)
  starting transfers between devices  54.5 us (7%)
  other arithmetic  42 us (6%)
  blocking collectives  31.2 us (4%)
  between operations  15.4 us (2%)
    ppermute x21, waiting for transfers between devices, row_scatter_sum(): lax.ppermute(outgoing, 'row', [(i, (i + shift) % count) for i in range(co...  140 us
    reduce_scatter x3, waiting for transfers between devices, feature_sum(): lax.psum_scatter(partial_rows.astype(jnp.bfloat16), 'col', scatter_dimens...  76 us
    all_gather x3, waiting for transfers between devices, feature_whole(): return lax.all_gather(blocked, 'col', axis=1, tiled=True)  72.2 us
    pallas_call x1, Pallas kernels, attention_backward(): pl.pallas_call(functools.partial(_bwd_kernel, scale), grid=grid, in_specs...  69 us
    ppermute x13, waiting for transfers between devices, axis_gather(): lax.ppermute(values, axis, [(i, (i + shift) % count) for i in range(count)])  51.4 us
    pallas_call x1, Pallas kernels, attention_forward(): pl.pallas_call(functools.partial(_fwd_kernel, scale), grid=grid, in_specs...  46.9 us
    ppermute x21, starting transfers between devices, row_scatter_sum(): lax.ppermute(outgoing, 'row', [(i, (i + shift) % count) for i in range(co...  25.5 us
    psum x1, blocking collectives, norm_both(): lax.psum(jnp.stack([jnp.sum(row_values, axis=1), jnp.sum(row_values * row...  20.8 us
  transfers between devices with their start and end apart: 49, of which 26 were waited for; matrix products, arithmetic and copies ran while one was open for 13% of the time, Pallas kernels for 6%

profile of v9, /device:TPU:12, one launch (start us, length us, event | category | flops | bytes accessed | tf_op | source)
XLA Modules:
  0.0 746.9 jit_solution(15787682815747605040)
XLA Ops:
  17.9 32.7 %collective-permute-done.10 = f32[3,192]{1,0:T(4,128)S(1)} collective-permute-done((f32[3,192]{1,0:T(4,128)S(1)}, f32[3,192]{1,0:T(4,128)S(1)}, u32[]{:S(2)}, u32[]{:S(2)}) %collective-permute-start.10) | collective-permute-done | bytes 2336 | tf_op jit(solution)/shard_map/ppermute | solution.py:206
  58.8 5.0 collective-permute-done.4
  66.4 5.7 collective-permute-done.5
  72.1 4.7 collective-permute-start.7
  117.3 4.6 fusion.26
  121.9 46.9 %shard_map.305 = (bf16[3,2048,64]{2,1,0:T(8,128)(2,1)S(1)}, f32[3,2048,1]{2,1,0:T(8,128)}, f32[3,2048,1]{2,1,0:T(8,128)}) custom-call(bf16[3,2048,64]{2,1,0:T(8,128)(2,1)S(1)} %get-tuple-element.145.q_ref, bf16[3,2048,64]{2,1,0:T(8,128)(2,1)S(1)} %bitcast.239, bf16[3,2048,64]{2,1,0:T(8,128)(2,1)} %get-tuple-element.146.v_ref, s32[2048,1]{1,0:T(8,128)S(1)} %copy-done.2, ...), custom_call_target="tpu_custom_call" | custom-call | flops 3221225472 | bytes 3145728 | tf_op jit(solution)/shard_map/pallas_call | solution.py:79
  170.6 4.1 reshape.326
  186.3 14.1 %all-gather.7.cloned.1.call-done = bf16[2048,768]{0,1:T(8,128)(2,1)} async-done(((bf16[2048,192]{0,1:T(8,128)(2,1)}), bf16[2048,768]{0,1:T(8,128)(2,1)}) %all-gather.7.cloned.1.call-update) | async-done | bytes 3145744 | tf_op jit(solution)/shard_map/all_gather | solution.py:130
  200.4 6.8 fusion.62
  211.0 18.0 %multiply_convert_fusion = (bf16[2048,768]{1,0:T(8,128)(2,1)S(1)}, f32[2048,768]{1,0:T(8,128)}, f32[2048,768]{1,0:T(8,128)}) fusion(f32[768]{0:T(1024)S(1)} %copy-done.34, bf16[768,768]{1,0:T(8,128)(2,1)S(1)} %copy-done.14, f32[2048,768]{0,1:T(8,128)S(1)} %get-tuple-element.88), kind=kOutput, calls=%fused_computation.10 | convolution fusion | flops 2521300992 | bytes 23202816 | tf_op jit(solution)/shard_map/dot_general | solution.py:318
  230.7 4.1 convolution_convert_fusion.1
  234.8 38.0 %reduce-scatter.4.cloned.1.call-done = bf16[2048,192]{0,1:T(8,128)(2,1)} async-done(((bf16[2048,768]{0,1:T(8,128)(2,1)}), bf16[2048,192]{0,1:T(8,128)(2,1)}) %reduce-scatter.4.cloned.1.call-update) | async-done | bytes 786448 | tf_op jit(solution)/shard_map/reduce_scatter | solution.py:134
  275.4 20.8 %psum.21 = f32[4,2048]{1,0:T(4,128)S(1)} all-reduce(f32[4,2048]{1,0:T(4,128)S(1)} %pad_maximum_fusion.4), channel_id=1, replica_groups=mesh['row'=8,'col'=4] {'col'}, use_global_device_ids=true, to_apply=%region_7.0 | all-reduce | flops 8192 | bytes 65536 | tf_op jit(solution)/shard_map/psum | solution.py:145
  299.4 29.0 %all-gather.11.cloned.1.call-done = bf16[2048,768]{0,1:T(8,128)(2,1)} async-done(((bf16[2048,192]{0,1:T(8,128)(2,1)}), bf16[2048,768]{0,1:T(8,128)(2,1)}) %all-gather.11.cloned.1.call-update) | async-done | bytes 3145744 | tf_op jit(solution)/shard_map/all_gather | solution.py:130
  328.4 10.9 %convert_reduce_fusion = (f32[768]{0:T(1024)S(1)}, bf16[2048,768]{1,0:T(8,128)(2,1)S(1)}) fusion(f32[2048,768]{1,0:T(8,128)} %get-tuple-element.87, f32[2048,768]{1,0:T(8,128)} %get-tuple-element.144, f32[768]{0:T(1024)S(1)} %copy-done.34, bf16[2048,768]{0,1:T(8,128)(2,1)} %all-gather.11.cloned.1.call-done, bf16[768,768]{0,1:T(8,128)(2,1)} %bitcast.258), kind=kOutput, calls=%fused_computation.8 | convolution fusion | flops 2442657024 | bytes 20060160 | tf_op jit(solution)/shard_map/dot_general | solution.py:329
  340.9 4.0 convolution_convert_fusion
  345.0 38.0 %reduce-scatter.6.cloned.1.call-done = bf16[2048,192]{0,1:T(8,128)(2,1)} async-done(((bf16[2048,768]{0,1:T(8,128)(2,1)}), bf16[2048,192]{0,1:T(8,128)(2,1)}) %reduce-scatter.6.cloned.1.call-update) | async-done | bytes 786448 | tf_op jit(solution)/shard_map/reduce_scatter | solution.py:134
  383.0 4.2 multiply_reduce_fusion.1
  387.2 10.4 %all-reduce = (f32[2048]{0:T(1024)S(1)}, f32[2048]{0:T(1024)S(1)}) all-reduce(f32[2048]{0:T(1024)S(1)} %get-tuple-element.66, f32[2048]{0:T(1024)S(1)} %get-tuple-element.67), channel_id=1, replica_groups=mesh['row'=8,'col'=4] {'col'}, use_global_device_ids=true, to_apply=%region_12.0 | all-reduce | flops 4096 | bytes 32768 | tf_op jit(solution)/shard_map/psum | solution.py:140
  400.9 29.0 %all-gather.13.cloned.1.call-done = bf16[2048,768]{0,1:T(8,128)(2,1)} async-done(((bf16[2048,192]{0,1:T(8,128)(2,1)}), bf16[2048,768]{0,1:T(8,128)(2,1)}) %all-gather.13.cloned.1.call-update) | async-done | bytes 3145744 | tf_op jit(solution)/shard_map/all_gather | solution.py:130
  436.8 69.0 %shard_map.306 = (bf16[3,2048,64]{2,1,0:T(8,128)(2,1)S(1)}, f32[3,2048,64]{2,1,0:T(8,128)}, f32[3,2048,64]{2,1,0:T(8,128)}) custom-call(bf16[3,2048,64]{2,1,0:T(8,128)(2,1)S(1)} %copy-done.1, bf16[3,2048,64]{2,1,0:T(8,128)(2,1)S(1)} %bitcast.240, bf16[3,2048,64]{2,1,0:T(8,128)(2,1)} %get-tuple-element.146.v_ref, bf16[3,2048,64]{2,1,0:T(8,128)(2,1)} %bitcast.256, ...), custom_call_target="tpu_custom_call" | custom-call | flops 8053063680 | bytes 6291456 | tf_op jit(solution)/shard_map/pallas_call | solution.py:107
  513.9 6.2 bitcast_convert_fusion
  520.2 5.6 fusion.73
  525.8 5.9 fusion.28
  534.1 6.1 copy.80
  551.4 8.2 %collective-permute-done.34 = f32[96,1536]{1,0:T(8,128)S(1)} collective-permute-done((f32[96,1536]{1,0:T(8,128)S(1)}, f32[96,1536]{1,0:T(8,128)S(1)}, u32[]{:S(2)}, u32[]{:S(2)}) %collective-permute-start.34) | collective-permute-done | bytes 589856 | tf_op jit(solution)/shard_map/ppermute | solution.py:184
  560.1 62.2 %collective-permute-done.35 = f32[96,1536]{1,0:T(8,128)S(1)} collective-permute-done((f32[96,1536]{1,0:T(8,128)S(1)}, f32[96,1536]{1,0:T(8,128)S(1)}, u32[]{:S(2)}, u32[]{:S(2)}) %collective-permute-start.35) | collective-permute-done | bytes 589856 | tf_op jit(solution)/shard_map/ppermute | solution.py:184
  623.3 11.9 %collective-permute-done.36 = f32[96,1536]{1,0:T(8,128)} collective-permute-done((f32[96,1536]{1,0:T(8,128)}, f32[96,1536]{1,0:T(8,128)}, u32[]{:S(2)}, u32[]{:S(2)}) %collective-permute-start.36) | collective-permute-done | bytes 589856 | tf_op jit(solution)/shard_map/ppermute | solution.py:184
  635.2 11.9 %collective-permute-done.37 = f32[96,1536]{1,0:T(8,128)} collective-permute-done((f32[96,1536]{1,0:T(8,128)}, f32[96,1536]{1,0:T(8,128)}, u32[]{:S(2)}, u32[]{:S(2)}) %collective-permute-start.37) | collective-permute-done | bytes 589856 | tf_op jit(solution)/shard_map/ppermute | solution.py:184
  694.4 13.3 %collective-permute-done.32 = f32[96,192]{1,0:T(8,128)S(1)} collective-permute-done((f32[96,192]{1,0:T(8,128)S(1)}, f32[96,192]{1,0:T(8,128)S(1)}, u32[]{:S(2)}, u32[]{:S(2)}) %collective-permute-start.32) | collective-permute-done | bytes 73760 | tf_op jit(solution)/shard_map/ppermute | solution.py:184
  713.0 13.3 %collective-permute-done.15 = f32[96,576]{1,0:T(8,128)} collective-permute-done((f32[96,576]{1,0:T(8,128)S(1)}, f32[96,576]{1,0:T(8,128)}, u32[]{:S(2)}, u32[]{:S(2)}) %collective-permute-start.15) | collective-permute-done | bytes 221216 | tf_op jit(solution)/shard_map/ppermute | solution.py:184
  726.3 4.0 collective-permute-done.16
  (259 shorter events, 182.9 us)
Async XLA Ops:
  7.2 163.4 %all-gather.15.cloned.1.call-start = ((), (), s32[]{:S(2)}) async-start(), calls=%async_computation.10 | async-start | bytes 2654208 | tf_op jit(solution)/shard_map/all_gather | solution.py:231
  10.5 175.8 %all-gather.9.cloned.1.call-start = ((), (), s32[]{:S(2)}) async-start(), calls=%async_computation.4 | async-start | bytes 1474560 | tf_op jit(solution)/shard_map/all_gather | solution.py:290
  12.6 44.5 %collective-permute-start.3 = (bf16[73728]{0:T(1024)(128)(2,1)S(1)}, bf16[73728]{0:T(1024)(128)(2,1)S(1)}, u32[]{:S(2)}, u32[]{:S(2)}) collective-permute-start(bf16[73728]{0:T(1024)(128)(2,1)S(1)} %constant_dynamic-update-slice_fusion), channel_id=1, source_target_pairs={{0,4},{4,8},{8,12},{12,16},{16,20},{20,24},{24,28},{28,0},{1,5},{5... | collective-permute-start | bytes 442376 | tf_op jit(solution)/shard_map/ppermute | solution.py:206
  14.1 86.8 %collective-permute-start = (bf16[192,2048]{1,0:T(8,128)(2,1)}, bf16[192,2048]{1,0:T(8,128)(2,1)}, u32[]{:S(2)}, u32[]{:S(2)}) collective-permute-start(bf16[192,2048]{1,0:T(8,128)(2,1)} %param.18), channel_id=1, source_target_pairs={{0,1},{1,2},{2,3},{3,0},{4,5},{5,6},{6,7},{7,4},{8,9},{9,10},{10,1... | collective-permute-start | bytes 2359304 | tf_op jit(solution)/shard_map/ppermute | solution.py:206
  14.1 86.8 %collective-permute-start.1 = (bf16[192,2048]{1,0:T(8,128)(2,1)}, bf16[192,2048]{1,0:T(8,128)(2,1)}, u32[]{:S(2)}, u32[]{:S(2)}) collective-permute-start(bf16[192,2048]{1,0:T(8,128)(2,1)} %param.18), channel_id=1, source_target_pairs={{0,2},{1,3},{2,0},{3,1},{4,6},{5,7},{6,4},{7,5},{8,10},{9,11},{10,... | collective-permute-start | bytes 2359304 | tf_op jit(solution)/shard_map/ppermute | solution.py:206
  15.6 85.3 %collective-permute-start.2 = (bf16[192,2048]{1,0:T(8,128)(2,1)}, bf16[192,2048]{1,0:T(8,128)(2,1)}, u32[]{:S(2)}, u32[]{:S(2)}) collective-permute-start(bf16[192,2048]{1,0:T(8,128)(2,1)} %param.18), channel_id=1, source_target_pairs={{0,3},{1,0},{2,1},{3,2},{4,7},{5,4},{6,5},{7,6},{8,11},{9,8},{10,9... | collective-permute-start | bytes 2359304 | tf_op jit(solution)/shard_map/ppermute | solution.py:206
  17.8 32.7 %collective-permute-start.10 = (f32[3,192]{1,0:T(4,128)S(1)}, f32[3,192]{1,0:T(4,128)S(1)}, u32[]{:S(2)}, u32[]{:S(2)}) collective-permute-start(f32[3,192]{1,0:T(4,128)S(1)} %get-tuple-element.142), channel_id=1, source_target_pairs={{0,1},{1,2},{2,3},{3,0},{4,5},{5,6},{6,7},{7,4},{8,9},{9,10},{10,1... | collective-permute-start | bytes 6920 | tf_op jit(solution)/shard_map/ppermute | solution.py:206
  63.8 15.8 %collective-permute-start.6 = (bf16[73728]{0:T(1024)(128)(2,1)S(1)}, bf16[73728]{0:T(1024)(128)(2,1)S(1)}, u32[]{:S(2)}, u32[]{:S(2)}) collective-permute-start(bf16[73728]{0:T(1024)(128)(2,1)S(1)} %constant_dynamic-update-slice_fusion), channel_id=1, source_target_pairs={{0,16},{4,20},{8,24},{12,28},{16,0},{20,4},{24,8},{28,12},{1,17},{... | collective-permute-start | bytes 442376 | tf_op jit(solution)/shard_map/ppermute | solution.py:206
  100.7 99.8 %all-gather.7.cloned.1.call-start = ((), (), s32[]{:S(2)}) async-start(), calls=%async_computation.3 | async-start | bytes 3932160 | tf_op jit(solution)/shard_map/all_gather | solution.py:130
  170.2 102.6 %reduce-scatter.4.cloned.1.call-start = ((), (), s32[]{:S(2)}) async-start(), calls=%async_computation.5 | async-start | bytes 3932160 | tf_op jit(solution)/shard_map/reduce_scatter | solution.py:134
  234.8 93.6 %all-gather.11.cloned.1.call-start = ((), (), s32[]{:S(2)}) async-start(), calls=%async_computation.6 | async-start | bytes 3932160 | tf_op jit(solution)/shard_map/all_gather | solution.py:130
  299.3 83.7 %reduce-scatter.6.cloned.1.call-start = ((), (), s32[]{:S(2)}) async-start(), calls=%async_computation.7 | async-start | bytes 3932160 | tf_op jit(solution)/shard_map/reduce_scatter | solution.py:134
  344.9 85.0 %all-gather.13.cloned.1.call-start = ((), (), s32[]{:S(2)}) async-start(), calls=%async_computation.8 | async-start | bytes 3932160 | tf_op jit(solution)/shard_map/all_gather | solution.py:130
  400.8 335.7 %reduce-scatter.8.cloned.1.call-start = ((), (), s32[]{:S(2)}) async-start(), calls=%async_computation.9 | async-start | bytes 3932160 | tf_op jit(solution)/shard_map/reduce_scatter | solution.py:134
  544.1 15.5 %collective-permute-start.34 = (f32[96,1536]{1,0:T(8,128)S(1)}, f32[96,1536]{1,0:T(8,128)S(1)}, u32[]{:S(2)}, u32[]{:S(2)}) collective-permute-start(f32[96,1536]{1,0:T(8,128)S(1)} %get-tuple-element.90), channel_id=1, source_target_pairs={{0,4},{4,8},{8,12},{12,16},{16,20},{20,24},{24,28},{28,0},{1,5},{5... | collective-permute-start | bytes 1769480 | tf_op jit(solution)/shard_map/ppermute | solution.py:184
  545.5 76.8 %collective-permute-start.35 = (f32[96,1536]{1,0:T(8,128)S(1)}, f32[96,1536]{1,0:T(8,128)S(1)}, u32[]{:S(2)}, u32[]{:S(2)}) collective-permute-start(f32[96,1536]{1,0:T(8,128)S(1)} %get-tuple-element.96), channel_id=1, source_target_pairs={{0,8},{4,12},{8,16},{12,20},{16,24},{20,28},{24,0},{28,4},{1,9},{5... | collective-permute-start | bytes 1769480 | tf_op jit(solution)/shard_map/ppermute | solution.py:184
  547.0 88.2 %collective-permute-start.36 = (f32[96,1536]{1,0:T(8,128)}, f32[96,1536]{1,0:T(8,128)}, u32[]{:S(2)}, u32[]{:S(2)}) collective-permute-start(f32[96,1536]{1,0:T(8,128)} %get-tuple-element.95), channel_id=1, source_target_pairs={{0,12},{4,16},{8,20},{12,24},{16,28},{20,0},{24,4},{28,8},{1,13},{... | collective-permute-start | bytes 1769480 | tf_op jit(solution)/shard_map/ppermute | solution.py:184
  548.4 98.7 %collective-permute-start.37 = (f32[96,1536]{1,0:T(8,128)}, f32[96,1536]{1,0:T(8,128)}, u32[]{:S(2)}, u32[]{:S(2)}) collective-permute-start(f32[96,1536]{1,0:T(8,128)} %get-tuple-element.94), channel_id=1, source_target_pairs={{0,16},{4,20},{8,24},{12,28},{16,0},{20,4},{24,8},{28,12},{1,17},{... | collective-permute-start | bytes 1769480 | tf_op jit(solution)/shard_map/ppermute | solution.py:184
  549.9 97.2 %collective-permute-start.38 = (f32[96,1536]{1,0:T(8,128)}, f32[96,1536]{1,0:T(8,128)}, u32[]{:S(2)}, u32[]{:S(2)}) collective-permute-start(f32[96,1536]{1,0:T(8,128)} %get-tuple-element.93), channel_id=1, source_target_pairs={{0,20},{4,24},{8,28},{12,0},{16,4},{20,8},{24,12},{28,16},{1,21},{... | collective-permute-start | bytes 1769480 | tf_op jit(solution)/shard_map/ppermute | solution.py:184
  559.5 89.7 %collective-permute-start.39 = (f32[96,1536]{1,0:T(8,128)}, f32[96,1536]{1,0:T(8,128)}, u32[]{:S(2)}, u32[]{:S(2)}) collective-permute-start(f32[96,1536]{1,0:T(8,128)} %get-tuple-element.92), channel_id=1, source_target_pairs={{0,24},{4,28},{8,0},{12,4},{16,8},{20,12},{24,16},{28,20},{1,25},{... | collective-permute-start | bytes 1769480 | tf_op jit(solution)/shard_map/ppermute | solution.py:184
  623.1 27.1 %collective-permute-start.40 = (f32[96,1536]{1,0:T(8,128)S(1)}, f32[96,1536]{1,0:T(8,128)}, u32[]{:S(2)}, u32[]{:S(2)}) collective-permute-start(f32[96,1536]{1,0:T(8,128)S(1)} %get-tuple-element.91), channel_id=1, source_target_pairs={{0,28},{4,0},{8,4},{12,8},{16,12},{20,16},{24,20},{28,24},{1,29},{... | collective-permute-start | bytes 1769480 | tf_op jit(solution)/shard_map/ppermute | solution.py:184
  654.5 16.9 %collective-permute-start.22 = (f32[2304]{0:T(1024)S(1)}, f32[2304]{0:T(1024)S(1)}, u32[]{:S(2)}, u32[]{:S(2)}) collective-permute-start(f32[2304]{0:T(1024)S(1)} %concatenate.18), channel_id=1, source_target_pairs={{0,12},{4,16},{8,20},{12,24},{16,28},{20,0},{24,4},{28,8},{1,13},{... | collective-permute-start | bytes 27656 | tf_op jit(solution)/shard_map/ppermute | solution.py:194
  676.2 17.9 %collective-permute-start.31 = (f32[96,192]{1,0:T(8,128)S(1)}, f32[96,192]{1,0:T(8,128)S(1)}, u32[]{:S(2)}, u32[]{:S(2)}) collective-permute-start(f32[96,192]{1,0:T(8,128)S(1)} %get-tuple-element.115), channel_id=1, source_target_pairs={{0,20},{4,24},{8,28},{12,0},{16,4},{20,8},{24,12},{28,16},{1,21},{... | collective-permute-start | bytes 221192 | tf_op jit(solution)/shard_map/ppermute | solution.py:184
  678.7 29.1 %collective-permute-start.32 = (f32[96,192]{1,0:T(8,128)S(1)}, f32[96,192]{1,0:T(8,128)S(1)}, u32[]{:S(2)}, u32[]{:S(2)}) collective-permute-start(f32[96,192]{1,0:T(8,128)S(1)} %get-tuple-element.114), channel_id=1, source_target_pairs={{0,24},{4,28},{8,0},{12,4},{16,8},{20,12},{24,16},{28,20},{1,25},{... | collective-permute-start | bytes 221192 | tf_op jit(solution)/shard_map/ppermute | solution.py:184
  684.9 22.9 %collective-permute-start.33 = (f32[96,192]{1,0:T(8,128)S(1)}, f32[96,192]{1,0:T(8,128)S(1)}, u32[]{:S(2)}, u32[]{:S(2)}) collective-permute-start(f32[96,192]{1,0:T(8,128)S(1)} %get-tuple-element.113), channel_id=1, source_target_pairs={{0,28},{4,0},{8,4},{12,8},{16,12},{20,16},{24,20},{28,24},{1,29},{... | collective-permute-start | bytes 221192 | tf_op jit(solution)/shard_map/ppermute | solution.py:184
  687.9 19.8 %collective-permute-start.13 = (f32[96,576]{1,0:T(8,128)S(1)}, f32[96,576]{1,0:T(8,128)S(1)}, u32[]{:S(2)}, u32[]{:S(2)}) collective-permute-start(f32[96,576]{1,0:T(8,128)S(1)} %get-tuple-element.104), channel_id=1, source_target_pairs={{0,4},{4,8},{8,12},{12,16},{16,20},{20,24},{24,28},{28,0},{1,5},{5... | collective-permute-start | bytes 663560 | tf_op jit(solution)/shard_map/ppermute | solution.py:184
  690.0 18.8 %collective-permute-start.14 = (f32[96,576]{1,0:T(8,128)S(1)}, f32[96,576]{1,0:T(8,128)S(1)}, u32[]{:S(2)}, u32[]{:S(2)}) collective-permute-start(f32[96,576]{1,0:T(8,128)S(1)} %get-tuple-element.110), channel_id=1, source_target_pairs={{0,8},{4,12},{8,16},{12,20},{16,24},{20,28},{24,0},{28,4},{1,9},{5... | collective-permute-start | bytes 663560 | tf_op jit(solution)/shard_map/ppermute | solution.py:184
  694.1 32.2 %collective-permute-start.15 = (f32[96,576]{1,0:T(8,128)S(1)}, f32[96,576]{1,0:T(8,128)}, u32[]{:S(2)}, u32[]{:S(2)}) collective-permute-start(f32[96,576]{1,0:T(8,128)S(1)} %get-tuple-element.109), channel_id=1, source_target_pairs={{0,12},{4,16},{8,20},{12,24},{16,28},{20,0},{24,4},{28,8},{1,13},{... | collective-permute-start | bytes 663560 | tf_op jit(solution)/shard_map/ppermute | solution.py:184
  707.7 22.6 %collective-permute-start.16 = (f32[96,576]{1,0:T(8,128)S(1)}, f32[96,576]{1,0:T(8,128)}, u32[]{:S(2)}, u32[]{:S(2)}) collective-permute-start(f32[96,576]{1,0:T(8,128)S(1)} %get-tuple-element.108), channel_id=1, source_target_pairs={{0,16},{4,20},{8,24},{12,28},{16,0},{20,4},{24,8},{28,12},{1,17},{... | collective-permute-start | bytes 663560 | tf_op jit(solution)/shard_map/ppermute | solution.py:184
  707.7 22.6 %collective-permute-start.17 = (f32[96,576]{1,0:T(8,128)S(1)}, f32[96,576]{1,0:T(8,128)}, u32[]{:S(2)}, u32[]{:S(2)}) collective-permute-start(f32[96,576]{1,0:T(8,128)S(1)} %get-tuple-element.107), channel_id=1, source_target_pairs={{0,20},{4,24},{8,28},{12,0},{16,4},{20,8},{24,12},{28,16},{1,21},{... | collective-permute-start | bytes 663560 | tf_op jit(solution)/shard_map/ppermute | solution.py:184
  707.8 26.4 %collective-permute-start.18 = (f32[96,576]{1,0:T(8,128)S(1)}, f32[96,576]{1,0:T(8,128)}, u32[]{:S(2)}, u32[]{:S(2)}) collective-permute-start(f32[96,576]{1,0:T(8,128)S(1)} %get-tuple-element.106), channel_id=1, source_target_pairs={{0,24},{4,28},{8,0},{12,4},{16,8},{20,12},{24,16},{28,20},{1,25},{... | collective-permute-start | bytes 663560 | tf_op jit(solution)/shard_map/ppermute | solution.py:184
  708.8 25.4 %collective-permute-start.19 = (f32[96,576]{1,0:T(8,128)S(1)}, f32[96,576]{1,0:T(8,128)}, u32[]{:S(2)}, u32[]{:S(2)}) collective-permute-start(f32[96,576]{1,0:T(8,128)S(1)} %get-tuple-element.105), channel_id=1, source_target_pairs={{0,28},{4,0},{8,4},{12,8},{16,12},{20,16},{24,20},{28,24},{1,29},{... | collective-permute-start | bytes 663560 | tf_op jit(solution)/shard_map/ppermute | solution.py:184
  (55 other events, 1030.4 us)
Sparse Core Ops, SparseCore 0:
  10.8 54.5 all-gather.14
  100.8 19.0 all-gather.8
  170.3 30.0 all-gather.6
  234.9 37.8 reduce-scatter.3
  299.4 28.9 all-gather.10
  345.1 37.8 reduce-scatter.5
  400.9 28.9 all-gather.12
  520.3 37.8 reduce-scatter.7

commit v10 on v9

--- a/solution.py
+++ b/solution.py
@@ -189,12 +189,36 @@
 
 def row_sum(values):
     count = lax.axis_size("row")
+    if count & (count - 1):
+        total = values
+        for shift in range(1, count):
+            total = total + lax.ppermute(
+                values, "row", [(i, (i + shift) % count) for i in range(count)]
+            )
+        return total
     total = values
-    for shift in range(1, count):
-        total = total + lax.ppermute(
-            values, "row", [(i, (i + shift) % count) for i in range(count)]
-        )
+    bit = count // 2
+    while bit >= 1:
+        total = total + lax.ppermute(total, "row", [(i, i ^ bit) for i in range(count)])
+        bit //= 2
     return total
+
+
+def row_scatter_halving(partial_rows):
+    count = lax.axis_size("row")
+    if count & (count - 1):
+        return row_scatter_sum(partial_rows)
+    me = lax.axis_index("row")
+    held = partial_rows.reshape((count, partial_rows.shape[0] // count) + partial_rows.shape[1:])
+    bit = count // 2
+    while bit >= 1:
+        side = lax.rem(me // bit, 2)
+        half = held.shape[0] // 2
+        keep = lax.dynamic_slice_in_dim(held, side * half, half, axis=0)
+        away = lax.dynamic_slice_in_dim(held, (1 - side) * half, half, axis=0)
+        held = keep + lax.ppermute(away, "row", [(i, i ^ bit) for i in range(count)])
+        bit //= 2
+    return held[0]
 
 
 def axis_gather(values, axis):
@@ -212,14 +236,6 @@
 def weight_partial(gathered, local_grad):
     return lax.dot_general(
         gathered, local_grad, (((0,), (0,)), ((), ())), preferred_element_type=jnp.float32
-    )
-
-
-def weight_grad(gathered, local_grad):
-    return row_scatter_sum(
-        lax.dot_general(
-            gathered, local_grad, (((0,), (0,)), ((), ())), preferred_element_type=jnp.float32
-        )
     )
 
 
@@ -344,7 +360,7 @@
     )
     attn_branch_grad = first_grad.astype(jnp.bfloat16)
     attn_branch_full = feature_whole(attn_branch_grad)
-    output_weight_grad = weight_grad(attn_branch_full, attended).T
+    output_weight_grad = row_scatter_halving(weight_partial(attn_branch_full, attended)).T
     attended_grad = lax.dot_general(
         attn_branch_full, output_rows, (((1,), (1,)), ((), ())), preferred_element_type=jnp.float32
     ).astype(jnp.bfloat16)
@@ -362,8 +378,8 @@
     key_grad = heads_beside(key_grad_h).astype(jnp.bfloat16)
     value_grad = heads_beside(value_grad_h).astype(jnp.bfloat16)
     column_count = query_weight.shape[1]
-    qkv_grads = weight_grad(
-        inputs_full, jnp.concatenate([query_grad, key_grad, value_grad], axis=1)
+    qkv_grads = row_scatter_halving(
+        weight_partial(inputs_full, jnp.concatenate([query_grad, key_grad, value_grad], axis=1))
     )
     input_grad = first_grad + feature_sum(
         jnp.einsum(

time: 755 us -> 785 us (1.040)
  waiting for transfers between devices: 340 us -> 355 us
  starting transfers between devices: 54.5 us -> 68.8 us
    ppermute x7 -> x9, waiting for transfers between devices: 0.02 us -> 64.7 us  [the longest x3 55.2 us: row_sum(): lax.ppermute(total, 'row', [(i, i ^ bit) for i in range(count)])]
    ppermute x21 -> x7, waiting for transfers between devices: 140 us -> 90.8 us  [row_scatter_sum(): lax.ppermute(outgoing, 'row', [(i, (i + shift) % count) for i in range(co...]
    ppermute x7 -> x9, starting transfers between devices: 9.65 us -> 39.1 us  [the longest x6 24.6 us: row_scatter_halving(): lax.ppermute(away, 'row', [(i, i ^ bit) for i in range(count)])]
    ppermute x21 -> x7, starting transfers between devices: 25.5 us -> 10.4 us  [row_scatter_sum(): lax.ppermute(outgoing, 'row', [(i, (i + shift) % count) for i in range(co...]
    dot_general x2 -> x4, matrix products: 11.5 us -> 17.3 us  [weight_partial(): lax.dot_general(gathered, local_grad, (((0,), (0,)), ((), ())), preferred...]
  transfers between devices with their start and end apart: 49 -> 37, of which waited for: 26 -> 20; matrix products, arithmetic and copies ran while one was open for 13% -> 12% of each run, Pallas kernels for 6% -> 6%
where the time goes in v10:
time: 785 us; the launch traced here: 773 us
  waiting for transfers between devices  355 us (45%)
  Pallas kernels  116 us (15%)
  matrix products  73.5 us (9%)
  local copies, waits for them, and re-layouts  72.6 us (9%)
  starting transfers between devices  68.8 us (9%)
  other arithmetic  40.2 us (5%)
  blocking collectives  31.3 us (4%)
  between operations  15.4 us (2%)
    ppermute x7, waiting for transfers between devices, row_scatter_sum(): lax.ppermute(outgoing, 'row', [(i, (i + shift) % count) for i in range(co...  90.8 us
    reduce_scatter x3, waiting for transfers between devices, feature_sum(): lax.psum_scatter(partial_rows.astype(jnp.bfloat16), 'col', scatter_dimens...  76 us
    all_gather x3, waiting for transfers between devices, feature_whole(): return lax.all_gather(blocked, 'col', axis=1, tiled=True)  72 us
    pallas_call x1, Pallas kernels, attention_backward(): pl.pallas_call(functools.partial(_bwd_kernel, scale), grid=grid, in_specs...  68.9 us
    ppermute x3, waiting for transfers between devices, row_sum(): lax.ppermute(total, 'row', [(i, i ^ bit) for i in range(count)])  55.2 us
    ppermute x13, waiting for transfers between devices, axis_gather(): lax.ppermute(values, axis, [(i, (i + shift) % count) for i in range(count)])  51.3 us
    pallas_call x1, Pallas kernels, attention_forward(): pl.pallas_call(functools.partial(_fwd_kernel, scale), grid=grid, in_specs...  46.9 us
    ppermute x6, starting transfers between devices, row_scatter_halving(): lax.ppermute(away, 'row', [(i, i ^ bit) for i in range(count)])  24.6 us
  transfers between devices with their start and end apart: 37, of which 20 were waited for; matrix products, arithmetic and copies ran while one was open for 12% of the time, Pallas kernels for 6%

profile of v10, /device:TPU:12, one launch (start us, length us, event | category | flops | bytes accessed | tf_op | source)
XLA Modules:
  0.0 772.7 jit_solution(9448833890110060322)
XLA Ops:
  17.9 32.7 %collective-permute-done.10 = f32[3,192]{1,0:T(4,128)S(1)} collective-permute-done((f32[3,192]{1,0:T(4,128)S(1)}, f32[3,192]{1,0:T(4,128)S(1)}, u32[]{:S(2)}, u32[]{:S(2)}) %collective-permute-start.10) | collective-permute-done | bytes 2336 | tf_op jit(solution)/shard_map/ppermute | solution.py:230
  58.8 5.0 collective-permute-done.4
  66.4 5.7 collective-permute-done.5
  72.1 4.7 collective-permute-start.7
  117.3 4.7 fusion.26
  122.0 46.9 %shard_map.305 = (bf16[3,2048,64]{2,1,0:T(8,128)(2,1)S(1)}, f32[3,2048,1]{2,1,0:T(8,128)}, f32[3,2048,1]{2,1,0:T(8,128)}) custom-call(bf16[3,2048,64]{2,1,0:T(8,128)(2,1)S(1)} %get-tuple-element.148.q_ref, bf16[3,2048,64]{2,1,0:T(8,128)(2,1)S(1)} %bitcast.185, bf16[3,2048,64]{2,1,0:T(8,128)(2,1)} %get-tuple-element.149.v_ref, s32[2048,1]{1,0:T(8,128)S(1)} %copy-done.2, ...), custom_call_target="tpu_custom_call" | custom-call | flops 3221225472 | bytes 3145728 | tf_op jit(solution)/shard_map/pallas_call | solution.py:79
  186.4 14.2 %all-gather.7.cloned.1.call-done = bf16[2048,768]{0,1:T(8,128)(2,1)} async-done(((bf16[2048,192]{0,1:T(8,128)(2,1)}), bf16[2048,768]{0,1:T(8,128)(2,1)}) %all-gather.7.cloned.1.call-update) | async-done | bytes 3145744 | tf_op jit(solution)/shard_map/all_gather | solution.py:130
  200.6 6.8 fusion.49
  211.1 18.0 %multiply_convert_fusion = (bf16[2048,768]{1,0:T(8,128)(2,1)S(1)}, f32[2048,768]{1,0:T(8,128)}, f32[2048,768]{1,0:T(8,128)}) fusion(f32[768]{0:T(1024)S(1)} %copy-done.32, bf16[768,768]{1,0:T(8,128)(2,1)S(1)} %copy-done.14, f32[2048,768]{0,1:T(8,128)S(1)} %get-tuple-element.105), kind=kOutput, calls=%fused_computation.10 | convolution fusion | flops 2521300992 | bytes 23202816 | tf_op jit(solution)/shard_map/dot_general | solution.py:334
  234.9 38.0 %reduce-scatter.4.cloned.1.call-done = bf16[2048,192]{0,1:T(8,128)(2,1)} async-done(((bf16[2048,768]{0,1:T(8,128)(2,1)}), bf16[2048,192]{0,1:T(8,128)(2,1)}) %reduce-scatter.4.cloned.1.call-update) | async-done | bytes 786448 | tf_op jit(solution)/shard_map/reduce_scatter | solution.py:134
  275.5 20.9 %psum.21 = f32[4,2048]{1,0:T(4,128)S(1)} all-reduce(f32[4,2048]{1,0:T(4,128)S(1)} %pad_maximum_fusion.4), channel_id=1, replica_groups=mesh['row'=8,'col'=4] {'col'}, use_global_device_ids=true, to_apply=%region_7.0 | all-reduce | flops 8192 | bytes 65536 | tf_op jit(solution)/shard_map/psum | solution.py:145
  299.5 29.0 %all-gather.11.cloned.1.call-done = bf16[2048,768]{0,1:T(8,128)(2,1)} async-done(((bf16[2048,192]{0,1:T(8,128)(2,1)}), bf16[2048,768]{0,1:T(8,128)(2,1)}) %all-gather.11.cloned.1.call-update) | async-done | bytes 3145744 | tf_op jit(solution)/shard_map/all_gather | solution.py:130
  328.6 10.9 %convert_reduce_fusion = (f32[768]{0:T(1024)S(1)}, bf16[2048,768]{1,0:T(8,128)(2,1)S(1)}) fusion(f32[2048,768]{1,0:T(8,128)} %get-tuple-element.104, f32[2048,768]{1,0:T(8,128)} %get-tuple-element.147, f32[768]{0:T(1024)S(1)} %copy-done.32, bf16[2048,768]{0,1:T(8,128)(2,1)} %all-gather.11.cloned.1.call-done, bf16[768,768]{0,1:T(8,128)(2,1)} %bitcast.204), kind=kOutput, calls=%fused_computation.8 | convolution fusion | flops 2442657024 | bytes 20060160 | tf_op jit(solution)/shard_map/dot_general | solution.py:345
  345.2 38.0 %reduce-scatter.6.cloned.1.call-done = bf16[2048,192]{0,1:T(8,128)(2,1)} async-done(((bf16[2048,768]{0,1:T(8,128)(2,1)}), bf16[2048,192]{0,1:T(8,128)(2,1)}) %reduce-scatter.6.cloned.1.call-update) | async-done | bytes 786448 | tf_op jit(solution)/shard_map/reduce_scatter | solution.py:134
  383.2 4.2 multiply_reduce_fusion.1
  387.4 10.4 %all-reduce = (f32[2048]{0:T(1024)S(1)}, f32[2048]{0:T(1024)S(1)}) all-reduce(f32[2048]{0:T(1024)S(1)} %get-tuple-element.83, f32[2048]{0:T(1024)S(1)} %get-tuple-element.84), channel_id=1, replica_groups=mesh['row'=8,'col'=4] {'col'}, use_global_device_ids=true, to_apply=%region_12.0 | all-reduce | flops 4096 | bytes 32768 | tf_op jit(solution)/shard_map/psum | solution.py:140
  401.3 28.8 %all-gather.13.cloned.1.call-done = bf16[2048,768]{0,1:T(8,128)(2,1)} async-done(((bf16[2048,192]{0,1:T(8,128)(2,1)}), bf16[2048,768]{0,1:T(8,128)(2,1)}) %all-gather.13.cloned.1.call-update) | async-done | bytes 3145744 | tf_op jit(solution)/shard_map/all_gather | solution.py:130
  437.0 68.9 %shard_map.306 = (bf16[3,2048,64]{2,1,0:T(8,128)(2,1)S(1)}, f32[3,2048,64]{2,1,0:T(8,128)}, f32[3,2048,64]{2,1,0:T(8,128)}) custom-call(bf16[3,2048,64]{2,1,0:T(8,128)(2,1)S(1)} %copy-done.1, bf16[3,2048,64]{2,1,0:T(8,128)(2,1)S(1)} %bitcast.186, bf16[3,2048,64]{2,1,0:T(8,128)(2,1)} %get-tuple-element.149.v_ref, bf16[3,2048,64]{2,1,0:T(8,128)(2,1)} %bitcast.202, ...), custom_call_target="tpu_custom_call" | custom-call | flops 8053063680 | bytes 6291456 | tf_op jit(solution)/shard_map/pallas_call | solution.py:107
  514.1 6.0 bitcast_convert_fusion
  520.1 5.6 fusion.60
  525.7 5.9 fusion.28
  534.1 6.1 copy.81
  540.2 4.2 dynamic-slice_bitcast_fusion.6
  555.5 4.7 collective-permute-done.22
  560.2 4.2 collective-permute-start.26
  564.4 58.8 %collective-permute-done.23 = f32[96,1536]{1,0:T(8,128)} collective-permute-done((f32[96,1536]{1,0:T(8,128)}, f32[96,1536]{1,0:T(8,128)}, u32[]{:S(2)}, u32[]{:S(2)}) %collective-permute-start.23) | collective-permute-done | bytes 589856 | tf_op jit(solution)/shard_map/ppermute | solution.py:184
  623.2 54.3 %collective-permute-done.16 = f32[2304]{0:T(1024)S(1)} collective-permute-done((f32[2304]{0:T(1024)S(1)}, f32[2304]{0:T(1024)S(1)}, u32[]{:S(2)}, u32[]{:S(2)}) %collective-permute-start.16) | collective-permute-done | bytes 9248 | tf_op jit(solution)/shard_map/ppermute | solution.py:202
  684.2 27.3 %collective-permute-done.28 = f32[96,1536]{1,0:T(8,128)S(1)} collective-permute-done((f32[96,1536]{1,0:T(8,128)S(1)}, f32[96,1536]{1,0:T(8,128)S(1)}, u32[]{:S(2)}, u32[]{:S(2)}) %collective-permute-start.28) | collective-permute-done | bytes 589856 | tf_op jit(solution)/shard_map/ppermute | solution.py:184
  713.6 13.0 %collective-permute-start.18 = (f32[2304]{0:T(1024)S(1)}, f32[2304]{0:T(1024)S(1)}, u32[]{:S(2)}, u32[]{:S(2)}) collective-permute-start(f32[2304]{0:T(1024)S(1)} %add.315), channel_id=1, source_target_pairs={{0,4},{4,0},{8,12},{12,8},{16,20},{20,16},{24,28},{28,24},{1,5},{5... | collective-permute-start | bytes 27656 | tf_op jit(solution)/shard_map/ppermute | solution.py:202
  736.3 8.6 %collective-permute-start.21 = (f32[1,96,192]{2,1,0:T(8,128)S(1)}, f32[1,96,192]{2,1,0:T(8,128)S(1)}, u32[]{:S(2)}, u32[]{:S(2)}) collective-permute-start(f32[1,96,192]{2,1,0:T(8,128)S(1)} %constant_dynamic-slice_fusion), channel_id=1, source_target_pairs={{0,4},{4,0},{8,12},{12,8},{16,20},{20,16},{24,28},{28,24},{1,5},{5... | collective-permute-start | bytes 221192 | tf_op jit(solution)/shard_map/ppermute | solution.py:219
  745.0 10.4 %collective-permute-start.15 = (f32[1,96,576]{2,1,0:T(8,128)S(1)}, f32[1,96,576]{2,1,0:T(8,128)S(1)}, u32[]{:S(2)}, u32[]{:S(2)}) collective-permute-start(f32[1,96,576]{2,1,0:T(8,128)S(1)} %constant_dynamic-slice_fusion.3), channel_id=1, source_target_pairs={{0,4},{4,0},{8,12},{12,8},{16,20},{20,16},{24,28},{28,24},{1,5},{5... | collective-permute-start | bytes 663560 | tf_op jit(solution)/shard_map/ppermute | solution.py:219
  756.1 5.4 collective-permute-done.15
  (241 shorter events, 154.9 us)
Async XLA Ops:
  7.2 163.5 %all-gather.15.cloned.1.call-start = ((), (), s32[]{:S(2)}) async-start(), calls=%async_computation.10 | async-start | bytes 2654208 | tf_op jit(solution)/shard_map/all_gather | solution.py:247
  10.5 175.9 %all-gather.9.cloned.1.call-start = ((), (), s32[]{:S(2)}) async-start(), calls=%async_computation.4 | async-start | bytes 1474560 | tf_op jit(solution)/shard_map/all_gather | solution.py:306
  12.6 44.5 %collective-permute-start.3 = (bf16[73728]{0:T(1024)(128)(2,1)S(1)}, bf16[73728]{0:T(1024)(128)(2,1)S(1)}, u32[]{:S(2)}, u32[]{:S(2)}) collective-permute-start(bf16[73728]{0:T(1024)(128)(2,1)S(1)} %constant_dynamic-update-slice_fusion), channel_id=1, source_target_pairs={{0,4},{4,8},{8,12},{12,16},{16,20},{20,24},{24,28},{28,0},{1,5},{5... | collective-permute-start | bytes 442376 | tf_op jit(solution)/shard_map/ppermute | solution.py:230
  14.1 86.8 %collective-permute-start = (bf16[192,2048]{1,0:T(8,128)(2,1)}, bf16[192,2048]{1,0:T(8,128)(2,1)}, u32[]{:S(2)}, u32[]{:S(2)}) collective-permute-start(bf16[192,2048]{1,0:T(8,128)(2,1)} %param.18), channel_id=1, source_target_pairs={{0,1},{1,2},{2,3},{3,0},{4,5},{5,6},{6,7},{7,4},{8,9},{9,10},{10,1... | collective-permute-start | bytes 2359304 | tf_op jit(solution)/shard_map/ppermute | solution.py:230
  14.1 86.8 %collective-permute-start.1 = (bf16[192,2048]{1,0:T(8,128)(2,1)}, bf16[192,2048]{1,0:T(8,128)(2,1)}, u32[]{:S(2)}, u32[]{:S(2)}) collective-permute-start(bf16[192,2048]{1,0:T(8,128)(2,1)} %param.18), channel_id=1, source_target_pairs={{0,2},{1,3},{2,0},{3,1},{4,6},{5,7},{6,4},{7,5},{8,10},{9,11},{10,... | collective-permute-start | bytes 2359304 | tf_op jit(solution)/shard_map/ppermute | solution.py:230
  15.6 85.3 %collective-permute-start.2 = (bf16[192,2048]{1,0:T(8,128)(2,1)}, bf16[192,2048]{1,0:T(8,128)(2,1)}, u32[]{:S(2)}, u32[]{:S(2)}) collective-permute-start(bf16[192,2048]{1,0:T(8,128)(2,1)} %param.18), channel_id=1, source_target_pairs={{0,3},{1,0},{2,1},{3,2},{4,7},{5,4},{6,5},{7,6},{8,11},{9,8},{10,9... | collective-permute-start | bytes 2359304 | tf_op jit(solution)/shard_map/ppermute | solution.py:230
  17.8 32.7 %collective-permute-start.10 = (f32[3,192]{1,0:T(4,128)S(1)}, f32[3,192]{1,0:T(4,128)S(1)}, u32[]{:S(2)}, u32[]{:S(2)}) collective-permute-start(f32[3,192]{1,0:T(4,128)S(1)} %get-tuple-element.145), channel_id=1, source_target_pairs={{0,1},{1,2},{2,3},{3,0},{4,5},{5,6},{6,7},{7,4},{8,9},{9,10},{10,1... | collective-permute-start | bytes 6920 | tf_op jit(solution)/shard_map/ppermute | solution.py:230
  55.5 8.4 %collective-permute-start.4 = (bf16[73728]{0:T(1024)(128)(2,1)S(1)}, bf16[73728]{0:T(1024)(128)(2,1)S(1)}, u32[]{:S(2)}, u32[]{:S(2)}) collective-permute-start(bf16[73728]{0:T(1024)(128)(2,1)S(1)} %constant_dynamic-update-slice_fusion), channel_id=1, source_target_pairs={{0,8},{4,12},{8,16},{12,20},{16,24},{20,28},{24,0},{28,4},{1,9},{5... | collective-permute-start | bytes 442376 | tf_op jit(solution)/shard_map/ppermute | solution.py:230
  57.1 15.1 %collective-permute-start.5 = (bf16[73728]{0:T(1024)(128)(2,1)S(1)}, bf16[73728]{0:T(1024)(128)(2,1)S(1)}, u32[]{:S(2)}, u32[]{:S(2)}) collective-permute-start(bf16[73728]{0:T(1024)(128)(2,1)S(1)} %constant_dynamic-update-slice_fusion), channel_id=1, source_target_pairs={{0,12},{4,16},{8,20},{12,24},{16,28},{20,0},{24,4},{28,8},{1,13},{... | collective-permute-start | bytes 442376 | tf_op jit(solution)/shard_map/ppermute | solution.py:230
  63.8 15.9 %collective-permute-start.6 = (bf16[73728]{0:T(1024)(128)(2,1)S(1)}, bf16[73728]{0:T(1024)(128)(2,1)S(1)}, u32[]{:S(2)}, u32[]{:S(2)}) collective-permute-start(bf16[73728]{0:T(1024)(128)(2,1)S(1)} %constant_dynamic-update-slice_fusion), channel_id=1, source_target_pairs={{0,16},{4,20},{8,24},{12,28},{16,0},{20,4},{24,8},{28,12},{1,17},{... | collective-permute-start | bytes 442376 | tf_op jit(solution)/shard_map/ppermute | solution.py:230
  72.1 9.0 %collective-permute-start.7 = (bf16[73728]{0:T(1024)(128)(2,1)S(1)}, bf16[73728]{0:T(1024)(128)(2,1)S(1)}, u32[]{:S(2)}, u32[]{:S(2)}) collective-permute-start(bf16[73728]{0:T(1024)(128)(2,1)S(1)} %constant_dynamic-update-slice_fusion), channel_id=1, source_target_pairs={{0,20},{4,24},{8,28},{12,0},{16,4},{20,8},{24,12},{28,16},{1,21},{... | collective-permute-start | bytes 442376 | tf_op jit(solution)/shard_map/ppermute | solution.py:230
  100.6 99.9 %all-gather.7.cloned.1.call-start = ((), (), s32[]{:S(2)}) async-start(), calls=%async_computation.3 | async-start | bytes 3932160 | tf_op jit(solution)/shard_map/all_gather | solution.py:130
  170.3 102.5 %reduce-scatter.4.cloned.1.call-start = ((), (), s32[]{:S(2)}) async-start(), calls=%async_computation.5 | async-start | bytes 3932160 | tf_op jit(solution)/shard_map/reduce_scatter | solution.py:134
  234.8 93.8 %all-gather.11.cloned.1.call-start = ((), (), s32[]{:S(2)}) async-start(), calls=%async_computation.6 | async-start | bytes 3932160 | tf_op jit(solution)/shard_map/all_gather | solution.py:130
  299.5 83.7 %reduce-scatter.6.cloned.1.call-start = ((), (), s32[]{:S(2)}) async-start(), calls=%async_computation.7 | async-start | bytes 3932160 | tf_op jit(solution)/shard_map/reduce_scatter | solution.py:134
  345.1 85.0 %all-gather.13.cloned.1.call-start = ((), (), s32[]{:S(2)}) async-start(), calls=%async_computation.8 | async-start | bytes 3932160 | tf_op jit(solution)/shard_map/all_gather | solution.py:130
  401.0 361.4 %reduce-scatter.8.cloned.1.call-start = ((), (), s32[]{:S(2)}) async-start(), calls=%async_computation.9 | async-start | bytes 3932160 | tf_op jit(solution)/shard_map/reduce_scatter | solution.py:134
  544.4 15.8 %collective-permute-start.22 = (f32[96,1536]{1,0:T(8,128)}, f32[96,1536]{1,0:T(8,128)}, u32[]{:S(2)}, u32[]{:S(2)}) collective-permute-start(f32[96,1536]{1,0:T(8,128)} %get-tuple-element.107), channel_id=1, source_target_pairs={{0,4},{4,8},{8,12},{12,16},{16,20},{20,24},{24,28},{28,0},{1,5},{5... | collective-permute-start | bytes 1769480 | tf_op jit(solution)/shard_map/ppermute | solution.py:184
  545.9 77.4 %collective-permute-start.23 = (f32[96,1536]{1,0:T(8,128)}, f32[96,1536]{1,0:T(8,128)}, u32[]{:S(2)}, u32[]{:S(2)}) collective-permute-start(f32[96,1536]{1,0:T(8,128)} %get-tuple-element.113), channel_id=1, source_target_pairs={{0,8},{4,12},{8,16},{12,20},{16,24},{20,28},{24,0},{28,4},{1,9},{5... | collective-permute-start | bytes 1769480 | tf_op jit(solution)/shard_map/ppermute | solution.py:184
  547.3 133.3 %collective-permute-start.24 = (f32[96,1536]{1,0:T(8,128)}, f32[96,1536]{1,0:T(8,128)}, u32[]{:S(2)}, u32[]{:S(2)}) collective-permute-start(f32[96,1536]{1,0:T(8,128)} %get-tuple-element.112), channel_id=1, source_target_pairs={{0,12},{4,16},{8,20},{12,24},{16,28},{20,0},{24,4},{28,8},{1,13},{... | collective-permute-start | bytes 1769480 | tf_op jit(solution)/shard_map/ppermute | solution.py:184
  548.8 135.3 %collective-permute-start.25 = (f32[96,1536]{1,0:T(8,128)}, f32[96,1536]{1,0:T(8,128)}, u32[]{:S(2)}, u32[]{:S(2)}) collective-permute-start(f32[96,1536]{1,0:T(8,128)} %get-tuple-element.111), channel_id=1, source_target_pairs={{0,16},{4,20},{8,24},{12,28},{16,0},{20,4},{24,8},{28,12},{1,17},{... | collective-permute-start | bytes 1769480 | tf_op jit(solution)/shard_map/ppermute | solution.py:184
  550.8 126.7 %collective-permute-start.16 = (f32[2304]{0:T(1024)S(1)}, f32[2304]{0:T(1024)S(1)}, u32[]{:S(2)}, u32[]{:S(2)}) collective-permute-start(f32[2304]{0:T(1024)S(1)} %concatenate.18), channel_id=1, source_target_pairs={{0,16},{4,20},{8,24},{12,28},{16,0},{20,4},{24,8},{28,12},{1,17},{... | collective-permute-start | bytes 27656 | tf_op jit(solution)/shard_map/ppermute | solution.py:202
  560.2 124.0 %collective-permute-start.26 = (f32[96,1536]{1,0:T(8,128)}, f32[96,1536]{1,0:T(8,128)S(1)}, u32[]{:S(2)}, u32[]{:S(2)}) collective-permute-start(f32[96,1536]{1,0:T(8,128)} %get-tuple-element.110), channel_id=1, source_target_pairs={{0,20},{4,24},{8,28},{12,0},{16,4},{20,8},{24,12},{28,16},{1,21},{... | collective-permute-start | bytes 1769480 | tf_op jit(solution)/shard_map/ppermute | solution.py:184
  623.2 61.0 %collective-permute-start.27 = (f32[96,1536]{1,0:T(8,128)S(1)}, f32[96,1536]{1,0:T(8,128)S(1)}, u32[]{:S(2)}, u32[]{:S(2)}) collective-permute-start(f32[96,1536]{1,0:T(8,128)S(1)} %copy-done.21), channel_id=1, source_target_pairs={{0,24},{4,28},{8,0},{12,4},{16,8},{20,12},{24,16},{28,20},{1,25},{... | collective-permute-start | bytes 1769480 | tf_op jit(solution)/shard_map/ppermute | solution.py:184
  677.6 33.9 %collective-permute-start.28 = (f32[96,1536]{1,0:T(8,128)S(1)}, f32[96,1536]{1,0:T(8,128)S(1)}, u32[]{:S(2)}, u32[]{:S(2)}) collective-permute-start(f32[96,1536]{1,0:T(8,128)S(1)} %copy-done.20), channel_id=1, source_target_pairs={{0,28},{4,0},{8,4},{12,8},{16,12},{20,16},{24,20},{28,24},{1,29},{... | collective-permute-start | bytes 1769480 | tf_op jit(solution)/shard_map/ppermute | solution.py:184
  680.6 47.7 %collective-permute-start.19 = (f32[4,96,192]{2,1,0:T(8,128)S(1)}, f32[4,96,192]{2,1,0:T(8,128)S(1)}, u32[]{:S(2)}, u32[]{:S(2)}) collective-permute-start(f32[4,96,192]{2,1,0:T(8,128)S(1)} %constant_dynamic-slice_fusion.2), channel_id=1, source_target_pairs={{0,16},{4,20},{8,24},{12,28},{16,0},{20,4},{24,8},{28,12},{1,17},{... | collective-permute-start | bytes 884744 | tf_op jit(solution)/shard_map/ppermute | solution.py:219
  684.1 44.4 %collective-permute-start.13 = (f32[4,96,576]{2,1,0:T(8,128)S(1)}, f32[4,96,576]{2,1,0:T(8,128)S(1)}, u32[]{:S(2)}, u32[]{:S(2)}) collective-permute-start(f32[4,96,576]{2,1,0:T(8,128)S(1)} %constant_dynamic-slice_fusion.5), channel_id=1, source_target_pairs={{0,16},{4,20},{8,24},{12,28},{16,0},{20,4},{24,8},{28,12},{1,17},{... | collective-permute-start | bytes 2654216 | tf_op jit(solution)/shard_map/ppermute | solution.py:219
  684.2 29.4 %collective-permute-start.17 = (f32[2304]{0:T(1024)S(1)}, f32[2304]{0:T(1024)S(1)}, u32[]{:S(2)}, u32[]{:S(2)}) collective-permute-start(f32[2304]{0:T(1024)S(1)} %add.314), channel_id=1, source_target_pairs={{0,8},{4,12},{8,0},{12,4},{16,24},{20,28},{24,16},{28,20},{1,9},{5... | collective-permute-start | bytes 27656 | tf_op jit(solution)/shard_map/ppermute | solution.py:202
  713.6 14.7 %collective-permute-start.18 = (f32[2304]{0:T(1024)S(1)}, f32[2304]{0:T(1024)S(1)}, u32[]{:S(2)}, u32[]{:S(2)}) collective-permute-start(f32[2304]{0:T(1024)S(1)} %add.315), channel_id=1, source_target_pairs={{0,4},{4,0},{8,12},{12,8},{16,20},{20,16},{24,28},{28,24},{1,5},{5... | collective-permute-start | bytes 27656 | tf_op jit(solution)/shard_map/ppermute | solution.py:202
  728.7 16.2 %collective-permute-start.14 = (f32[2,96,576]{2,1,0:T(8,128)S(1)}, f32[2,96,576]{2,1,0:T(8,128)S(1)}, u32[]{:S(2)}, u32[]{:S(2)}) collective-permute-start(f32[2,96,576]{2,1,0:T(8,128)S(1)} %constant_dynamic-slice_fusion.4), channel_id=1, source_target_pairs={{0,8},{4,12},{8,0},{12,4},{16,24},{20,28},{24,16},{28,20},{1,9},{5... | collective-permute-start | bytes 1327112 | tf_op jit(solution)/shard_map/ppermute | solution.py:219
  736.3 19.1 %collective-permute-start.21 = (f32[1,96,192]{2,1,0:T(8,128)S(1)}, f32[1,96,192]{2,1,0:T(8,128)S(1)}, u32[]{:S(2)}, u32[]{:S(2)}) collective-permute-start(f32[1,96,192]{2,1,0:T(8,128)S(1)} %constant_dynamic-slice_fusion), channel_id=1, source_target_pairs={{0,4},{4,0},{8,12},{12,8},{16,20},{20,16},{24,28},{28,24},{1,5},{5... | collective-permute-start | bytes 221192 | tf_op jit(solution)/shard_map/ppermute | solution.py:219
  745.0 16.5 %collective-permute-start.15 = (f32[1,96,576]{2,1,0:T(8,128)S(1)}, f32[1,96,576]{2,1,0:T(8,128)S(1)}, u32[]{:S(2)}, u32[]{:S(2)}) collective-permute-start(f32[1,96,576]{2,1,0:T(8,128)S(1)} %constant_dynamic-slice_fusion.3), channel_id=1, source_target_pairs={{0,4},{4,0},{8,12},{12,8},{16,20},{20,16},{24,28},{28,24},{1,5},{5... | collective-permute-start | bytes 663560 | tf_op jit(solution)/shard_map/ppermute | solution.py:219
  (41 other events, 1258.1 us)
Sparse Core Ops, SparseCore 0:
  10.8 54.5 all-gather.14
  100.8 19.0 all-gather.8
  170.4 30.1 all-gather.6
  234.9 37.8 reduce-scatter.3
  299.6 28.9 all-gather.10
  345.2 37.8 reduce-scatter.5
  401.1 28.9 all-gather.12
  520.2 37.8 reduce-scatter.7
